TPU v7x, 256 devices: a whole 4x4x8 slice. The times are simulated.
256 devices in a mesh: dp: 32 (over z_lo, x, core), mp: 8 (over z_hi, y).
Axes of the slice: x: 4, y: 4, z: 8 (z_hi: 2, z_lo: 4; z = z_hi * 4 + z_lo), core: 2. Of those that a mesh axis runs over, the one named last changes fastest.
Arguments:
- tokens_in: bfloat16 [8192, 8192], P('dp', 'mp'), may hold values from -6 to 6
- grad_out: bfloat16 [8192, 8192], P('dp', 'mp'), may hold values from -6 to 6
- gate_in: bfloat16 [64, 128, 128], P('mp'), may hold values from -0.5 to 0.5
- gate_out: bfloat16 [64, 128, 448], P('mp'), may hold values from -0.5 to 0.5
- up_in: bfloat16 [64, 128, 128], P('mp'), may hold values from -0.5 to 0.5
- up_out: bfloat16 [64, 128, 448], P('mp'), may hold values from -0.5 to 0.5
- down_in: bfloat16 [64, 448, 128], P('mp'), may hold values from -0.25 to 0.25
- down_out: bfloat16 [64, 128, 128], P('mp'), may hold values from -0.5 to 0.5
Outputs:
- grad_x: bfloat16 [8192, 8192], P('dp', 'mp')
- grad_gate_in: float32 [64, 128, 128], P('mp', 'dp')
- grad_gate_out: float32 [64, 128, 448], P('mp', 'dp')
- grad_up_in: float32 [64, 128, 128], P('mp', 'dp')
- grad_up_out: float32 [64, 128, 448], P('mp', 'dp')
- grad_down_in: float32 [64, 448, 128], P('mp', 'dp')
- grad_down_out: float32 [64, 128, 128], P('mp', 'dp')
All inputs are finite; a program needn't handle non-finite values.
Results may differ from a plain program's by a relative error of at most 0.0072.
Values may be sent and summed in bfloat16 or wider, within the bound.
No kernel may reach another device: no remote copies, remote signals or barrier semaphores. Data moves between devices by JAX's collectives and lax.ppermute only.
A program may use at most 64 MiB of HBM per device.

v0:
```python
import math

import jax
import jax.numpy as jnp
from jax import lax
from jax.sharding import PartitionSpec as P

BLK = 128
NBLK = 64
PAIR = 2
FBLK = 448


def shards(tokens_in, grad_out, gate_in, gate_out, up_in, up_out, down_in, down_out):
    local_blocks = gate_in.shape[0]
    rows = tokens_in.shape[0]
    scale = 1.0 / math.sqrt(rows * lax.axis_size("dp"))
    x_blocks = tokens_in.reshape(rows, local_blocks, BLK)
    dy_blocks = grad_out.reshape(rows, local_blocks, BLK)

    def mix_in(weight):
        shaped = weight.reshape(local_blocks, BLK, NBLK, PAIR)
        spread = jnp.einsum("tki,kijp->jkpt", x_blocks, shaped, preferred_element_type=jnp.float32)
        return spread.astype(jnp.bfloat16).reshape(NBLK, local_blocks * PAIR, rows)

    def widen(mixed, weight):
        return jnp.einsum("jct,jco->jot", mixed, weight, preferred_element_type=jnp.float32)

    gate_mid = mix_in(gate_in)
    up_mid = mix_in(up_in)
    gate_recv, up_recv = (
        lax.all_to_all(gate_mid, "mp", split_axis=0, concat_axis=1, tiled=True),
        lax.all_to_all(up_mid, "mp", split_axis=0, concat_axis=1, tiled=True),
    )
    gate_pre = widen(gate_recv, gate_out)
    up_pre = widen(up_recv, up_out)
    sigmoid_gate = jax.nn.sigmoid(gate_pre)
    activated = gate_pre * sigmoid_gate
    hidden = (activated * up_pre).astype(jnp.bfloat16)
    down_shaped = down_in.reshape(local_blocks, FBLK, NBLK, PAIR)
    down_mid = jnp.einsum("jot,jokp->kjpt", hidden, down_shaped, preferred_element_type=jnp.float32)
    down_mid = down_mid.astype(jnp.bfloat16).reshape(NBLK, local_blocks * PAIR, rows)
    down_recv = lax.all_to_all(down_mid, "mp", split_axis=0, concat_axis=1, tiled=True)
    term_down_out = jnp.einsum(
        "kct,tkr->kcr", down_recv, dy_blocks, preferred_element_type=jnp.float32
    )
    back_shaped = down_out.reshape(local_blocks, NBLK, PAIR, BLK)
    back_mid = jnp.einsum(
        "tkr,kjpr->jkpt", dy_blocks, back_shaped, preferred_element_type=jnp.float32
    )
    back_mid = back_mid.astype(jnp.bfloat16).reshape(NBLK, local_blocks * PAIR, rows)
    back_recv = lax.all_to_all(back_mid, "mp", split_axis=0, concat_axis=1, tiled=True)
    term_down_in = jnp.einsum("jot,jqt->joq", hidden, back_recv, preferred_element_type=jnp.float32)
    hidden_grad = jnp.einsum("joq,jqt->jot", down_in, back_recv, preferred_element_type=jnp.float32)
    gate_grad = (
        hidden_grad * up_pre * sigmoid_gate * (1.0 + gate_pre * (1.0 - sigmoid_gate))
    ).astype(jnp.bfloat16)
    up_grad = (hidden_grad * activated).astype(jnp.bfloat16)
    term_gate_out = jnp.einsum(
        "jct,jot->jco", gate_recv, gate_grad, preferred_element_type=jnp.float32
    )
    term_up_out = jnp.einsum("jct,jot->jco", up_recv, up_grad, preferred_element_type=jnp.float32)

    def narrow(grad, weight):
        shaped = weight.reshape(local_blocks, NBLK, PAIR, FBLK)
        spread = jnp.einsum("jot,jkpo->kjpt", grad, shaped, preferred_element_type=jnp.float32)
        return spread.astype(jnp.bfloat16).reshape(NBLK, local_blocks * PAIR, rows)

    gate_back, up_back = (
        lax.all_to_all(narrow(gate_grad, gate_out), "mp", split_axis=0, concat_axis=1, tiled=True),
        lax.all_to_all(narrow(up_grad, up_out), "mp", split_axis=0, concat_axis=1, tiled=True),
    )
    input_grad = jnp.einsum("kio,kot->tki", gate_in, gate_back, preferred_element_type=jnp.float32)
    input_grad = input_grad + jnp.einsum(
        "kio,kot->tki", up_in, up_back, preferred_element_type=jnp.float32
    )
    term_gate_in = jnp.einsum(
        "tki,kot->kio", x_blocks, gate_back, preferred_element_type=jnp.float32
    )
    term_up_in = jnp.einsum("tki,kot->kio", x_blocks, up_back, preferred_element_type=jnp.float32)
    grad_x = input_grad.astype(jnp.bfloat16).reshape(rows, local_blocks * BLK)
    (
        summed_gate_in,
        summed_gate_out,
        summed_up_in,
        summed_up_out,
        summed_down_in,
        summed_down_out,
    ) = (
        lax.psum_scatter(term_gate_in, "dp", scatter_dimension=1, tiled=True),
        lax.psum_scatter(term_gate_out, "dp", scatter_dimension=1, tiled=True),
        lax.psum_scatter(term_up_in, "dp", scatter_dimension=1, tiled=True),
        lax.psum_scatter(term_up_out, "dp", scatter_dimension=1, tiled=True),
        lax.psum_scatter(term_down_in, "dp", scatter_dimension=1, tiled=True),
        lax.psum_scatter(term_down_out, "dp", scatter_dimension=1, tiled=True),
    )
    return (
        grad_x,
        summed_gate_in * scale,
        summed_gate_out * scale,
        summed_up_in * scale,
        summed_up_out * scale,
        summed_down_in * scale,
        summed_down_out * scale,
    )


def solution(mesh):
    in_specs = (
        P("dp", "mp"),
        P("dp", "mp"),
        P("mp", None, None),
        P("mp", None, None),
        P("mp", None, None),
        P("mp", None, None),
        P("mp", None, None),
        P("mp", None, None),
    )
    out_specs = (
        P("dp", "mp"),
        P("mp", "dp", None),
        P("mp", "dp", None),
        P("mp", "dp", None),
        P("mp", "dp", None),
        P("mp", "dp", None),
        P("mp", "dp", None),
    )
    return jax.shard_map(shards, mesh=mesh, in_specs=in_specs, out_specs=out_specs, check_vma=False)
```

profile of v0, /device:TPU:1, one launch (start us, length us, event | category | flops | bytes accessed | tf_op | source)
XLA Modules:
  0.0 1000.8 jit_solution(9095258258835023995)
XLA Ops:
  10.9 11.6 %all-to-all-start.2 = ((bf16[64,16,256]{2,1,0:T(8,128)(2,1)}), bf16[64,16,256]{2,1,0:T(8,128)(2,1)S(1)}, u32[]{:S(2)}, u32[]{:S(2)}) async-start(bf16[64,16,256]{2,1,0:T(8,128)(2,1)} %copy.80), calls=%async_computation.2 | async-start | bytes 1048576 | tf_op jit(solution)/shard_map/all_to_all | solution.py:32
  24.2 10.0 all-to-all-done.2
  34.2 5.3 all-to-all-start.1
  41.0 9.5 all-to-all-done.1
  50.5 4.1 all-to-all-start
  54.6 1.9 copy.82
  56.6 2.4 fusion.45
  59.0 6.6 all-to-all-done
  69.1 3.8 fusion.7
  72.9 2.3 fusion.15
  76.3 3.5 all-to-all-start.3
  79.8 2.7 copy.86
  82.5 2.5 fusion.18
  86.2 4.6 all-to-all-done.3
  90.8 4.4 all-to-all-start.4
  98.5 2.5 fusion.21
  102.2 7.9 all-to-all-done.4
  110.0 4.1 all-to-all-start.5
  116.4 2.1 copy.94
  118.7 9.9 all-to-all-done.5
  131.2 2.2 fusion.41
  133.5 2.5 copy.92
  137.0 2.2 fusion.42
  139.2 2.5 copy.95
  141.8 2.1 fusion.43
  144.0 2.3 copy.96
  148.5 116.0 %reduce-scatter.7.cloned.1.call-done = f32[8,4,128]{2,0,1:T(8,128)} async-done(((f32[8,128,128]{2,0,1:T(8,128)}), f32[8,4,128]{2,0,1:T(8,128)}) %reduce-scatter.7.cloned.1.call-update) | async-done | bytes 16400 | tf_op jit(solution)/shard_map/reduce_scatter | solution.py:90
  265.9 141.0 %reduce-scatter.11.cloned.1.call-done = f32[8,4,128]{2,0,1:T(8,128)} async-done(((f32[8,128,128]{2,0,1:T(8,128)}), f32[8,4,128]{2,0,1:T(8,128)}) %reduce-scatter.11.cloned.1.call-update) | async-done | bytes 16400 | tf_op jit(solution)/shard_map/reduce_scatter | solution.py:92
  408.2 143.3 %reduce-scatter.17.cloned.1.call-done = f32[8,4,128]{2,0,1:T(8,128)} async-done(((f32[8,128,128]{2,0,1:T(8,128)}), f32[8,4,128]{2,0,1:T(8,128)}) %reduce-scatter.17.cloned.1.call-update) | async-done | bytes 16400 | tf_op jit(solution)/shard_map/reduce_scatter | solution.py:95
  552.8 145.8 %reduce-scatter.9.cloned.1.call-done = f32[8,4,448]{2,0,1:T(8,128)} async-done(((f32[8,128,448]{2,0,1:T(8,128)}), f32[8,4,448]{2,0,1:T(8,128)}) %reduce-scatter.9.cloned.1.call-update) | async-done | bytes 57360 | tf_op jit(solution)/shard_map/reduce_scatter | solution.py:91
  700.2 145.7 %reduce-scatter.13.cloned.1.call-done = f32[8,4,448]{2,0,1:T(8,128)} async-done(((f32[8,128,448]{2,0,1:T(8,128)}), f32[8,4,448]{2,0,1:T(8,128)}) %reduce-scatter.13.cloned.1.call-update) | async-done | bytes 57360 | tf_op jit(solution)/shard_map/reduce_scatter | solution.py:93
  847.4 145.1 %reduce-scatter.15.cloned.1.call-done = f32[8,14,128]{2,0,1:T(8,128)} async-done(((f32[8,448,128]{2,0,1:T(8,128)}), f32[8,14,128]{2,0,1:T(8,128)}) %reduce-scatter.15.cloned.1.call-update) | async-done | bytes 57360 | tf_op jit(solution)/shard_map/reduce_scatter | solution.py:94
  (80 shorter events, 33.6 us)
Async XLA Ops:
  8.3 14.2 %copy-start.9 = (bf16[8,128,128]{2,1,0:T(8,128)(2,1)S(1)}, bf16[8,128,128]{2,1,0:T(8,128)(2,1)}, u32[]{:S(2)}) copy-start(bf16[8,128,128]{2,1,0:T(8,128)(2,1)} %param.12) | copy-start | bytes 786436
  10.9 23.3 %all-to-all-start.2 = ((bf16[64,16,256]{2,1,0:T(8,128)(2,1)}), bf16[64,16,256]{2,1,0:T(8,128)(2,1)S(1)}, u32[]{:S(2)}, u32[]{:S(2)}) async-start(bf16[64,16,256]{2,1,0:T(8,128)(2,1)} %copy.80), calls=%async_computation.2 | async-start | bytes 1048576 | tf_op jit(solution)/shard_map/all_to_all | solution.py:32
  22.5 16.9 %copy-start.4 = (bf16[256,1024]{1,0:T(8,128)(2,1)S(1)}, bf16[256,1024]{1,0:T(8,128)(2,1)}, u32[]{:S(2)}) copy-start(bf16[256,1024]{1,0:T(8,128)(2,1)} %param.9) | copy-start | bytes 1572868
  23.1 16.5 %copy-start.13 = (bf16[8,128,128]{2,1,0:T(8,128)(2,1)S(1)}, bf16[8,128,128]{2,1,0:T(8,128)(2,1)}, u32[]{:S(2)}) copy-start(bf16[8,128,128]{2,1,0:T(8,128)(2,1)} %param.15) | copy-start | bytes 786436
  34.2 16.3 %all-to-all-start.1 = ((bf16[64,16,256]{2,1,0:T(8,128)(2,1)}), bf16[64,16,256]{2,1,0:T(8,128)(2,1)S(1)}, u32[]{:S(2)}, u32[]{:S(2)}) async-start(bf16[64,16,256]{2,1,0:T(8,128)(2,1)} %copy.75), calls=%async_computation.1 | async-start | bytes 1048576 | tf_op jit(solution)/shard_map/all_to_all | solution.py:33
  39.5 15.2 %copy-start.2 = (bf16[8,128,448]{1,2,0:T(8,128)(2,1)S(1)}, bf16[8,128,448]{1,2,0:T(8,128)(2,1)}, u32[]{:S(2)}) copy-start(bf16[8,128,448]{1,2,0:T(8,128)(2,1)} %param.11) | copy-start | bytes 2752516
  50.5 15.2 %all-to-all-start = ((bf16[64,16,256]{2,1,0:T(8,128)(2,1)}), bf16[64,16,256]{2,1,0:T(8,128)(2,1)}, u32[]{:S(2)}, u32[]{:S(2)}) async-start(bf16[64,16,256]{2,1,0:T(8,128)(2,1)} %copy.70), calls=%async_computation | async-start | bytes 1048576 | tf_op jit(solution)/shard_map/all_to_all | solution.py:52
  56.6 10.8 %copy-start.6 = (bf16[8,8,16,256]{3,2,0,1:T(8,128)(2,1)}, bf16[8,8,16,256]{3,2,0,1:T(8,128)(2,1)S(1)}, u32[]{:S(2)}) copy-start(bf16[8,8,16,256]{3,2,0,1:T(8,128)(2,1)S(1)} %copy.76) | copy-start | bytes 1572868
  56.6 10.2 %copy-start.3 = (bf16[8,448,128]{2,1,0:T(8,128)(2,1)S(1)}, bf16[8,448,128]{2,1,0:T(8,128)(2,1)}, u32[]{:S(2)}) copy-start(bf16[8,448,128]{2,1,0:T(8,128)(2,1)} %param.14) | copy-start | bytes 2752516
  66.8 2.0 copy-start.1
  66.8 2.3 copy-start.12
  69.1 3.8 copy-start.11
  76.3 14.5 %all-to-all-start.3 = ((bf16[64,16,256]{2,1,0:T(8,128)(2,1)}), bf16[64,16,256]{2,1,0:T(8,128)(2,1)S(1)}, u32[]{:S(2)}, u32[]{:S(2)}) async-start(bf16[64,16,256]{2,1,0:T(8,128)(2,1)} %copy.84), calls=%async_computation.3 | async-start | bytes 1048576 | tf_op jit(solution)/shard_map/all_to_all | solution.py:70
  85.0 10.2 %copy-start = (bf16[256,1024]{1,0:T(8,128)(2,1)S(1)}, bf16[256,1024]{1,0:T(8,128)(2,1)}, u32[]{:S(2)}) copy-start(bf16[256,1024]{1,0:T(8,128)(2,1)} %param.8) | copy-start | bytes 1572868
  90.8 19.2 %all-to-all-start.4 = ((bf16[64,16,256]{2,1,0:T(8,128)(2,1)}), bf16[64,16,256]{2,1,0:T(8,128)(2,1)}, u32[]{:S(2)}, u32[]{:S(2)}) async-start(bf16[64,16,256]{2,1,0:T(8,128)(2,1)} %copy.88), calls=%async_computation.4 | async-start | bytes 1048576 | tf_op jit(solution)/shard_map/all_to_all | solution.py:71
  95.2 169.4 %reduce-scatter.7.cloned.1.call-start = ((), (), s32[]{:S(2)}) async-start(), calls=%async_computation.12 | async-start | bytes 540672 | tf_op jit(solution)/shard_map/reduce_scatter | solution.py:90
  110.0 18.6 %all-to-all-start.5 = ((bf16[64,16,256]{2,1,0:T(8,128)(2,1)}), bf16[64,16,256]{2,1,0:T(8,128)(2,1)}, u32[]{:S(2)}, u32[]{:S(2)}) async-start(bf16[64,16,256]{2,1,0:T(8,128)(2,1)} %copy.99), calls=%async_computation.10 | async-start | bytes 1048576 | tf_op jit(solution)/shard_map/all_to_all | solution.py:43
  114.2 292.7 %reduce-scatter.11.cloned.1.call-start = ((), (), s32[]{:S(2)}) async-start(), calls=%async_computation.14 | async-start | bytes 540672 | tf_op jit(solution)/shard_map/reduce_scatter | solution.py:92
  115.3 14.4 %copy-start.5 = (bf16[256,1024]{1,0:T(8,128)(2,1)S(1)}, bf16[256,1024]{1,0:T(8,128)(2,1)}, u32[]{:S(2)}) copy-start(bf16[256,1024]{1,0:T(8,128)(2,1)} %param.9) | copy-start | bytes 1572868
  118.5 433.0 %reduce-scatter.17.cloned.1.call-start = ((), (), s32[]{:S(2)}) async-start(), calls=%async_computation.17 | async-start | bytes 540672 | tf_op jit(solution)/shard_map/reduce_scatter | solution.py:95
  131.2 567.5 %reduce-scatter.9.cloned.1.call-start = ((), (), s32[]{:S(2)}) async-start(), calls=%async_computation.13 | async-start | bytes 2162688 | tf_op jit(solution)/shard_map/reduce_scatter | solution.py:91
  136.0 1.0 copy-start.7
  136.0 709.8 %reduce-scatter.13.cloned.1.call-start = ((), (), s32[]{:S(2)}) async-start(), calls=%async_computation.15 | async-start | bytes 2162688 | tf_op jit(solution)/shard_map/reduce_scatter | solution.py:93
  141.8 850.7 %reduce-scatter.15.cloned.1.call-start = ((), (), s32[]{:S(2)}) async-start(), calls=%async_computation.16 | async-start | bytes 1892352 | tf_op jit(solution)/shard_map/reduce_scatter | solution.py:94
  144.0 2.4 copy-start.8
  146.3 0.9 copy-start.10
Sparse Core Ops, SparseCore 0:
  98.5 166.0 reduce-scatter.6
  267.1 139.8 reduce-scatter.10
  409.4 142.0 reduce-scatter.16
  553.9 144.7 reduce-scatter.8
  701.0 144.7 reduce-scatter.12
  848.2 144.2 reduce-scatter.14
where the time goes:
time: 1010 us; the launch traced here: 1000 us
  waiting for transfers between devices  886 us (88%)
  local copies, waits for them, and re-layouts  38 us (4%)
  starting transfers between devices  33.5 us (3%)
  matrix products  24 us (2%)
  between operations  14.5 us (1%)
    reduce_scatter x1, waiting for transfers between devices, shards(): lax.psum_scatter(term_gate_out, 'dp', scatter_dimension=1, tiled=True)  146 us
    reduce_scatter x1, waiting for transfers between devices, shards(): lax.psum_scatter(term_up_out, 'dp', scatter_dimension=1, tiled=True)  146 us
    reduce_scatter x1, waiting for transfers between devices, shards(): lax.psum_scatter(term_down_in, 'dp', scatter_dimension=1, tiled=True)  145 us
    reduce_scatter x1, waiting for transfers between devices, shards(): lax.psum_scatter(term_down_out, 'dp', scatter_dimension=1, tiled=True)  143 us
    reduce_scatter x1, waiting for transfers between devices, shards(): lax.psum_scatter(term_up_in, 'dp', scatter_dimension=1, tiled=True)  141 us
    reduce_scatter x1, waiting for transfers between devices, shards(): lax.psum_scatter(term_gate_in, 'dp', scatter_dimension=1, tiled=True)  116 us
  transfers between devices with their start and end apart: 12, of which 12 were waited for; matrix products, arithmetic and copies ran while one was open for 5% of the time, Pallas kernels for 0%

commit v1 on v0

--- a/solution.py
+++ b/solution.py
@@ -28,10 +28,15 @@
 
     gate_mid = mix_in(gate_in)
     up_mid = mix_in(up_in)
-    gate_recv, up_recv = (
-        lax.all_to_all(gate_mid, "mp", split_axis=0, concat_axis=1, tiled=True),
-        lax.all_to_all(up_mid, "mp", split_axis=0, concat_axis=1, tiled=True),
+    back_shaped = down_out.reshape(local_blocks, NBLK, PAIR, BLK)
+    back_mid = jnp.einsum(
+        "tkr,kjpr->jkpt", dy_blocks, back_shaped, preferred_element_type=jnp.float32
     )
+    back_mid = back_mid.astype(jnp.bfloat16).reshape(NBLK, local_blocks * PAIR, rows)
+    first_recv = lax.all_to_all(
+        jnp.stack([gate_mid, up_mid, back_mid]), "mp", split_axis=1, concat_axis=2, tiled=True
+    )
+    gate_recv, up_recv, back_recv = first_recv[0], first_recv[1], first_recv[2]
     gate_pre = widen(gate_recv, gate_out)
     up_pre = widen(up_recv, up_out)
     sigmoid_gate = jax.nn.sigmoid(gate_pre)
@@ -44,12 +49,6 @@
     term_down_out = jnp.einsum(
         "kct,tkr->kcr", down_recv, dy_blocks, preferred_element_type=jnp.float32
     )
-    back_shaped = down_out.reshape(local_blocks, NBLK, PAIR, BLK)
-    back_mid = jnp.einsum(
-        "tkr,kjpr->jkpt", dy_blocks, back_shaped, preferred_element_type=jnp.float32
-    )
-    back_mid = back_mid.astype(jnp.bfloat16).reshape(NBLK, local_blocks * PAIR, rows)
-    back_recv = lax.all_to_all(back_mid, "mp", split_axis=0, concat_axis=1, tiled=True)
     term_down_in = jnp.einsum("jot,jqt->joq", hidden, back_recv, preferred_element_type=jnp.float32)
     hidden_grad = jnp.einsum("joq,jqt->jot", down_in, back_recv, preferred_element_type=jnp.float32)
     gate_grad = (
@@ -66,10 +65,11 @@
         spread = jnp.einsum("jot,jkpo->kjpt", grad, shaped, preferred_element_type=jnp.float32)
         return spread.astype(jnp.bfloat16).reshape(NBLK, local_blocks * PAIR, rows)
 
-    gate_back, up_back = (
-        lax.all_to_all(narrow(gate_grad, gate_out), "mp", split_axis=0, concat_axis=1, tiled=True),
-        lax.all_to_all(narrow(up_grad, up_out), "mp", split_axis=0, concat_axis=1, tiled=True),
+    back_recv2 = lax.all_to_all(
+        jnp.stack([narrow(gate_grad, gate_out), narrow(up_grad, up_out)]),
+        "mp", split_axis=1, concat_axis=2, tiled=True,
     )
+    gate_back, up_back = back_recv2[0], back_recv2[1]
     input_grad = jnp.einsum("kio,kot->tki", gate_in, gate_back, preferred_element_type=jnp.float32)
     input_grad = input_grad + jnp.einsum(
         "kio,kot->tki", up_in, up_back, preferred_element_type=jnp.float32
@@ -79,30 +79,20 @@
     )
     term_up_in = jnp.einsum("tki,kot->kio", x_blocks, up_back, preferred_element_type=jnp.float32)
     grad_x = input_grad.astype(jnp.bfloat16).reshape(rows, local_blocks * BLK)
-    (
-        summed_gate_in,
-        summed_gate_out,
-        summed_up_in,
-        summed_up_out,
-        summed_down_in,
-        summed_down_out,
-    ) = (
-        lax.psum_scatter(term_gate_in, "dp", scatter_dimension=1, tiled=True),
-        lax.psum_scatter(term_gate_out, "dp", scatter_dimension=1, tiled=True),
-        lax.psum_scatter(term_up_in, "dp", scatter_dimension=1, tiled=True),
-        lax.psum_scatter(term_up_out, "dp", scatter_dimension=1, tiled=True),
-        lax.psum_scatter(term_down_in, "dp", scatter_dimension=1, tiled=True),
-        lax.psum_scatter(term_down_out, "dp", scatter_dimension=1, tiled=True),
+    terms = (term_gate_in, term_gate_out, term_up_in, term_up_out, term_down_in, term_down_out)
+    groups = lax.axis_size("dp")
+    flat = [term.reshape(term.shape[0], groups, -1) for term in terms]
+    widths = [piece.shape[2] for piece in flat]
+    summed = lax.psum_scatter(
+        jnp.concatenate(flat, axis=2), "dp", scatter_dimension=1, tiled=True
     )
-    return (
-        grad_x,
-        summed_gate_in * scale,
-        summed_gate_out * scale,
-        summed_up_in * scale,
-        summed_up_out * scale,
-        summed_down_in * scale,
-        summed_down_out * scale,
-    )
+    outs = []
+    start = 0
+    for term, width in zip(terms, widths):
+        piece = summed[:, 0, start:start + width]
+        start += width
+        outs.append(piece.reshape(term.shape[0], term.shape[1] // groups, term.shape[2]) * scale)
+    return (grad_x, *outs)
 
 
 def solution(mesh):

time: 1010 us -> 309 us (0.31)
  waiting for transfers between devices: 886 us -> 197 us
  starting transfers between devices: 33.5 us -> 23 us
    reduce_scatter x6 -> x1, waiting for transfers between devices: 837 us -> 169 us  [shards(): lax.psum_scatter(jnp.concatenate(flat, axis=2), 'dp', scatter_dimension=1...]
    all_to_all x5 -> x2, waiting for transfers between devices: 38.6 us -> 26.3 us  [the longest x1 23.6 us: shards(): lax.all_to_all(jnp.stack([gate_mid, up_mid, back_mid]), 'mp', split_axis=...]
    all_to_all x5 -> x2, starting transfers between devices: 28.9 us -> 18.7 us  [the longest x1 11.8 us: shards(): lax.all_to_all(jnp.stack([gate_mid, up_mid, back_mid]), 'mp', split_axis=...]
    unnamed x41 -> x58, local copies, waits for them, and re-layouts: 16.5 us -> 20.5 us
  transfers between devices with their start and end apart: 12 -> 4, of which waited for: 12 -> 4; matrix products, arithmetic and copies ran while one was open for 5% -> 8% of each run, Pallas kernels for 0% -> 0%
where the time goes in v1:
time: 309 us; the launch traced here: 303 us
  waiting for transfers between devices  197 us (64%)
  local copies, waits for them, and re-layouts  45 us (15%)
  starting transfers between devices  23 us (7%)
  matrix products  18.8 us (6%)
  between operations  14.4 us (5%)
  other arithmetic  4.72 us (2%)
    reduce_scatter x1, waiting for transfers between devices, shards(): lax.psum_scatter(jnp.concatenate(flat, axis=2), 'dp', scatter_dimension=1...  169 us
    all_to_all x1, waiting for transfers between devices, shards(): lax.all_to_all(jnp.stack([gate_mid, up_mid, back_mid]), 'mp', split_axis=...  23.6 us
    unnamed x58, local copies, waits for them, and re-layouts  20.5 us
    all_to_all x1, starting transfers between devices, shards(): lax.all_to_all(jnp.stack([gate_mid, up_mid, back_mid]), 'mp', split_axis=...  11.8 us
    reshape x6, local copies, waits for them, and re-layouts, shards(): flat = [term.reshape(term.shape[0], groups, -1) for term in terms]  9.45 us
    concatenate x2, local copies, waits for them, and re-layouts, shards(): jnp.concatenate(flat, axis=2)  7 us
    all_to_all x1, starting transfers between devices, shards(): lax.all_to_all(jnp.stack([narrow(gate_grad, gate_out), narrow(up_grad, up...  6.92 us
  transfers between devices with their start and end apart: 4, of which 4 were waited for; matrix products, arithmetic and copies ran while one was open for 8% of the time, Pallas kernels for 0%

profile of v1, /device:TPU:1, one launch (start us, length us, event | category | flops | bytes accessed | tf_op | source)
XLA Modules:
  0.0 303.2 jit_solution(11403869746238706733)
XLA Ops:
  7.2 1.1 copy.57
  8.3 1.1 copy.60
  9.4 1.1 copy.108
  12.6 1.4 pad_maximum_fusion
  14.0 11.8 %all-to-all-start = ((bf16[3,64,16,256]{3,2,0,1:T(8,128)(2,1)}), bf16[3,64,16,256]{3,2,0,1:T(8,128)(2,1)S(1)}, u32[]{:S(2)}, u32[]{:S(2)}) async-start(bf16[3,64,16,256]{3,2,0,1:T(8,128)(2,1)} %pad_maximum_fusion), calls=%async_computation | async-start | bytes 3145728 | tf_op jit(solution)/shard_map/all_to_all | solution.py:36
  25.7 1.8 copy.82
  27.6 23.6 %all-to-all-done = bf16[3,64,16,256]{3,2,0,1:T(8,128)(2,1)S(1)} async-done(((bf16[3,64,16,256]{3,2,0,1:T(8,128)(2,1)}), bf16[3,64,16,256]{3,2,0,1:T(8,128)(2,1)S(1)}, u32[]{:S(2)}, u32[]{:S(2)}) %all-to-all-start) | async-done | bytes 1572896 | tf_op jit(solution)/shard_map/all_to_all | solution.py:36
  54.8 3.6 %fusion.7 = (bf16[8,448,256]{2,1,0:T(8,128)(2,1)S(1)}, bf16[8,448,256]{2,1,0:T(8,128)(2,1)}, bf16[8,448,256]{2,1,0:T(8,128)(2,1)}) fusion(f32[8,256,448]{1,2,0:T(8,128)S(1)} %fusion.51, f32[8,256,448]{1,2,0:T(8,128)S(1)} %fusion.50, bf16[8,128,448]{1,2,0:T(8,128)(2,1)S(1)} %copy-done.19, bf16[8,128,256]{2,1,0:T(8,128)(2,1)S(1)} %bitcast.182), kind=kOutput, calls=%fused_computation.12 | convolution fusion | flops 248643584 | bytes 14286848 | tf_op jit(solution)/shard_map/jct,jco->jot/dot_general | solution.py:27
  58.4 1.2 copy-done.15
  60.4 1.1 copy.84
  61.5 4.1 %all-to-all-start.2 = ((bf16[64,16,256]{2,1,0:T(8,128)(2,1)}), bf16[64,16,256]{2,1,0:T(8,128)(2,1)S(1)}, u32[]{:S(2)}, u32[]{:S(2)}) async-start(bf16[64,16,256]{2,1,0:T(8,128)(2,1)} %copy.84), calls=%async_computation.2 | async-start | bytes 1048576 | tf_op jit(solution)/shard_map/all_to_all | solution.py:48
  65.6 1.8 copy.69
  67.4 1.9 copy.71
  69.3 2.7 fusion.15
  73.4 1.1 pad_maximum_fusion.1
  74.5 2.1 all-to-all-done.2
  76.7 6.9 %all-to-all-start.1 = ((bf16[2,64,16,256]{3,2,0,1:T(8,128)(2,1)}), bf16[2,64,16,256]{3,2,0,1:T(8,128)(2,1)}, u32[]{:S(2)}, u32[]{:S(2)}) async-start(bf16[2,64,16,256]{3,2,0,1:T(8,128)(2,1)} %pad_maximum_fusion.1), calls=%async_computation.1 | async-start | bytes 2097152 | tf_op jit(solution)/shard_map/all_to_all | solution.py:68
  83.8 2.1 fusion.49
  86.0 1.6 reshape.96
  87.5 2.2 fusion.47
  89.7 2.1 reshape.93
  91.8 2.2 fusion.48
  94.0 2.1 reshape.95
  97.4 2.7 all-to-all-done.1
  100.1 1.4 copy.143
  103.0 1.1 convolution_bitcast_fusion
  104.0 2.1 copy.80
  106.2 1.9 reshape.94
  110.0 1.3 copy-done
  112.4 7.0 %copy.87 = f32[8,32,6912]{2,0,1:T(8,128)} copy(f32[8,32,6912]{2,1,0:T(8,128)S(1)} %constant_dynamic-update-slice_fusion) | data formatting | bytes 14155776 | tf_op jit(solution)/shard_map/concatenate | solution.py:87
  121.9 168.9 %reduce-scatter.2.cloned.1.call-done = f32[8,1,6912]{2,0,1:T(8,128)} async-done(((f32[8,32,6912]{2,0,1:T(8,128)}), f32[8,1,6912]{2,0,1:T(8,128)}) %reduce-scatter.2.cloned.1.call-update) | async-done | bytes 221200 | tf_op jit(solution)/shard_map/reduce_scatter | solution.py:86
  293.4 1.5 fusion.41
  (79 shorter events, 20.2 us)
Async XLA Ops:
  10.6 1.3 copy-start.7
  10.9 1.1 copy-start.20
  14.0 11.8 %copy-start.4 = (bf16[8,448,128]{2,1,0:T(8,128)(2,1)S(1)}, bf16[8,448,128]{2,1,0:T(8,128)(2,1)}, u32[]{:S(2)}) copy-start(bf16[8,448,128]{2,1,0:T(8,128)(2,1)} %param.14) | copy-start | bytes 2752516
  14.0 37.2 %all-to-all-start = ((bf16[3,64,16,256]{3,2,0,1:T(8,128)(2,1)}), bf16[3,64,16,256]{3,2,0,1:T(8,128)(2,1)S(1)}, u32[]{:S(2)}, u32[]{:S(2)}) async-start(bf16[3,64,16,256]{3,2,0,1:T(8,128)(2,1)} %pad_maximum_fusion), calls=%async_computation | async-start | bytes 3145728 | tf_op jit(solution)/shard_map/all_to_all | solution.py:36
  51.3 1.2 copy-start.5
  52.5 1.2 copy-start.6
  53.7 1.2 copy-start.19
  54.8 4.8 %copy-start.18 = (bf16[8,448,128]{1,0,2:T(8,128)(2,1)S(1)}, bf16[8,448,128]{1,0,2:T(8,128)(2,1)}, u32[]{:S(2)}) copy-start(bf16[8,448,128]{1,0,2:T(8,128)(2,1)} %copy.82) | copy-start | bytes 2752516
  58.4 1.3 copy-start.15
  61.5 15.1 %all-to-all-start.2 = ((bf16[64,16,256]{2,1,0:T(8,128)(2,1)}), bf16[64,16,256]{2,1,0:T(8,128)(2,1)S(1)}, u32[]{:S(2)}, u32[]{:S(2)}) async-start(bf16[64,16,256]{2,1,0:T(8,128)(2,1)} %copy.84), calls=%async_computation.2 | async-start | bytes 1048576 | tf_op jit(solution)/shard_map/all_to_all | solution.py:48
  69.3 3.0 copy-start.14
  76.7 6.9 %copy-start.9 = (bf16[64,16,256]{2,1,0:T(8,128)(2,1)}, bf16[64,16,256]{2,1,0:T(8,128)(2,1)S(1)}, u32[]{:S(2)}) copy-start(bf16[64,16,256]{2,1,0:T(8,128)(2,1)S(1)} %all-to-all-done.2) | copy-start | bytes 1572868
  76.7 23.4 %all-to-all-start.1 = ((bf16[2,64,16,256]{3,2,0,1:T(8,128)(2,1)}), bf16[2,64,16,256]{3,2,0,1:T(8,128)(2,1)}, u32[]{:S(2)}, u32[]{:S(2)}) async-start(bf16[2,64,16,256]{3,2,0,1:T(8,128)(2,1)} %pad_maximum_fusion.1), calls=%async_computation.1 | async-start | bytes 2097152 | tf_op jit(solution)/shard_map/all_to_all | solution.py:68
  83.6 207.2 %reduce-scatter.2.cloned.1.call-start = ((), (), s32[]{:S(2)}) async-start(), calls=%async_computation.4 | async-start | bytes 7299072 | tf_op jit(solution)/shard_map/reduce_scatter | solution.py:86
  94.0 2.1 copy-start.10
  94.0 2.1 copy-start.8
  100.1 1.5 copy-start.3
  103.0 5.2 %copy-start.2 = (f32[8,32,1792]{2,1,0:T(8,128)S(1)}, f32[8,32,1792]{2,1,0:T(8,128)}, u32[]{:S(2)}) copy-start(f32[8,32,1792]{2,1,0:T(8,128)} %reshape.93) | copy-start | bytes 5505028
  104.0 4.1 %copy-start.12 = (f32[8,32,512]{2,1,0:T(8,128)S(1)}, f32[8,32,512]{2,1,0:T(8,128)}, u32[]{:S(2)}) copy-start(f32[8,32,512]{2,1,0:T(8,128)} %reshape.92) | copy-start | bytes 1572868
  108.2 1.0 copy-start.13
  108.2 1.7 copy-start.1
  109.8 1.5 copy-start
  111.3 1.0 copy-start.11
  119.4 0.9 copy-start.16
  119.4 1.2 copy-start.17
Sparse Core Ops, SparseCore 0:
  119.5 171.2 reduce-scatter.1

commit v2 on v1

--- a/solution.py
+++ b/solution.py
@@ -3,18 +3,20 @@
 import jax
 import jax.numpy as jnp
 from jax import lax
-from jax.sharding import PartitionSpec as P
+from jax.sharding import Mesh, PartitionSpec as P
 
 BLK = 128
 NBLK = 64
 PAIR = 2
 FBLK = 448
+DP = ("dz", "dx", "dc")
 
 
 def shards(tokens_in, grad_out, gate_in, gate_out, up_in, up_out, down_in, down_out):
     local_blocks = gate_in.shape[0]
     rows = tokens_in.shape[0]
-    scale = 1.0 / math.sqrt(rows * lax.axis_size("dp"))
+    groups = lax.axis_size(DP)
+    scale = 1.0 / math.sqrt(rows * groups)
     x_blocks = tokens_in.reshape(rows, local_blocks, BLK)
     dy_blocks = grad_out.reshape(rows, local_blocks, BLK)
 
@@ -80,12 +82,14 @@
     term_up_in = jnp.einsum("tki,kot->kio", x_blocks, up_back, preferred_element_type=jnp.float32)
     grad_x = input_grad.astype(jnp.bfloat16).reshape(rows, local_blocks * BLK)
     terms = (term_gate_in, term_gate_out, term_up_in, term_up_out, term_down_in, term_down_out)
-    groups = lax.axis_size("dp")
     flat = [term.reshape(term.shape[0], groups, -1) for term in terms]
     widths = [piece.shape[2] for piece in flat]
-    summed = lax.psum_scatter(
-        jnp.concatenate(flat, axis=2), "dp", scatter_dimension=1, tiled=True
-    )
+    stacked = jnp.concatenate(flat, axis=2)
+    sizes = [lax.axis_size(name) for name in DP]
+    summed = stacked.reshape(stacked.shape[0], *sizes, stacked.shape[2])
+    for position in reversed(range(len(DP))):
+        summed = lax.psum_scatter(summed, DP[position], scatter_dimension=1 + position, tiled=True)
+    summed = summed.reshape(stacked.shape[0], 1, stacked.shape[2])
     outs = []
     start = 0
     for term, width in zip(terms, widths):
@@ -96,9 +100,14 @@
 
 
 def solution(mesh):
+    dp = mesh.shape["dp"]
+    mp = mesh.shape["mp"]
+    sub = (dp // 8, 4, 2) if dp % 8 == 0 else (dp,)
+    fine = Mesh(mesh.devices.reshape(*sub, mp), DP[-len(sub):] + ("mp",))
+    names = DP[-len(sub):]
     in_specs = (
-        P("dp", "mp"),
-        P("dp", "mp"),
+        P(names, "mp"),
+        P(names, "mp"),
         P("mp", None, None),
         P("mp", None, None),
         P("mp", None, None),
@@ -107,12 +116,12 @@
         P("mp", None, None),
     )
     out_specs = (
-        P("dp", "mp"),
-        P("mp", "dp", None),
-        P("mp", "dp", None),
-        P("mp", "dp", None),
-        P("mp", "dp", None),
-        P("mp", "dp", None),
-        P("mp", "dp", None),
+        P(names, "mp"),
+        P("mp", names, None),
+        P("mp", names, None),
+        P("mp", names, None),
+        P("mp", names, None),
+        P("mp", names, None),
+        P("mp", names, None),
     )
-    return jax.shard_map(shards, mesh=mesh, in_specs=in_specs, out_specs=out_specs, check_vma=False)
+    return jax.shard_map(shards, mesh=fine, in_specs=in_specs, out_specs=out_specs, check_vma=False)

time: 309 us -> 260 us (0.84); the launches traced: 303 us -> 259 us
  waiting for transfers between devices: 197 us -> 147 us
  local copies, waits for them, and re-layouts: 45 us -> 51.6 us
    reduce_scatter x1 -> x3, waiting for transfers between devices: 169 us -> 120 us  [shards(): lax.psum_scatter(summed, DP[position], scatter_dimension=1 + position, ti...]
    concatenate x2 -> x8, local copies, waits for them, and re-layouts: 7 us -> 19.5 us  [shards(): stacked = jnp.concatenate(flat, axis=2)]
    reshape x6 -> x0, local copies, waits for them, and re-layouts: 9.45 us -> none  [shards(): flat = [term.reshape(term.shape[0], groups, -1) for term in terms]]
    reduce_scatter x0 -> x1, local copies, waits for them, and re-layouts: none -> 3.97 us  [shards(): lax.psum_scatter(summed, DP[position], scatter_dimension=1 + position, ti...]
    unnamed x58 -> x60, local copies, waits for them, and re-layouts: 20.5 us -> 18.9 us
  transfers between devices with their start and end apart: 4 -> 6, of which waited for: 4 -> 5; matrix products, arithmetic and copies ran while one was open for 8% -> 11% of each run, Pallas kernels for 0% -> 0%
where the time goes in v2:
time: 260 us; the launch traced here: 259 us
  waiting for transfers between devices  147 us (57%)
  local copies, waits for them, and re-layouts  51.6 us (20%)
  starting transfers between devices  22.3 us (9%)
  matrix products  18.7 us (7%)
  between operations  14.2 us (5%)
  other arithmetic  4.76 us (2%)
    reduce_scatter x3, waiting for transfers between devices, shards(): lax.psum_scatter(summed, DP[position], scatter_dimension=1 + position, ti...  120 us
    all_to_all x1, waiting for transfers between devices, shards(): lax.all_to_all(jnp.stack([gate_mid, up_mid, back_mid]), 'mp', split_axis=...  23.6 us
    concatenate x8, local copies, waits for them, and re-layouts, shards(): stacked = jnp.concatenate(flat, axis=2)  19.5 us
    unnamed x60, local copies, waits for them, and re-layouts  18.9 us
    all_to_all x1, starting transfers between devices, shards(): lax.all_to_all(jnp.stack([gate_mid, up_mid, back_mid]), 'mp', split_axis=...  11.8 us
    all_to_all x1, starting transfers between devices, shards(): lax.all_to_all(jnp.stack([narrow(gate_grad, gate_out), narrow(up_grad, up...  6.1 us
  transfers between devices with their start and end apart: 6, of which 5 were waited for; matrix products, arithmetic and copies ran while one was open for 11% of the time, Pallas kernels for 0%

profile of v2, /device:TPU:1, one launch (start us, length us, event | category | flops | bytes accessed | tf_op | source)
XLA Modules:
  0.0 258.5 jit_solution(17003886585841551956)
XLA Ops:
  7.2 1.1 copy.57
  8.3 1.1 copy.60
  9.4 1.1 copy.110
  12.6 1.4 pad_maximum_fusion
  14.0 11.8 %all-to-all-start = ((bf16[3,64,16,256]{3,2,0,1:T(8,128)(2,1)}), bf16[3,64,16,256]{3,2,0,1:T(8,128)(2,1)S(1)}, u32[]{:S(2)}, u32[]{:S(2)}) async-start(bf16[3,64,16,256]{3,2,0,1:T(8,128)(2,1)} %pad_maximum_fusion), calls=%async_computation | async-start | bytes 3145728 | tf_op jit(solution)/shard_map/all_to_all | solution.py:38
  25.8 1.8 copy.82
  27.6 23.6 %all-to-all-done = bf16[3,64,16,256]{3,2,0,1:T(8,128)(2,1)S(1)} async-done(((bf16[3,64,16,256]{3,2,0,1:T(8,128)(2,1)}), bf16[3,64,16,256]{3,2,0,1:T(8,128)(2,1)S(1)}, u32[]{:S(2)}, u32[]{:S(2)}) %all-to-all-start) | async-done | bytes 1572896 | tf_op jit(solution)/shard_map/all_to_all | solution.py:38
  51.5 1.2 copy-done.5
  55.1 3.5 %fusion.7 = (bf16[8,448,256]{2,1,0:T(8,128)(2,1)S(1)}, bf16[8,448,256]{2,1,0:T(8,128)(2,1)}, bf16[8,448,256]{2,1,0:T(8,128)(2,1)}) fusion(f32[8,256,448]{1,2,0:T(8,128)S(1)} %fusion.51, f32[8,256,448]{1,2,0:T(8,128)S(1)} %fusion.50, bf16[8,128,448]{1,2,0:T(8,128)(2,1)S(1)} %copy-done.20, bf16[8,128,256]{2,1,0:T(8,128)(2,1)S(1)} %bitcast.184), kind=kOutput, calls=%fused_computation.12 | convolution fusion | flops 248643584 | bytes 14286848 | tf_op jit(solution)/shard_map/jct,jco->jot/dot_general | solution.py:29
  58.6 1.3 copy-done.16
  61.7 4.1 %all-to-all-start.2 = ((bf16[64,16,256]{2,1,0:T(8,128)(2,1)}), bf16[64,16,256]{2,1,0:T(8,128)(2,1)S(1)}, u32[]{:S(2)}, u32[]{:S(2)}) async-start(bf16[64,16,256]{2,1,0:T(8,128)(2,1)} %copy.84), calls=%async_computation.2 | async-start | bytes 1048576 | tf_op jit(solution)/shard_map/all_to_all | solution.py:50
  65.8 1.8 copy.69
  68.7 2.7 %fusion.15 = bf16[8,256,64,2]{1,2,3,0:T(8,128)(2,1)S(1)} fusion(bf16[8,448,256]{2,1,0:T(8,128)(2,1)} %get-tuple-element.29, bf16[8,64,2,448]{3,0,2,1:T(8,128)(2,1)} %bitcast.196), kind=kOutput, calls=%fused_computation.24 | convolution fusion | flops 235143168 | bytes 3276800 | tf_op jit(solution)/shard_map/jot,jkpo->kjpt/dot_general | solution.py:67
  73.9 2.9 %all-to-all-done.2 = bf16[64,16,256]{2,1,0:T(8,128)(2,1)S(1)} async-done(((bf16[64,16,256]{2,1,0:T(8,128)(2,1)}), bf16[64,16,256]{2,1,0:T(8,128)(2,1)S(1)}, u32[]{:S(2)}, u32[]{:S(2)}) %all-to-all-start.2) | async-done | bytes 524320 | tf_op jit(solution)/shard_map/all_to_all | solution.py:50
  76.8 6.1 %all-to-all-start.1 = ((bf16[2,64,16,256]{3,2,0,1:T(8,128)(2,1)}), bf16[2,64,16,256]{3,2,0,1:T(8,128)(2,1)}, u32[]{:S(2)}, u32[]{:S(2)}) async-start(bf16[2,64,16,256]{3,2,0,1:T(8,128)(2,1)} %pad_maximum_fusion.1), calls=%async_computation.1 | async-start | bytes 2097152 | tf_op jit(solution)/shard_map/all_to_all | solution.py:70
  83.2 2.1 fusion.49
  85.3 2.2 concatenate.20
  87.5 2.2 fusion.47
  89.8 2.9 %concatenate.17 = f32[8,4,4,2,1792]{4,3,2,1,0:T(2,128)} reshape(f32[8,128,448]{2,1,0:T(8,128)S(1)} %fusion.47) | data formatting | bytes 3670016 | tf_op jit(solution)/shard_map/concatenate | solution.py:87
  92.7 2.2 fusion.48
  94.9 2.9 %concatenate.19 = f32[8,4,4,2,1792]{4,3,2,1,0:T(2,128)} reshape(f32[8,128,448]{2,1,0:T(8,128)S(1)} %fusion.48) | data formatting | bytes 3670016 | tf_op jit(solution)/shard_map/concatenate | solution.py:87
  99.2 1.1 concatenate.21
  100.3 1.4 copy.145
  104.4 2.1 copy.80
  106.5 2.1 concatenate.18
  110.7 1.2 copy-done
  113.0 7.2 %copy.87 = f32[8,4,4,2,6912]{4,0,2,1,3:T(8,128)} copy(f32[8,4,4,2,6912]{4,3,2,1,0:T(2,128)S(1)} %constant_dynamic-update-slice_fusion) | data formatting | bytes 14155776 | tf_op jit(solution)/shard_map/concatenate | solution.py:87
  120.3 44.5 %reduce-scatter.4.cloned.1.call-done = f32[8,4,4,1,6912]{4,0,2,1,3:T(8,128)} async-done(((f32[8,4,4,2,6912]{4,0,2,1,3:T(8,128)}), f32[8,4,4,1,6912]{4,0,2,1,3:T(8,128)}) %reduce-scatter.4.cloned.1.call-update) | async-done | bytes 3538960 | tf_op jit(solution)/shard_map/reduce_scatter | solution.py:91
  164.8 4.0 %copy.88 = f32[8,4,4,1,6912]{4,0,3,1,2:T(8,128)} copy(f32[8,4,4,1,6912]{4,0,2,1,3:T(8,128)} %reduce-scatter.4.cloned.1.call-done) | data formatting | bytes 7077888 | tf_op jit(solution)/shard_map/reduce_scatter | solution.py:91
  168.8 45.8 %reduce-scatter.6.cloned.1.call-done = f32[8,4,1,1,6912]{4,0,3,1,2:T(8,128)} async-done(((f32[8,4,4,1,6912]{4,0,3,1,2:T(8,128)}), f32[8,4,1,1,6912]{4,0,3,1,2:T(8,128)}) %reduce-scatter.6.cloned.1.call-update) | async-done | bytes 884752 | tf_op jit(solution)/shard_map/reduce_scatter | solution.py:91
  216.3 30.1 %reduce-scatter.8.cloned.1.call-done = f32[8,1,1,1,6912]{4,0,3,2,1:T(8,128)} async-done(((f32[8,4,1,1,6912]{4,0,3,2,1:T(8,128)}), f32[8,1,1,1,6912]{4,0,3,2,1:T(8,128)}) %reduce-scatter.8.cloned.1.call-update) | async-done | bytes 221200 | tf_op jit(solution)/shard_map/reduce_scatter | solution.py:91
  247.2 1.5 fusion.41
  (88 shorter events, 23.1 us)
Async XLA Ops:
  10.6 1.3 copy-start.7
  10.9 1.1 copy-start.21
  14.0 11.8 %copy-start.4 = (bf16[8,448,128]{2,1,0:T(8,128)(2,1)S(1)}, bf16[8,448,128]{2,1,0:T(8,128)(2,1)}, u32[]{:S(2)}) copy-start(bf16[8,448,128]{2,1,0:T(8,128)(2,1)} %param.14) | copy-start | bytes 2752516
  14.0 37.2 %all-to-all-start = ((bf16[3,64,16,256]{3,2,0,1:T(8,128)(2,1)}), bf16[3,64,16,256]{3,2,0,1:T(8,128)(2,1)S(1)}, u32[]{:S(2)}, u32[]{:S(2)}) async-start(bf16[3,64,16,256]{3,2,0,1:T(8,128)(2,1)} %pad_maximum_fusion), calls=%async_computation | async-start | bytes 3145728 | tf_op jit(solution)/shard_map/all_to_all | solution.py:38
  51.3 1.4 copy-start.5
  51.4 3.1 %copy-start.9 = (bf16[1,8,8,16,256]{4,3,2,1,0:T(8,128)(2,1)}, bf16[1,8,8,16,256]{4,3,2,1,0:T(8,128)(2,1)S(1)}, u32[]{:S(2)}) copy-start(bf16[1,8,8,16,256]{4,3,2,1,0:T(8,128)(2,1)S(1)} %get-tuple-element.31) | copy-start | bytes 1572868
  52.7 1.2 copy-start.6
  53.9 1.2 copy-start.20
  55.1 4.8 %copy-start.19 = (bf16[8,448,128]{1,0,2:T(8,128)(2,1)S(1)}, bf16[8,448,128]{1,0,2:T(8,128)(2,1)}, u32[]{:S(2)}) copy-start(bf16[8,448,128]{1,0,2:T(8,128)(2,1)} %copy.82) | copy-start | bytes 2752516
  58.6 1.3 copy-start.16
  61.7 15.1 %all-to-all-start.2 = ((bf16[64,16,256]{2,1,0:T(8,128)(2,1)}), bf16[64,16,256]{2,1,0:T(8,128)(2,1)S(1)}, u32[]{:S(2)}, u32[]{:S(2)}) async-start(bf16[64,16,256]{2,1,0:T(8,128)(2,1)} %copy.84), calls=%async_computation.2 | async-start | bytes 1048576 | tf_op jit(solution)/shard_map/all_to_all | solution.py:50
  68.7 3.0 %copy-start.15 = (bf16[8,448,256]{2,1,0:T(8,128)(2,1)S(1)}, bf16[8,448,256]{2,1,0:T(8,128)(2,1)}, u32[]{:S(2)}) copy-start(bf16[8,448,256]{2,1,0:T(8,128)(2,1)} %get-tuple-element.30) | copy-start | bytes 5505028
  76.8 6.1 %copy-start.11 = (bf16[64,16,256]{2,1,0:T(8,128)(2,1)}, bf16[64,16,256]{2,1,0:T(8,128)(2,1)S(1)}, u32[]{:S(2)}) copy-start(bf16[64,16,256]{2,1,0:T(8,128)(2,1)S(1)} %all-to-all-done.2) | copy-start | bytes 1572868
  76.8 23.4 %all-to-all-start.1 = ((bf16[2,64,16,256]{3,2,0,1:T(8,128)(2,1)}), bf16[2,64,16,256]{3,2,0,1:T(8,128)(2,1)}, u32[]{:S(2)}, u32[]{:S(2)}) async-start(bf16[2,64,16,256]{3,2,0,1:T(8,128)(2,1)} %pad_maximum_fusion.1), calls=%async_computation.1 | async-start | bytes 2097152 | tf_op jit(solution)/shard_map/all_to_all | solution.py:70
  83.0 81.8 %reduce-scatter.4.cloned.1.call-start = ((), (), s32[]{:S(2)}) async-start(), calls=%async_computation.6 | async-start | bytes 10616832 | tf_op jit(solution)/shard_map/reduce_scatter | solution.py:91
  89.7 2.9 %copy-start.10 = (bf16[1,8,8,16,256]{4,3,2,1,0:T(8,128)(2,1)S(1)}, bf16[1,8,8,16,256]{4,3,2,1,0:T(8,128)(2,1)}, u32[]{:S(2)}) copy-start(bf16[1,8,8,16,256]{4,3,2,1,0:T(8,128)(2,1)} %copy-done.9) | copy-start | bytes 1572868
  94.9 4.0 %copy-start.8 = (bf16[256,1024]{1,0:T(8,128)(2,1)S(1)}, bf16[256,1024]{1,0:T(8,128)(2,1)}, u32[]{:S(2)}) copy-start(bf16[256,1024]{1,0:T(8,128)(2,1)} %param.9) | copy-start | bytes 1572868
  100.3 1.5 copy-start.3
  103.3 5.4 %copy-start.2 = (f32[8,4,4,2,1792]{4,3,2,1,0:T(2,128)S(1)}, f32[8,4,4,2,1792]{4,3,2,1,0:T(2,128)}, u32[]{:S(2)}) copy-start(f32[8,4,4,2,1792]{4,3,2,1,0:T(2,128)} %concatenate.17) | copy-start | bytes 5505028
  104.4 4.2 %copy-start.13 = (f32[8,4,4,2,512]{4,3,2,1,0:T(2,128)S(1)}, f32[8,4,4,2,512]{4,3,2,1,0:T(2,128)}, u32[]{:S(2)}) copy-start(f32[8,4,4,2,512]{4,3,2,1,0:T(2,128)} %concatenate.16) | copy-start | bytes 1572868
  108.7 1.0 copy-start.14
  108.7 1.7 copy-start.1
  110.4 1.5 copy-start
  111.9 1.0 copy-start.12
  120.2 94.5 %reduce-scatter.6.cloned.1.call-start = ((), (), s32[]{:S(2)}) async-start(), calls=%async_computation.7 | async-start | bytes 4423680 | tf_op jit(solution)/shard_map/reduce_scatter | solution.py:91
  168.8 45.9 %copy-start.17 = (bf16[8,128,128]{2,1,0:T(8,128)(2,1)S(1)}, bf16[8,128,128]{2,1,0:T(8,128)(2,1)}, u32[]{:S(2)}) copy-start(bf16[8,128,128]{2,1,0:T(8,128)(2,1)} %param.10) | copy-start | bytes 786436
  168.8 46.2 %copy-start.18 = (bf16[8,128,128]{2,1,0:T(8,128)(2,1)S(1)}, bf16[8,128,128]{2,1,0:T(8,128)(2,1)}, u32[]{:S(2)}) copy-start(bf16[8,128,128]{2,1,0:T(8,128)(2,1)} %param.12) | copy-start | bytes 786436
  168.8 77.6 %reduce-scatter.8.cloned.1.call-start = ((), (), s32[]{:S(2)}) async-start(), calls=%async_computation.8 | async-start | bytes 1105920 | tf_op jit(solution)/shard_map/reduce_scatter | solution.py:91
Sparse Core Ops, SparseCore 0:
  120.3 44.4 reduce-scatter.3
  168.9 45.7 reduce-scatter.5
  217.2 29.1 reduce-scatter.7

commit v3 on v2

--- a/solution.py
+++ b/solution.py
@@ -88,7 +88,9 @@
     sizes = [lax.axis_size(name) for name in DP]
     summed = stacked.reshape(stacked.shape[0], *sizes, stacked.shape[2])
     for position in reversed(range(len(DP))):
-        summed = lax.psum_scatter(summed, DP[position], scatter_dimension=1 + position, tiled=True)
+        summed = lax.all_to_all(
+            summed, DP[position], split_axis=1 + position, concat_axis=1 + position, tiled=True
+        ).sum(axis=1 + position, keepdims=True)
     summed = summed.reshape(stacked.shape[0], 1, stacked.shape[2])
     outs = []
     start = 0

time: 260 us -> 227 us (0.87)
  waiting for transfers between devices: 147 us -> 45 us
  blocking collectives: 0 us -> 73.5 us
  between operations: 14.2 us -> 1.1 us
  starting transfers between devices: 22.3 us -> 32.3 us
  local copies, waits for them, and re-layouts: 51.6 us -> 45.6 us
  other arithmetic: 4.76 us -> 10.7 us
    reduce_scatter x3 -> x0, waiting for transfers between devices: 120 us -> none  [shards(): lax.psum_scatter(summed, DP[position], scatter_dimension=1 + position, ti...]
    all_to_all x0 -> x2, blocking collectives: none -> 73.5 us  [shards(): lax.all_to_all(summed, DP[position], split_axis=1 + position, concat_axis...]
    all_to_all x0 -> x1, waiting for transfers between devices: none -> 20.2 us  [shards(): lax.all_to_all(summed, DP[position], split_axis=1 + position, concat_axis...]
    all_to_all x0 -> x1, starting transfers between devices: none -> 8.75 us  [shards(): lax.all_to_all(summed, DP[position], split_axis=1 + position, concat_axis...]
    reduce_sum x0 -> x3, other arithmetic: none -> 7.58 us  [shards(): summed = lax.all_to_all(summed, DP[position], split_axis=1 + position, co...]
    concatenate x8, local copies, waits for them, and re-layouts: 19.5 us -> 13.3 us  [shards(): stacked = jnp.concatenate(flat, axis=2)]
    reduce_scatter x1 -> x0, local copies, waits for them, and re-layouts: 3.97 us -> none  [shards(): lax.psum_scatter(summed, DP[position], scatter_dimension=1 + position, ti...]
    broadcast_in_dim x0 -> x2, local copies, waits for them, and re-layouts: none -> 3.25 us  [shards(): summed = lax.all_to_all(summed, DP[position], split_axis=1 + position, co...]
  transfers between devices with their start and end apart: 6 -> 4, of which waited for: 5 -> 3; matrix products, arithmetic and copies ran while one was open for 11% -> 13% of each run, Pallas kernels for 0% -> 0%
where the time goes in v3:
time: 227 us; the launch traced here: 226 us
  blocking collectives  73.5 us (32%)
  local copies, waits for them, and re-layouts  45.6 us (20%)
  waiting for transfers between devices  45 us (20%)
  starting transfers between devices  32.3 us (14%)
  matrix products  18.1 us (8%)
  other arithmetic  10.7 us (5%)
    all_to_all x2, blocking collectives, shards(): lax.all_to_all(summed, DP[position], split_axis=1 + position, concat_axis...  73.5 us
    all_to_all x1, waiting for transfers between devices, shards(): lax.all_to_all(jnp.stack([gate_mid, up_mid, back_mid]), 'mp', split_axis=...  23.5 us
    all_to_all x1, waiting for transfers between devices, shards(): lax.all_to_all(summed, DP[position], split_axis=1 + position, concat_axis...  20.2 us
    unnamed x63, local copies, waits for them, and re-layouts  20.2 us
    concatenate x8, local copies, waits for them, and re-layouts, shards(): stacked = jnp.concatenate(flat, axis=2)  13.3 us
    all_to_all x1, starting transfers between devices, shards(): lax.all_to_all(jnp.stack([gate_mid, up_mid, back_mid]), 'mp', split_axis=...  11.8 us
    all_to_all x1, starting transfers between devices, shards(): lax.all_to_all(summed, DP[position], split_axis=1 + position, concat_axis...  8.75 us
    all_to_all x1, starting transfers between devices, shards(): lax.all_to_all(jnp.stack([narrow(gate_grad, gate_out), narrow(up_grad, up...  7.74 us
  transfers between devices with their start and end apart: 4, of which 3 were waited for; matrix products, arithmetic and copies ran while one was open for 13% of the time, Pallas kernels for 0%

profile of v3, /device:TPU:1, one launch (start us, length us, event | category | flops | bytes accessed | tf_op | source)
XLA Modules:
  0.0 226.3 jit_solution(17050245475701278778)
XLA Ops:
  0.6 1.1 copy.88
  1.8 1.1 copy.91
  2.9 1.1 copy.138
  6.1 1.4 pad_maximum_fusion
  7.4 11.8 %all-to-all-start = ((bf16[3,64,16,256]{3,2,0,1:T(8,128)(2,1)}), bf16[3,64,16,256]{3,2,0,1:T(8,128)(2,1)S(1)}, u32[]{:S(2)}, u32[]{:S(2)}) async-start(bf16[3,64,16,256]{3,2,0,1:T(8,128)(2,1)} %pad_maximum_fusion), calls=%async_computation | async-start | bytes 3145728 | tf_op jit(solution)/shard_map/all_to_all | solution.py:38
  19.2 1.8 copy.113
  21.0 23.5 %all-to-all-done = bf16[3,64,16,256]{3,2,0,1:T(8,128)(2,1)S(1)} async-done(((bf16[3,64,16,256]{3,2,0,1:T(8,128)(2,1)}), bf16[3,64,16,256]{3,2,0,1:T(8,128)(2,1)S(1)}, u32[]{:S(2)}, u32[]{:S(2)}) %all-to-all-start) | async-done | bytes 1572896 | tf_op jit(solution)/shard_map/all_to_all | solution.py:38
  44.9 1.2 copy-done.9
  48.5 3.6 %fusion.7 = (bf16[8,448,256]{2,1,0:T(8,128)(2,1)S(1)}, bf16[8,448,256]{2,1,0:T(8,128)(2,1)}, bf16[8,448,256]{2,1,0:T(8,128)(2,1)}) fusion(f32[8,256,448]{1,2,0:T(8,128)S(1)} %fusion.48, f32[8,256,448]{1,2,0:T(8,128)S(1)} %fusion.47, bf16[8,128,448]{1,2,0:T(8,128)(2,1)S(1)} %copy-done.23, bf16[8,128,256]{2,1,0:T(8,128)(2,1)S(1)} %bitcast.187), kind=kOutput, calls=%fused_computation.12 | convolution fusion | flops 248643584 | bytes 14286848 | tf_op jit(solution)/shard_map/jct,jco->jot/dot_general | solution.py:29
  52.0 1.2 copy-done.18
  55.2 4.1 %all-to-all-start.2 = ((bf16[64,16,256]{2,1,0:T(8,128)(2,1)}), bf16[64,16,256]{2,1,0:T(8,128)(2,1)S(1)}, u32[]{:S(2)}, u32[]{:S(2)}) async-start(bf16[64,16,256]{2,1,0:T(8,128)(2,1)} %copy.115), calls=%async_computation.2 | async-start | bytes 1048576 | tf_op jit(solution)/shard_map/all_to_all | solution.py:50
  59.2 1.9 copy.100
  61.1 2.7 %copy.102 = bf16[8,128,448]{2,0,1:T(8,128)(2,1)} copy(bf16[8,128,448]{1,2,0:T(8,128)(2,1)} %param.13) | data formatting | bytes 1835008 | tf_op args[5]
  63.8 2.7 %fusion.15 = bf16[8,256,64,2]{1,2,3,0:T(8,128)(2,1)S(1)} fusion(bf16[8,448,256]{2,1,0:T(8,128)(2,1)} %get-tuple-element.36, bf16[8,64,2,448]{3,0,2,1:T(8,128)(2,1)} %bitcast.199), kind=kOutput, calls=%fused_computation.24 | convolution fusion | flops 235143168 | bytes 3276800 | tf_op jit(solution)/shard_map/jot,jkpo->kjpt/dot_general | solution.py:67
  69.0 1.3 all-to-all-done.2
  71.1 7.7 %all-to-all-start.1 = ((bf16[2,64,16,256]{3,2,0,1:T(8,128)(2,1)}), bf16[2,64,16,256]{3,2,0,1:T(8,128)(2,1)}, u32[]{:S(2)}, u32[]{:S(2)}) async-start(bf16[2,64,16,256]{3,2,0,1:T(8,128)(2,1)} %pad_maximum_fusion.1), calls=%async_computation.1 | async-start | bytes 2097152 | tf_op jit(solution)/shard_map/all_to_all | solution.py:70
  78.9 2.1 fusion.46
  81.0 2.2 concatenate.20
  83.2 2.2 fusion.44
  85.4 2.9 %concatenate.17 = f32[8,4,4,2,1792]{4,3,2,1,0:T(2,128)} reshape(f32[8,128,448]{2,1,0:T(8,128)S(1)} %fusion.44) | data formatting | bytes 3670016 | tf_op jit(solution)/shard_map/concatenate | solution.py:87
  88.3 2.4 %fusion.45 = f32[8,128,448]{2,1,0:T(8,128)S(1)} fusion(bf16[8,128,256]{2,1,0:T(8,128)(2,1)} %bitcast.188, bf16[8,448,256]{2,1,0:T(8,128)(2,1)} %get-tuple-element.37), kind=kOutput, calls=%fused_computation.67 | convolution fusion | flops 234881024 | bytes 4194304 | tf_op jit(solution)/shard_map/jct,jot->jco/dot_general | solution.py:63
  90.7 2.9 %concatenate.19 = f32[8,4,4,2,1792]{4,3,2,1,0:T(2,128)} reshape(f32[8,128,448]{2,1,0:T(8,128)S(1)} %fusion.45) | data formatting | bytes 3670016 | tf_op jit(solution)/shard_map/concatenate | solution.py:87
  95.0 1.4 copy.173
  100.2 1.3 concatenate.18
  105.7 1.8 copy.118
  107.5 28.4 %all_to_all.63 = f32[8,4,4,2,6912]{4,2,1,0,3:T(4,128)} all-to-all(f32[8,4,4,2,6912]{4,2,1,0,3:T(4,128)S(1)} %copy.118), channel_id=1, replica_groups=mesh['dz'=4,'dx'=4,'dc'=2,'mp'=8] {'dc'}, dimensions={3} | all-to-all | bytes 14155776 | tf_op jit(solution)/shard_map/all_to_all | solution.py:91
  135.9 5.6 %reduce_sum.27 = f32[8,4,4,6912]{3,2,1,0:T(4,128)S(1)} reduce(f32[8,4,4,2,6912]{4,2,1,0,3:T(4,128)} %all_to_all.63, f32[]{:T(128)} %constant.4.clone.1), dimensions={3}, to_apply=%region_0.0 | reduce | flops 884736 | bytes 10616836 | tf_op jit(solution)/shard_map/reduce_sum | solution.py:93
  142.4 45.1 %all_to_all.64 = f32[8,4,4,1,6912]{4,1,0,3,2:T(4,128)S(1)} all-to-all(f32[8,4,4,1,6912]{4,1,0,3,2:T(4,128)S(1)} %copy.119), channel_id=1, replica_groups=mesh['dz'=4,'dx'=4,'dc'=2,'mp'=8] {'dx'}, dimensions={2} | all-to-all | bytes 7077888 | tf_op jit(solution)/shard_map/all_to_all | solution.py:91
  187.4 2.0 reduce_sum.28
  189.4 2.3 %copy.120 = f32[8,4,1,1,6912]{4,0,3,2,1:T(8,128)} copy(f32[8,4,1,1,6912]{4,1,0,3,2:T(4,128)} %bitcast.184) | data formatting | bytes 1769472 | tf_op jit(solution)/shard_map/broadcast_in_dim | solution.py:93
  191.8 8.8 %all-to-all-start.5 = ((f32[8,4,1,1,6912]{4,0,3,2,1:T(8,128)}), f32[8,4,1,1,6912]{4,0,3,2,1:T(8,128)S(1)}, u32[]{:S(2)}, u32[]{:S(2)}) async-start(f32[8,4,1,1,6912]{4,0,3,2,1:T(8,128)} %copy.120), calls=%async_computation.5 | async-start | bytes 1769472 | tf_op jit(solution)/shard_map/all_to_all | solution.py:91
  202.1 20.2 %all-to-all-done.5 = f32[8,4,1,1,6912]{4,0,3,2,1:T(8,128)S(1)} async-done(((f32[8,4,1,1,6912]{4,0,3,2,1:T(8,128)}), f32[8,4,1,1,6912]{4,0,3,2,1:T(8,128)S(1)}, u32[]{:S(2)}, u32[]{:S(2)}) %all-to-all-start.5) | async-done | bytes 884768 | tf_op jit(solution)/shard_map/all_to_all | solution.py:91
  (93 shorter events, 25.5 us)
Async XLA Ops:
  4.1 1.3 copy-start.11
  4.4 1.0 copy-start.24
  7.4 11.8 %copy-start.8 = (bf16[8,448,128]{2,1,0:T(8,128)(2,1)S(1)}, bf16[8,448,128]{2,1,0:T(8,128)(2,1)}, u32[]{:S(2)}) copy-start(bf16[8,448,128]{2,1,0:T(8,128)(2,1)} %param.14) | copy-start | bytes 2752516
  7.4 37.1 %all-to-all-start = ((bf16[3,64,16,256]{3,2,0,1:T(8,128)(2,1)}), bf16[3,64,16,256]{3,2,0,1:T(8,128)(2,1)S(1)}, u32[]{:S(2)}, u32[]{:S(2)}) async-start(bf16[3,64,16,256]{3,2,0,1:T(8,128)(2,1)} %pad_maximum_fusion), calls=%async_computation | async-start | bytes 3145728 | tf_op jit(solution)/shard_map/all_to_all | solution.py:38
  44.7 1.4 copy-start.9
  44.9 7.2 %copy-start.12 = (bf16[1,8,8,16,256]{4,3,2,1,0:T(8,128)(2,1)}, bf16[1,8,8,16,256]{4,3,2,1,0:T(8,128)(2,1)S(1)}, u32[]{:S(2)}) copy-start(bf16[1,8,8,16,256]{4,3,2,1,0:T(8,128)(2,1)S(1)} %get-tuple-element.38) | copy-start | bytes 1572868
  46.1 1.2 copy-start.10
  47.3 1.2 copy-start.23
  48.5 4.8 %copy-start.21 = (bf16[8,448,128]{1,0,2:T(8,128)(2,1)S(1)}, bf16[8,448,128]{1,0,2:T(8,128)(2,1)}, u32[]{:S(2)}) copy-start(bf16[8,448,128]{1,0,2:T(8,128)(2,1)} %copy.113) | copy-start | bytes 2752516
  52.0 1.2 copy-start.18
  55.2 15.1 %all-to-all-start.2 = ((bf16[64,16,256]{2,1,0:T(8,128)(2,1)}), bf16[64,16,256]{2,1,0:T(8,128)(2,1)S(1)}, u32[]{:S(2)}, u32[]{:S(2)}) async-start(bf16[64,16,256]{2,1,0:T(8,128)(2,1)} %copy.115), calls=%async_computation.2 | async-start | bytes 1048576 | tf_op jit(solution)/shard_map/all_to_all | solution.py:50
  63.8 3.0 %copy-start.17 = (bf16[8,448,256]{2,1,0:T(8,128)(2,1)S(1)}, bf16[8,448,256]{2,1,0:T(8,128)(2,1)}, u32[]{:S(2)}) copy-start(bf16[8,448,256]{2,1,0:T(8,128)(2,1)} %get-tuple-element.37) | copy-start | bytes 5505028
  63.8 3.0 %copy-start.22 = (bf16[8,128,448]{2,0,1:T(8,128)(2,1)S(1)}, bf16[8,128,448]{2,0,1:T(8,128)(2,1)}, u32[]{:S(2)}) copy-start(bf16[8,128,448]{2,0,1:T(8,128)(2,1)} %copy.102) | copy-start | bytes 2752516
  70.3 0.8 copy-start.13
  71.1 23.9 %all-to-all-start.1 = ((bf16[2,64,16,256]{3,2,0,1:T(8,128)(2,1)}), bf16[2,64,16,256]{3,2,0,1:T(8,128)(2,1)}, u32[]{:S(2)}, u32[]{:S(2)}) async-start(bf16[2,64,16,256]{3,2,0,1:T(8,128)(2,1)} %pad_maximum_fusion.1), calls=%async_computation.1 | async-start | bytes 2097152 | tf_op jit(solution)/shard_map/all_to_all | solution.py:70
  90.7 2.9 %copy-start.14 = (bf16[64,16,256]{2,1,0:T(8,128)(2,1)S(1)}, bf16[64,16,256]{2,1,0:T(8,128)(2,1)}, u32[]{:S(2)}) copy-start(bf16[64,16,256]{2,1,0:T(8,128)(2,1)} %copy-done.13) | copy-start | bytes 1572868
  95.0 2.3 %copy-start.3 = (bf16[256,1024]{1,0:T(8,128)(2,1)S(1)}, bf16[256,1024]{1,0:T(8,128)(2,1)}, u32[]{:S(2)}) copy-start(bf16[256,1024]{1,0:T(8,128)(2,1)} %param.8) | copy-start | bytes 1572868
  96.5 0.8 copy-start.4
  96.5 2.6 %copy-start.6 = (bf16[1,8,8,16,256]{4,3,2,1,0:T(8,128)(2,1)}, bf16[1,8,8,16,256]{4,3,2,1,0:T(8,128)(2,1)S(1)}, u32[]{:S(2)}) copy-start(bf16[1,8,8,16,256]{4,3,2,1,0:T(8,128)(2,1)S(1)} %get-tuple-element.41) | copy-start | bytes 1572868
  98.9 2.7 %copy-start.2 = (f32[8,4,4,2,1792]{4,3,2,1,0:T(2,128)S(1)}, f32[8,4,4,2,1792]{4,3,2,1,0:T(2,128)}, u32[]{:S(2)}) copy-start(f32[8,4,4,2,1792]{4,3,2,1,0:T(2,128)} %concatenate.17) | copy-start | bytes 5505028
  99.2 2.3 %copy-start.16 = (f32[8,4,4,2,512]{4,3,2,1,0:T(2,128)S(1)}, f32[8,4,4,2,512]{4,3,2,1,0:T(2,128)}, u32[]{:S(2)}) copy-start(f32[8,4,4,2,512]{4,3,2,1,0:T(2,128)} %concatenate.16) | copy-start | bytes 1572868
  101.5 1.5 copy-start.1
  103.0 1.5 copy-start
  104.5 1.0 copy-start.15
  189.4 11.1 %copy-start.5 = (bf16[1,8,8,16,256]{4,3,2,1,0:T(8,128)(2,1)S(1)}, bf16[1,8,8,16,256]{4,3,2,1,0:T(8,128)(2,1)}, u32[]{:S(2)}) copy-start(bf16[1,8,8,16,256]{4,3,2,1,0:T(8,128)(2,1)} %copy-done.4) | copy-start | bytes 1572868
  189.4 11.1 %copy-start.19 = (bf16[8,128,128]{2,1,0:T(8,128)(2,1)S(1)}, bf16[8,128,128]{2,1,0:T(8,128)(2,1)}, u32[]{:S(2)}) copy-start(bf16[8,128,128]{2,1,0:T(8,128)(2,1)} %param.10) | copy-start | bytes 786436
  191.8 9.1 %copy-start.7 = (bf16[1,8,8,16,256]{4,3,2,1,0:T(8,128)(2,1)S(1)}, bf16[1,8,8,16,256]{4,3,2,1,0:T(8,128)(2,1)}, u32[]{:S(2)}) copy-start(bf16[1,8,8,16,256]{4,3,2,1,0:T(8,128)(2,1)} %copy-done.6) | copy-start | bytes 1572868
  191.8 9.1 %copy-start.20 = (bf16[8,128,128]{2,1,0:T(8,128)(2,1)S(1)}, bf16[8,128,128]{2,1,0:T(8,128)(2,1)}, u32[]{:S(2)}) copy-start(bf16[8,128,128]{2,1,0:T(8,128)(2,1)} %param.12) | copy-start | bytes 786436
  191.8 30.5 %all-to-all-start.5 = ((f32[8,4,1,1,6912]{4,0,3,2,1:T(8,128)}), f32[8,4,1,1,6912]{4,0,3,2,1:T(8,128)S(1)}, u32[]{:S(2)}, u32[]{:S(2)}) async-start(f32[8,4,1,1,6912]{4,0,3,2,1:T(8,128)} %copy.120), calls=%async_computation.5 | async-start | bytes 1769472 | tf_op jit(solution)/shard_map/all_to_all | solution.py:91

commit v4 on v3

--- a/solution.py
+++ b/solution.py
@@ -88,9 +88,10 @@
     sizes = [lax.axis_size(name) for name in DP]
     summed = stacked.reshape(stacked.shape[0], *sizes, stacked.shape[2])
     for position in reversed(range(len(DP))):
+        wire = summed if position == len(DP) - 1 else summed.astype(jnp.bfloat16)
         summed = lax.all_to_all(
-            summed, DP[position], split_axis=1 + position, concat_axis=1 + position, tiled=True
-        ).sum(axis=1 + position, keepdims=True)
+            wire, DP[position], split_axis=1 + position, concat_axis=1 + position, tiled=True
+        ).astype(jnp.float32).sum(axis=1 + position, keepdims=True)
     summed = summed.reshape(stacked.shape[0], 1, stacked.shape[2])
     outs = []
     start = 0

time: 227 us -> 196 us (0.86)
  blocking collectives: 73.5 us -> 55.2 us
  waiting for transfers between devices: 45 us -> 35.5 us
    all_to_all x2, blocking collectives: 73.5 us -> 55.2 us  [shards(): lax.all_to_all(wire, DP[position], split_axis=1 + position, concat_axis=1...]
    all_to_all x1, waiting for transfers between devices: 20.2 us -> 10.6 us  [shards(): lax.all_to_all(wire, DP[position], split_axis=1 + position, concat_axis=1...]
    broadcast_in_dim x2 -> x0, local copies, waits for them, and re-layouts: 3.25 us -> none  [shards(): summed = lax.all_to_all(summed, DP[position], split_axis=1 + position, co...]
    unnamed x63 -> x67, local copies, waits for them, and re-layouts: 20.2 us -> 20.2 us
  transfers between devices with their start and end apart: 4 -> 4, of which waited for: 3 -> 3; matrix products, arithmetic and copies ran while one was open for 13% -> 15% of each run, Pallas kernels for 0% -> 0%
where the time goes in v4:
time: 196 us; the launch traced here: 195 us
  blocking collectives  55.2 us (28%)
  local copies, waits for them, and re-layouts  43.9 us (22%)
  waiting for transfers between devices  35.5 us (18%)
  starting transfers between devices  31.6 us (16%)
  matrix products  17.9 us (9%)
  other arithmetic  9.93 us (5%)
    all_to_all x2, blocking collectives, shards(): lax.all_to_all(wire, DP[position], split_axis=1 + position, concat_axis=1...  55.2 us
    all_to_all x1, waiting for transfers between devices, shards(): lax.all_to_all(jnp.stack([gate_mid, up_mid, back_mid]), 'mp', split_axis=...  23.5 us
    unnamed x67, local copies, waits for them, and re-layouts  20.2 us
    concatenate x8, local copies, waits for them, and re-layouts, shards(): stacked = jnp.concatenate(flat, axis=2)  13.4 us
    all_to_all x1, starting transfers between devices, shards(): lax.all_to_all(jnp.stack([gate_mid, up_mid, back_mid]), 'mp', split_axis=...  11.8 us
    all_to_all x1, waiting for transfers between devices, shards(): lax.all_to_all(wire, DP[position], split_axis=1 + position, concat_axis=1...  10.6 us
    all_to_all x1, starting transfers between devices, shards(): lax.all_to_all(wire, DP[position], split_axis=1 + position, concat_axis=1...  7.98 us
    all_to_all x1, starting transfers between devices, shards(): lax.all_to_all(jnp.stack([narrow(gate_grad, gate_out), narrow(up_grad, up...  7.72 us
  transfers between devices with their start and end apart: 4, of which 3 were waited for; matrix products, arithmetic and copies ran while one was open for 15% of the time, Pallas kernels for 0%

profile of v4, /device:TPU:1, one launch (start us, length us, event | category | flops | bytes accessed | tf_op | source)
XLA Modules:
  0.0 195.2 jit_solution(11559601574837449792)
XLA Ops:
  0.6 1.1 copy.88
  2.9 1.1 copy.138
  6.1 1.4 pad_maximum_fusion
  7.4 11.8 %all-to-all-start = ((bf16[3,64,16,256]{3,2,0,1:T(8,128)(2,1)}), bf16[3,64,16,256]{3,2,0,1:T(8,128)(2,1)S(1)}, u32[]{:S(2)}, u32[]{:S(2)}) async-start(bf16[3,64,16,256]{3,2,0,1:T(8,128)(2,1)} %pad_maximum_fusion), calls=%async_computation | async-start | bytes 3145728 | tf_op jit(solution)/shard_map/all_to_all | solution.py:38
  19.2 1.8 copy.113
  21.0 23.5 %all-to-all-done = bf16[3,64,16,256]{3,2,0,1:T(8,128)(2,1)S(1)} async-done(((bf16[3,64,16,256]{3,2,0,1:T(8,128)(2,1)}), bf16[3,64,16,256]{3,2,0,1:T(8,128)(2,1)S(1)}, u32[]{:S(2)}, u32[]{:S(2)}) %all-to-all-start) | async-done | bytes 1572896 | tf_op jit(solution)/shard_map/all_to_all | solution.py:38
  44.9 1.2 copy-done.9
  48.5 3.5 %fusion.7 = (bf16[8,448,256]{2,1,0:T(8,128)(2,1)S(1)}, bf16[8,448,256]{2,1,0:T(8,128)(2,1)}, bf16[8,448,256]{2,1,0:T(8,128)(2,1)}) fusion(f32[8,256,448]{1,2,0:T(8,128)S(1)} %fusion.48, f32[8,256,448]{1,2,0:T(8,128)S(1)} %fusion.47, bf16[8,128,448]{1,2,0:T(8,128)(2,1)S(1)} %copy-done.25, bf16[8,128,256]{2,1,0:T(8,128)(2,1)S(1)} %bitcast.188), kind=kOutput, calls=%fused_computation.12 | convolution fusion | flops 248643584 | bytes 14286848 | tf_op jit(solution)/shard_map/jct,jco->jot/dot_general | solution.py:29
  52.0 1.2 copy-done.20
  54.0 1.1 copy.115
  55.2 4.1 %all-to-all-start.2 = ((bf16[64,16,256]{2,1,0:T(8,128)(2,1)}), bf16[64,16,256]{2,1,0:T(8,128)(2,1)S(1)}, u32[]{:S(2)}, u32[]{:S(2)}) async-start(bf16[64,16,256]{2,1,0:T(8,128)(2,1)} %copy.115), calls=%async_computation.2 | async-start | bytes 1048576 | tf_op jit(solution)/shard_map/all_to_all | solution.py:50
  59.3 1.9 copy.100
  61.1 2.7 %copy.102 = bf16[8,128,448]{2,0,1:T(8,128)(2,1)} copy(bf16[8,128,448]{1,2,0:T(8,128)(2,1)} %param.13) | data formatting | bytes 1835008 | tf_op args[5]
  63.8 2.7 %fusion.15 = bf16[8,256,64,2]{1,2,3,0:T(8,128)(2,1)S(1)} fusion(bf16[8,448,256]{2,1,0:T(8,128)(2,1)} %get-tuple-element.36, bf16[8,64,2,448]{3,0,2,1:T(8,128)(2,1)} %bitcast.201), kind=kOutput, calls=%fused_computation.25 | convolution fusion | flops 235143168 | bytes 3276800 | tf_op jit(solution)/shard_map/jot,jkpo->kjpt/dot_general | solution.py:67
  69.0 1.3 all-to-all-done.2
  71.1 7.7 %all-to-all-start.1 = ((bf16[2,64,16,256]{3,2,0,1:T(8,128)(2,1)}), bf16[2,64,16,256]{3,2,0,1:T(8,128)(2,1)}, u32[]{:S(2)}, u32[]{:S(2)}) async-start(bf16[2,64,16,256]{3,2,0,1:T(8,128)(2,1)} %pad_maximum_fusion.1), calls=%async_computation.1 | async-start | bytes 2097152 | tf_op jit(solution)/shard_map/all_to_all | solution.py:70
  78.9 2.1 %fusion.46 = f32[8,448,128]{2,1,0:T(8,128)S(1)} fusion(bf16[8,448,256]{2,1,0:T(8,128)(2,1)} %copy-done.20, bf16[8,128,256]{2,1,0:T(8,128)(2,1)S(1)} %bitcast.184), kind=kOutput, calls=%fused_computation.70 | convolution fusion | flops 234881024 | bytes 4194304 | tf_op jit(solution)/shard_map/jot,jqt->joq/dot_general | solution.py:54
  81.0 2.2 %concatenate.20 = f32[8,4,4,2,1792]{4,3,2,1,0:T(2,128)} reshape(f32[8,448,128]{2,1,0:T(8,128)S(1)} %fusion.46) | data formatting | bytes 3670016 | tf_op jit(solution)/shard_map/concatenate | solution.py:87
  83.2 2.2 %fusion.44 = f32[8,128,448]{2,1,0:T(8,128)S(1)} fusion(bf16[8,128,256]{2,1,0:T(8,128)(2,1)S(1)} %bitcast.178, bf16[8,448,256]{2,1,0:T(8,128)(2,1)} %get-tuple-element.36), kind=kOutput, calls=%fused_computation.68 | convolution fusion | flops 234881024 | bytes 4194304 | tf_op jit(solution)/shard_map/jct,jot->jco/dot_general | solution.py:60
  85.4 2.9 %concatenate.17 = f32[8,4,4,2,1792]{4,3,2,1,0:T(2,128)} reshape(f32[8,128,448]{2,1,0:T(8,128)S(1)} %fusion.44) | data formatting | bytes 3670016 | tf_op jit(solution)/shard_map/concatenate | solution.py:87
  88.3 2.2 %fusion.45 = f32[8,128,448]{2,1,0:T(8,128)S(1)} fusion(bf16[8,128,256]{2,1,0:T(8,128)(2,1)S(1)} %bitcast.189, bf16[8,448,256]{2,1,0:T(8,128)(2,1)} %get-tuple-element.37), kind=kOutput, calls=%fused_computation.69 | convolution fusion | flops 234881024 | bytes 4194304 | tf_op jit(solution)/shard_map/jct,jot->jco/dot_general | solution.py:63
  90.5 2.9 %concatenate.19 = f32[8,4,4,2,1792]{4,3,2,1,0:T(2,128)} reshape(f32[8,128,448]{2,1,0:T(8,128)S(1)} %fusion.45) | data formatting | bytes 3670016 | tf_op jit(solution)/shard_map/concatenate | solution.py:87
  94.9 1.4 copy.173
  100.1 1.3 concatenate.18
  103.2 1.2 copy-done
  105.6 1.8 copy.118
  107.4 29.3 %all_to_all.63 = f32[8,4,4,2,6912]{4,2,1,0,3:T(4,128)} all-to-all(f32[8,4,4,2,6912]{4,2,1,0,3:T(4,128)S(1)} %copy.118), channel_id=1, replica_groups=mesh['dz'=4,'dx'=4,'dc'=2,'mp'=8] {'dc'}, dimensions={3} | all-to-all | bytes 14155776 | tf_op jit(solution)/shard_map/all_to_all | solution.py:92
  136.7 5.6 %reduce_sum.30 = bf16[8,4,4,6912]{3,2,1,0:T(4,128)(2,1)S(1)} reduce(f32[8,4,4,2,6912]{4,2,1,0,3:T(4,128)} %all_to_all.63, f32[]{:T(128)} %constant.1.clone.1), dimensions={3}, to_apply=%region_0.0 | reduce | flops 884736 | bytes 8847364 | tf_op jit(solution)/shard_map/reduce_sum | solution.py:94
  143.0 25.9 %all_to_all.64 = bf16[8,4,4,1,6912]{4,1,0,3,2:T(4,128)(2,1)S(1)} all-to-all(bf16[8,4,4,1,6912]{4,1,0,3,2:T(4,128)(2,1)S(1)} %copy.119), channel_id=1, replica_groups=mesh['dz'=4,'dx'=4,'dc'=2,'mp'=8] {'dx'}, dimensions={2} | all-to-all | bytes 3538944 | tf_op jit(solution)/shard_map/all_to_all | solution.py:92
  168.8 1.2 reduce_sum.31
  170.9 8.0 %all-to-all-start.5 = ((bf16[8,4,1,1,6912]{4,0,3,2,1:T(8,128)(2,1)}), bf16[8,4,1,1,6912]{4,0,3,2,1:T(8,128)(2,1)S(1)}, u32[]{:S(2)}, u32[]{:S(2)}) async-start(bf16[8,4,1,1,6912]{4,0,3,2,1:T(8,128)(2,1)} %copy.120), calls=%async_computation.5 | async-start | bytes 884736 | tf_op jit(solution)/shard_map/all_to_all | solution.py:92
  180.5 10.6 %all-to-all-done.5 = bf16[8,4,1,1,6912]{4,0,3,2,1:T(8,128)(2,1)S(1)} async-done(((bf16[8,4,1,1,6912]{4,0,3,2,1:T(8,128)(2,1)}), bf16[8,4,1,1,6912]{4,0,3,2,1:T(8,128)(2,1)S(1)}, u32[]{:S(2)}, u32[]{:S(2)}) %all-to-all-start.5) | async-done | bytes 442400 | tf_op jit(solution)/shard_map/all_to_all | solution.py:92
  (97 shorter events, 24.9 us)
Async XLA Ops:
  4.1 1.3 copy-start.11
  4.4 1.1 copy-start.26
  7.4 11.8 %copy-start.8 = (bf16[8,448,128]{2,1,0:T(8,128)(2,1)S(1)}, bf16[8,448,128]{2,1,0:T(8,128)(2,1)}, u32[]{:S(2)}) copy-start(bf16[8,448,128]{2,1,0:T(8,128)(2,1)} %param.14) | copy-start | bytes 2752516
  7.4 37.2 %all-to-all-start = ((bf16[3,64,16,256]{3,2,0,1:T(8,128)(2,1)}), bf16[3,64,16,256]{3,2,0,1:T(8,128)(2,1)S(1)}, u32[]{:S(2)}, u32[]{:S(2)}) async-start(bf16[3,64,16,256]{3,2,0,1:T(8,128)(2,1)} %pad_maximum_fusion), calls=%async_computation | async-start | bytes 3145728 | tf_op jit(solution)/shard_map/all_to_all | solution.py:38
  44.8 1.4 copy-start.9
  44.9 3.1 %copy-start.13 = (bf16[1,8,8,16,256]{4,3,2,1,0:T(8,128)(2,1)}, bf16[1,8,8,16,256]{4,3,2,1,0:T(8,128)(2,1)S(1)}, u32[]{:S(2)}) copy-start(bf16[1,8,8,16,256]{4,3,2,1,0:T(8,128)(2,1)S(1)} %get-tuple-element.38) | copy-start | bytes 1572868
  46.1 1.2 copy-start.10
  47.3 1.2 copy-start.25
  48.5 4.8 %copy-start.23 = (bf16[8,448,128]{1,0,2:T(8,128)(2,1)S(1)}, bf16[8,448,128]{1,0,2:T(8,128)(2,1)}, u32[]{:S(2)}) copy-start(bf16[8,448,128]{1,0,2:T(8,128)(2,1)} %copy.113) | copy-start | bytes 2752516
  52.0 1.2 copy-start.20
  55.2 15.1 %all-to-all-start.2 = ((bf16[64,16,256]{2,1,0:T(8,128)(2,1)}), bf16[64,16,256]{2,1,0:T(8,128)(2,1)S(1)}, u32[]{:S(2)}, u32[]{:S(2)}) async-start(bf16[64,16,256]{2,1,0:T(8,128)(2,1)} %copy.115), calls=%async_computation.2 | async-start | bytes 1048576 | tf_op jit(solution)/shard_map/all_to_all | solution.py:50
  63.8 3.0 %copy-start.19 = (bf16[8,448,256]{2,1,0:T(8,128)(2,1)S(1)}, bf16[8,448,256]{2,1,0:T(8,128)(2,1)}, u32[]{:S(2)}) copy-start(bf16[8,448,256]{2,1,0:T(8,128)(2,1)} %get-tuple-element.37) | copy-start | bytes 5505028
  63.8 3.0 %copy-start.24 = (bf16[8,128,448]{2,0,1:T(8,128)(2,1)S(1)}, bf16[8,128,448]{2,0,1:T(8,128)(2,1)}, u32[]{:S(2)}) copy-start(bf16[8,128,448]{2,0,1:T(8,128)(2,1)} %copy.102) | copy-start | bytes 2752516
  70.3 0.8 copy-start.15
  71.1 23.8 %all-to-all-start.1 = ((bf16[2,64,16,256]{3,2,0,1:T(8,128)(2,1)}), bf16[2,64,16,256]{3,2,0,1:T(8,128)(2,1)}, u32[]{:S(2)}, u32[]{:S(2)}) async-start(bf16[2,64,16,256]{3,2,0,1:T(8,128)(2,1)} %pad_maximum_fusion.1), calls=%async_computation.1 | async-start | bytes 2097152 | tf_op jit(solution)/shard_map/all_to_all | solution.py:70
  85.4 2.9 %copy-start.14 = (bf16[1,8,8,16,256]{4,3,2,1,0:T(8,128)(2,1)S(1)}, bf16[1,8,8,16,256]{4,3,2,1,0:T(8,128)(2,1)}, u32[]{:S(2)}) copy-start(bf16[1,8,8,16,256]{4,3,2,1,0:T(8,128)(2,1)} %copy-done.13) | copy-start | bytes 1572868
  90.5 2.9 %copy-start.16 = (bf16[64,16,256]{2,1,0:T(8,128)(2,1)S(1)}, bf16[64,16,256]{2,1,0:T(8,128)(2,1)}, u32[]{:S(2)}) copy-start(bf16[64,16,256]{2,1,0:T(8,128)(2,1)} %copy-done.15) | copy-start | bytes 1572868
  90.5 3.0 %copy-start.12 = (bf16[256,1024]{1,0:T(8,128)(2,1)S(1)}, bf16[256,1024]{1,0:T(8,128)(2,1)}, u32[]{:S(2)}) copy-start(bf16[256,1024]{1,0:T(8,128)(2,1)} %param.9) | copy-start | bytes 1572868
  94.9 2.3 %copy-start.3 = (bf16[256,1024]{1,0:T(8,128)(2,1)S(1)}, bf16[256,1024]{1,0:T(8,128)(2,1)}, u32[]{:S(2)}) copy-start(bf16[256,1024]{1,0:T(8,128)(2,1)} %param.8) | copy-start | bytes 1572868
  96.4 0.8 copy-start.4
  96.4 2.6 %copy-start.6 = (bf16[1,8,8,16,256]{4,3,2,1,0:T(8,128)(2,1)}, bf16[1,8,8,16,256]{4,3,2,1,0:T(8,128)(2,1)S(1)}, u32[]{:S(2)}) copy-start(bf16[1,8,8,16,256]{4,3,2,1,0:T(8,128)(2,1)S(1)} %get-tuple-element.41) | copy-start | bytes 1572868
  98.8 2.7 %copy-start.2 = (f32[8,4,4,2,1792]{4,3,2,1,0:T(2,128)S(1)}, f32[8,4,4,2,1792]{4,3,2,1,0:T(2,128)}, u32[]{:S(2)}) copy-start(f32[8,4,4,2,1792]{4,3,2,1,0:T(2,128)} %concatenate.17) | copy-start | bytes 5505028
  99.1 2.3 %copy-start.18 = (f32[8,4,4,2,512]{4,3,2,1,0:T(2,128)S(1)}, f32[8,4,4,2,512]{4,3,2,1,0:T(2,128)}, u32[]{:S(2)}) copy-start(f32[8,4,4,2,512]{4,3,2,1,0:T(2,128)} %concatenate.16) | copy-start | bytes 1572868
  101.4 1.5 copy-start.1
  102.9 1.5 copy-start
  104.4 1.0 copy-start.17
  168.8 10.1 %copy-start.5 = (bf16[1,8,8,16,256]{4,3,2,1,0:T(8,128)(2,1)S(1)}, bf16[1,8,8,16,256]{4,3,2,1,0:T(8,128)(2,1)}, u32[]{:S(2)}) copy-start(bf16[1,8,8,16,256]{4,3,2,1,0:T(8,128)(2,1)} %copy-done.4) | copy-start | bytes 1572868
  168.8 10.1 %copy-start.21 = (bf16[8,128,128]{2,1,0:T(8,128)(2,1)S(1)}, bf16[8,128,128]{2,1,0:T(8,128)(2,1)}, u32[]{:S(2)}) copy-start(bf16[8,128,128]{2,1,0:T(8,128)(2,1)} %param.10) | copy-start | bytes 786436
  170.1 9.1 %copy-start.7 = (bf16[1,8,8,16,256]{4,3,2,1,0:T(8,128)(2,1)S(1)}, bf16[1,8,8,16,256]{4,3,2,1,0:T(8,128)(2,1)}, u32[]{:S(2)}) copy-start(bf16[1,8,8,16,256]{4,3,2,1,0:T(8,128)(2,1)} %copy-done.6) | copy-start | bytes 1572868
  170.1 9.1 %copy-start.22 = (bf16[8,128,128]{2,1,0:T(8,128)(2,1)S(1)}, bf16[8,128,128]{2,1,0:T(8,128)(2,1)}, u32[]{:S(2)}) copy-start(bf16[8,128,128]{2,1,0:T(8,128)(2,1)} %param.12) | copy-start | bytes 786436
  170.9 20.2 %all-to-all-start.5 = ((bf16[8,4,1,1,6912]{4,0,3,2,1:T(8,128)(2,1)}), bf16[8,4,1,1,6912]{4,0,3,2,1:T(8,128)(2,1)S(1)}, u32[]{:S(2)}, u32[]{:S(2)}) async-start(bf16[8,4,1,1,6912]{4,0,3,2,1:T(8,128)(2,1)} %copy.120), calls=%async_computation.5 | async-start | bytes 884736 | tf_op jit(solution)/shard_map/all_to_all | solution.py:92

commit v5 on v4

--- a/solution.py
+++ b/solution.py
@@ -82,23 +82,38 @@
     term_up_in = jnp.einsum("tki,kot->kio", x_blocks, up_back, preferred_element_type=jnp.float32)
     grad_x = input_grad.astype(jnp.bfloat16).reshape(rows, local_blocks * BLK)
     terms = (term_gate_in, term_gate_out, term_up_in, term_up_out, term_down_in, term_down_out)
-    flat = [term.reshape(term.shape[0], groups, -1) for term in terms]
-    widths = [piece.shape[2] for piece in flat]
-    stacked = jnp.concatenate(flat, axis=2)
     sizes = [lax.axis_size(name) for name in DP]
-    summed = stacked.reshape(stacked.shape[0], *sizes, stacked.shape[2])
-    for position in reversed(range(len(DP))):
+
+    def reduce_stage(summed, position, ring=False):
         wire = summed if position == len(DP) - 1 else summed.astype(jnp.bfloat16)
-        summed = lax.all_to_all(
+        if ring:
+            return lax.psum_scatter(
+                wire, DP[position], scatter_dimension=1 + position, tiled=True
+            ).astype(jnp.float32)
+        return lax.all_to_all(
             wire, DP[position], split_axis=1 + position, concat_axis=1 + position, tiled=True
         ).astype(jnp.float32).sum(axis=1 + position, keepdims=True)
-    summed = summed.reshape(stacked.shape[0], 1, stacked.shape[2])
-    outs = []
+
+    def inner_stages(members, ring):
+        flat = [terms[m].reshape(terms[m].shape[0], groups, -1) for m in members]
+        stacked = jnp.concatenate(flat, axis=2)
+        summed = stacked.reshape(stacked.shape[0], *sizes, stacked.shape[2])
+        for position in reversed(range(1, len(DP))):
+            summed = reduce_stage(summed, position, ring)
+        return summed, [piece.shape[2] for piece in flat]
+
+    order = (1, 3, 4, 5, 0, 2)
+    early, early_widths = inner_stages(order[:4], True)
+    late, late_widths = inner_stages(order[4:], False)
+    summed = reduce_stage(jnp.concatenate([early, late], axis=-1), 0)
+    summed = summed.reshape(summed.shape[0], summed.shape[-1])
+    outs = [None] * len(terms)
     start = 0
-    for term, width in zip(terms, widths):
-        piece = summed[:, 0, start:start + width]
+    for member, width in zip(order, early_widths + late_widths):
+        term = terms[member]
+        piece = summed[:, start:start + width]
         start += width
-        outs.append(piece.reshape(term.shape[0], term.shape[1] // groups, term.shape[2]) * scale)
+        outs[member] = piece.reshape(term.shape[0], term.shape[1] // groups, term.shape[2]) * scale
     return (grad_x, *outs)
 
 

time: 196 us -> 217 us (1.11)
  waiting for transfers between devices: 35.5 us -> 59.8 us
  between operations: 1.14 us -> 14.5 us
  starting transfers between devices: 31.6 us -> 21.7 us
  local copies, waits for them, and re-layouts: 43.9 us -> 37.5 us
  blocking collectives: 55.2 us -> 50.5 us
    reduce_scatter x0 -> x2, waiting for transfers between devices: none -> 27.4 us  [reduce_stage(): lax.psum_scatter(wire, DP[position], scatter_dimension=1 + position, tile...]
    all_to_all x2 -> x1, starting transfers between devices: 15.7 us -> 5.32 us  [reduce_stage(): lax.all_to_all(wire, DP[position], split_axis=1 + position, concat_axis=1...]
    unnamed x67 -> x42, local copies, waits for them, and re-layouts: 20.2 us -> 12.9 us
    concatenate x0 -> x3, other arithmetic: none -> 6.96 us  [the longest x2 5.14 us: inner_stages(): stacked = jnp.concatenate(flat, axis=2)]
    reduce_sum x3, other arithmetic: 6.85 us -> 0.63 us  [reduce_stage(): return lax.all_to_all(wire, DP[position], split_axis=1 + position, concat...]
    all_to_all x2 -> x3, blocking collectives: 55.2 us -> 50.5 us  [the longest x1 30.5 us: shards(): lax.all_to_all(jnp.stack([narrow(gate_grad, gate_out), narrow(up_grad, up...]
    concatenate x8 -> x9, local copies, waits for them, and re-layouts: 13.4 us -> 15.3 us  [the longest x8 15.3 us: inner_stages(): stacked = jnp.concatenate(flat, axis=2)]
    all_to_all x2 -> x1, waiting for transfers between devices: 10.6 us -> 8.87 us  [reduce_stage(): lax.all_to_all(wire, DP[position], split_axis=1 + position, concat_axis=1...]
  transfers between devices with their start and end apart: 4 -> 5, of which waited for: 3 -> 3; matrix products, arithmetic and copies ran while one was open for 15% -> 14% of each run, Pallas kernels for 0% -> 0%
where the time goes in v5:
time: 217 us; the launch traced here: 215 us
  waiting for transfers between devices  59.8 us (28%)
  blocking collectives  50.5 us (23%)
  local copies, waits for them, and re-layouts  37.5 us (17%)
  starting transfers between devices  21.7 us (10%)
  matrix products  19.6 us (9%)
  between operations  14.5 us (7%)
  other arithmetic  11.7 us (5%)
    all_to_all x1, blocking collectives, shards(): lax.all_to_all(jnp.stack([narrow(gate_grad, gate_out), narrow(up_grad, up...  30.5 us
    reduce_scatter x2, waiting for transfers between devices, reduce_stage(): lax.psum_scatter(wire, DP[position], scatter_dimension=1 + position, tile...  27.4 us
    all_to_all x1, waiting for transfers between devices, shards(): lax.all_to_all(jnp.stack([gate_mid, up_mid, back_mid]), 'mp', split_axis=...  23.5 us
    all_to_all x2, blocking collectives, reduce_stage(): lax.all_to_all(wire, DP[position], split_axis=1 + position, concat_axis=1...  20.1 us
    concatenate x8, local copies, waits for them, and re-layouts, inner_stages(): stacked = jnp.concatenate(flat, axis=2)  15.3 us
    unnamed x42, local copies, waits for them, and re-layouts  12.9 us
    all_to_all x1, starting transfers between devices, shards(): lax.all_to_all(jnp.stack([gate_mid, up_mid, back_mid]), 'mp', split_axis=...  11.8 us
    all_to_all x1, waiting for transfers between devices, reduce_stage(): lax.all_to_all(wire, DP[position], split_axis=1 + position, concat_axis=1...  8.87 us
  transfers between devices with their start and end apart: 5, of which 3 were waited for; matrix products, arithmetic and copies ran while one was open for 14% of the time, Pallas kernels for 0%

profile of v5, /device:TPU:1, one launch (start us, length us, event | category | flops | bytes accessed | tf_op | source)
XLA Modules:
  0.0 215.4 jit_solution(12875016116957438921)
XLA Ops:
  7.2 1.2 copy.150
  8.4 1.3 convolution_convert_fusion
  11.8 1.4 pad_maximum_fusion.1
  13.2 11.8 %all-to-all-start = ((bf16[3,64,16,256]{3,2,0,1:T(8,128)(2,1)}), bf16[3,64,16,256]{3,2,0,1:T(8,128)(2,1)S(1)}, u32[]{:S(2)}, u32[]{:S(2)}) async-start(bf16[3,64,16,256]{3,2,0,1:T(8,128)(2,1)} %pad_maximum_fusion.1), calls=%async_computation | async-start | bytes 3145728 | tf_op jit(solution)/shard_map/all_to_all | solution.py:38
  24.9 1.9 copy.114
  26.8 23.5 %all-to-all-done = bf16[3,64,16,256]{3,2,0,1:T(8,128)(2,1)S(1)} async-done(((bf16[3,64,16,256]{3,2,0,1:T(8,128)(2,1)}), bf16[3,64,16,256]{3,2,0,1:T(8,128)(2,1)S(1)}, u32[]{:S(2)}, u32[]{:S(2)}) %all-to-all-start) | async-done | bytes 1572896 | tf_op jit(solution)/shard_map/all_to_all | solution.py:38
  50.6 1.2 copy-done.3
  54.2 3.5 %fusion.7 = (bf16[8,448,256]{2,1,0:T(8,128)(2,1)S(1)}, bf16[8,448,256]{2,1,0:T(8,128)(2,1)}, bf16[8,448,256]{2,1,0:T(8,128)(2,1)}) fusion(f32[8,256,448]{1,2,0:T(8,128)S(1)} %fusion.48, f32[8,256,448]{1,2,0:T(8,128)S(1)} %fusion.47, bf16[8,128,448]{1,2,0:T(8,128)(2,1)S(1)} %copy-done.16, bf16[8,128,256]{2,1,0:T(8,128)(2,1)S(1)} %bitcast.179), kind=kOutput, calls=%fused_computation.13 | convolution fusion | flops 248643584 | bytes 14286848 | tf_op jit(solution)/shard_map/jct,jco->jot/dot_general | solution.py:29
  57.7 1.3 copy-done.9
  60.9 4.1 %all-to-all-start.2 = ((bf16[64,16,256]{2,1,0:T(8,128)(2,1)}), bf16[64,16,256]{2,1,0:T(8,128)(2,1)}, u32[]{:S(2)}, u32[]{:S(2)}) async-start(bf16[64,16,256]{2,1,0:T(8,128)(2,1)} %copy.116), calls=%async_computation.2 | async-start | bytes 1048576 | tf_op jit(solution)/shard_map/all_to_all | solution.py:50
  65.2 2.1 fusion.46
  67.4 2.2 %concatenate.36 = f32[8,4,4,2,1792]{4,3,2,1,0:T(2,128)} reshape(f32[8,448,128]{2,1,0:T(8,128)S(1)} %fusion.46) | data formatting | bytes 3670016 | tf_op jit(solution)/shard_map/concatenate | solution.py:99
  69.6 2.4 %fusion.45 = f32[8,128,448]{2,1,0:T(8,128)S(1)} fusion(bf16[8,128,256]{2,1,0:T(8,128)(2,1)} %bitcast.180, bf16[8,448,256]{2,1,0:T(8,128)(2,1)} %get-tuple-element.37), kind=kOutput, calls=%fused_computation.66 | convolution fusion | flops 234881024 | bytes 4194304 | tf_op jit(solution)/shard_map/jct,jot->jco/dot_general | solution.py:63
  72.0 2.9 %concatenate.35 = f32[8,4,4,2,1792]{4,3,2,1,0:T(2,128)} reshape(f32[8,128,448]{2,1,0:T(8,128)S(1)} %fusion.45) | data formatting | bytes 3670016 | tf_op jit(solution)/shard_map/concatenate | solution.py:99
  74.8 2.2 %fusion.44 = f32[8,128,448]{2,1,0:T(8,128)S(1)} fusion(bf16[8,128,256]{2,1,0:T(8,128)(2,1)S(1)} %bitcast.168, bf16[8,448,256]{2,1,0:T(8,128)(2,1)} %get-tuple-element.36), kind=kOutput, calls=%fused_computation.65 | convolution fusion | flops 234881024 | bytes 4194304 | tf_op jit(solution)/shard_map/jct,jot->jco/dot_general | solution.py:60
  77.0 2.9 %concatenate.34 = f32[8,4,4,2,1792]{4,3,2,1,0:T(2,128)} reshape(f32[8,128,448]{2,1,0:T(8,128)S(1)} %fusion.44) | data formatting | bytes 3670016 | tf_op jit(solution)/shard_map/concatenate | solution.py:99
  80.0 1.2 copy.117
  81.2 1.3 fusion.30
  82.8 4.6 %pad_maximum_fusion = f32[8,4,4,2,5888]{4,3,2,1,0:T(2,128)S(1)} fusion(f32[8,4,4,2,512]{4,3,2,1,0:T(2,128)S(1)} %concatenate.37, f32[8,4,4,2,1792]{4,3,2,1,0:T(2,128)S(1)} %copy-done, f32[8,4,4,2,1792]{4,3,2,1,0:T(2,128)} %concatenate.35, f32[8,4,4,2,1792]{4,3,2,1,0:T(2,128)} %concatenate.34), kind=kLoop, calls=%fused_computation | loop fusion | flops 4521984 | bytes 12058624 | tf_op jit(solution)/shard_map/concatenate | solution.py:99
  87.4 6.1 %copy.119 = f32[8,4,4,2,5888]{4,0,2,1,3:T(8,128)} copy(f32[8,4,4,2,5888]{4,3,2,1,0:T(2,128)S(1)} %pad_maximum_fusion) | data formatting | bytes 12058624 | tf_op jit(solution)/shard_map/concatenate | solution.py:99
  93.8 2.8 %copy.107 = bf16[8,128,448]{2,0,1:T(8,128)(2,1)} copy(bf16[8,128,448]{1,2,0:T(8,128)(2,1)} %param.13) | data formatting | bytes 1835008 | tf_op args[5]
  96.6 1.9 copy.105
  98.5 2.1 fusion.18
  102.1 27.4 %reduce-scatter.3.cloned.1.call-done = f32[8,4,4,1,5888]{4,0,2,1,3:T(8,128)} async-done(((f32[8,4,4,2,5888]{4,0,2,1,3:T(8,128)}), f32[8,4,4,1,5888]{4,0,2,1,3:T(8,128)}) %reduce-scatter.3.cloned.1.call-update) | async-done | bytes 3014672 | tf_op jit(solution)/shard_map/reduce_scatter | solution.py:90
  129.4 2.0 convert_element_type.101
  131.4 1.2 copy.120
  132.8 30.5 %all_to_all.63 = bf16[2,64,16,256]{3,2,0,1:T(8,128)(2,1)S(1)} all-to-all(bf16[2,64,16,256]{3,2,0,1:T(8,128)(2,1)S(1)} %pad_maximum_fusion.2), channel_id=1, replica_groups=mesh['dz'=4,'dx'=4,'dc'=2,'mp'=8] {'mp'}, dimensions={1} | all-to-all | bytes 2097152 | tf_op jit(solution)/shard_map/all_to_all | solution.py:70
  166.0 10.5 %all_to_all.64 = f32[8,4,4,2,1024]{4,2,1,0,3:T(4,128)S(1)} all-to-all(f32[8,4,4,2,1024]{4,2,1,0,3:T(4,128)S(1)} %copy.125), channel_id=1, replica_groups=mesh['dz'=4,'dx'=4,'dc'=2,'mp'=8] {'dc'}, dimensions={3} | all-to-all | bytes 2097152 | tf_op jit(solution)/shard_map/all_to_all | solution.py:93
  177.1 9.6 %all_to_all.65 = bf16[8,4,4,1,1024]{4,1,0,3,2:T(4,128)(2,1)S(1)} all-to-all(bf16[8,4,4,1,1024]{4,1,0,3,2:T(4,128)(2,1)S(1)} %copy.126), channel_id=1, replica_groups=mesh['dz'=4,'dx'=4,'dc'=2,'mp'=8] {'dx'}, dimensions={2} | all-to-all | bytes 524288 | tf_op jit(solution)/shard_map/all_to_all | solution.py:93
  186.9 1.8 maximum_bitcast_fusion
  188.7 5.3 %all-to-all-start.5 = ((bf16[8,4,1,1,6912]{4,0,3,2,1:T(8,128)(2,1)}), bf16[8,4,1,1,6912]{4,0,3,2,1:T(8,128)(2,1)S(1)}, u32[]{:S(2)}, u32[]{:S(2)}) async-start(bf16[8,4,1,1,6912]{4,0,3,2,1:T(8,128)(2,1)} %maximum_bitcast_fusion), calls=%async_computation.7 | async-start | bytes 884736 | tf_op jit(solution)/shard_map/all_to_all | solution.py:93
  195.6 8.9 %all-to-all-done.5 = bf16[8,4,1,1,6912]{4,0,3,2,1:T(8,128)(2,1)S(1)} async-done(((bf16[8,4,1,1,6912]{4,0,3,2,1:T(8,128)(2,1)}), bf16[8,4,1,1,6912]{4,0,3,2,1:T(8,128)(2,1)S(1)}, u32[]{:S(2)}, u32[]{:S(2)}) %all-to-all-start.5) | async-done | bytes 442400 | tf_op jit(solution)/shard_map/all_to_all | solution.py:93
  (82 shorter events, 17.8 us)
Async XLA Ops:
  7.2 2.8 %copy-start.1 = (bf16[256,1024]{1,0:T(8,128)(2,1)S(1)}, bf16[256,1024]{1,0:T(8,128)(2,1)}, u32[]{:S(2)}) copy-start(bf16[256,1024]{1,0:T(8,128)(2,1)} %param.8) | copy-start | bytes 1572868
  8.4 1.8 copy-start.12
  10.0 1.0 copy-start.10
  13.2 11.8 %copy-start.2 = (bf16[8,448,128]{2,1,0:T(8,128)(2,1)S(1)}, bf16[8,448,128]{2,1,0:T(8,128)(2,1)}, u32[]{:S(2)}) copy-start(bf16[8,448,128]{2,1,0:T(8,128)(2,1)} %param.14) | copy-start | bytes 2752516
  13.2 37.2 %all-to-all-start = ((bf16[3,64,16,256]{3,2,0,1:T(8,128)(2,1)}), bf16[3,64,16,256]{3,2,0,1:T(8,128)(2,1)S(1)}, u32[]{:S(2)}, u32[]{:S(2)}) async-start(bf16[3,64,16,256]{3,2,0,1:T(8,128)(2,1)} %pad_maximum_fusion.1), calls=%async_computation | async-start | bytes 3145728 | tf_op jit(solution)/shard_map/all_to_all | solution.py:38
  50.5 1.4 copy-start.3
  50.6 3.1 %copy-start.6 = (bf16[1,8,8,16,256]{4,3,2,1,0:T(8,128)(2,1)}, bf16[1,8,8,16,256]{4,3,2,1,0:T(8,128)(2,1)S(1)}, u32[]{:S(2)}) copy-start(bf16[1,8,8,16,256]{4,3,2,1,0:T(8,128)(2,1)S(1)} %get-tuple-element.38) | copy-start | bytes 1572868
  51.9 1.2 copy-start.4
  53.1 1.2 copy-start.16
  54.2 4.8 %copy-start.14 = (bf16[8,448,128]{1,0,2:T(8,128)(2,1)S(1)}, bf16[8,448,128]{1,0,2:T(8,128)(2,1)}, u32[]{:S(2)}) copy-start(bf16[8,448,128]{1,0,2:T(8,128)(2,1)} %copy.114) | copy-start | bytes 2752516
  57.7 1.3 copy-start.9
  60.9 19.1 %all-to-all-start.2 = ((bf16[64,16,256]{2,1,0:T(8,128)(2,1)}), bf16[64,16,256]{2,1,0:T(8,128)(2,1)}, u32[]{:S(2)}, u32[]{:S(2)}) async-start(bf16[64,16,256]{2,1,0:T(8,128)(2,1)} %copy.116), calls=%async_computation.2 | async-start | bytes 1048576 | tf_op jit(solution)/shard_map/all_to_all | solution.py:50
  65.0 64.4 %reduce-scatter.3.cloned.1.call-start = ((), (), s32[]{:S(2)}) async-start(), calls=%async_computation.8 | async-start | bytes 9043968 | tf_op jit(solution)/shard_map/reduce_scatter | solution.py:90
  80.0 2.8 %copy-start = (f32[8,4,4,2,1792]{4,3,2,1,0:T(2,128)S(1)}, f32[8,4,4,2,1792]{4,3,2,1,0:T(2,128)}, u32[]{:S(2)}) copy-start(f32[8,4,4,2,1792]{4,3,2,1,0:T(2,128)} %concatenate.36) | copy-start | bytes 5505028
  93.5 3.1 %copy-start.5 = (bf16[8,128,448]{1,2,0:T(8,128)(2,1)S(1)}, bf16[8,128,448]{1,2,0:T(8,128)(2,1)}, u32[]{:S(2)}) copy-start(bf16[8,128,448]{1,2,0:T(8,128)(2,1)} %param.11) | copy-start | bytes 2752516
  93.5 5.0 %copy-start.8 = (bf16[8,448,256]{2,1,0:T(8,128)(2,1)S(1)}, bf16[8,448,256]{2,1,0:T(8,128)(2,1)}, u32[]{:S(2)}) copy-start(bf16[8,448,256]{2,1,0:T(8,128)(2,1)} %get-tuple-element.37) | copy-start | bytes 5505028
  93.5 93.3 %reduce-scatter.5.cloned.1.call-start = ((), (), s32[]{:S(2)}) async-start(), calls=%async_computation.9 | async-start | bytes 1884160 | tf_op jit(solution)/shard_map/reduce_scatter | solution.py:90
  98.5 2.5 %copy-start.7 = (bf16[8,448,256]{2,1,0:T(8,128)(2,1)S(1)}, bf16[8,448,256]{2,1,0:T(8,128)(2,1)}, u32[]{:S(2)}) copy-start(bf16[8,448,256]{2,1,0:T(8,128)(2,1)} %get-tuple-element.36) | copy-start | bytes 5505028
  98.5 2.5 %copy-start.15 = (bf16[8,128,448]{2,0,1:T(8,128)(2,1)S(1)}, bf16[8,128,448]{2,0,1:T(8,128)(2,1)}, u32[]{:S(2)}) copy-start(bf16[8,128,448]{2,0,1:T(8,128)(2,1)} %copy.105) | copy-start | bytes 2752516
  176.9 17.1 %copy-start.11 = (bf16[8,128,128]{2,1,0:T(8,128)(2,1)S(1)}, bf16[8,128,128]{2,1,0:T(8,128)(2,1)}, u32[]{:S(2)}) copy-start(bf16[8,128,128]{2,1,0:T(8,128)(2,1)} %param.10) | copy-start | bytes 786436
  186.8 7.5 %copy-start.13 = (bf16[8,128,128]{2,1,0:T(8,128)(2,1)S(1)}, bf16[8,128,128]{2,1,0:T(8,128)(2,1)}, u32[]{:S(2)}) copy-start(bf16[8,128,128]{2,1,0:T(8,128)(2,1)} %param.12) | copy-start | bytes 786436
  188.7 15.8 %all-to-all-start.5 = ((bf16[8,4,1,1,6912]{4,0,3,2,1:T(8,128)(2,1)}), bf16[8,4,1,1,6912]{4,0,3,2,1:T(8,128)(2,1)S(1)}, u32[]{:S(2)}, u32[]{:S(2)}) async-start(bf16[8,4,1,1,6912]{4,0,3,2,1:T(8,128)(2,1)} %maximum_bitcast_fusion), calls=%async_computation.7 | async-start | bytes 884736 | tf_op jit(solution)/shard_map/all_to_all | solution.py:93
Sparse Core Ops, SparseCore 0:
  93.6 35.7 reduce-scatter.2
  132.8 27.8 reduce-scatter.4

commit v6 on v4

--- a/solution.py
+++ b/solution.py
@@ -36,9 +36,10 @@
     )
     back_mid = back_mid.astype(jnp.bfloat16).reshape(NBLK, local_blocks * PAIR, rows)
     first_recv = lax.all_to_all(
-        jnp.stack([gate_mid, up_mid, back_mid]), "mp", split_axis=1, concat_axis=2, tiled=True
+        jnp.stack([gate_mid, up_mid]), "mp", split_axis=1, concat_axis=2, tiled=True
     )
-    gate_recv, up_recv, back_recv = first_recv[0], first_recv[1], first_recv[2]
+    gate_recv, up_recv = first_recv[0], first_recv[1]
+    back_recv = lax.all_to_all(back_mid, "mp", split_axis=0, concat_axis=1, tiled=True)
     gate_pre = widen(gate_recv, gate_out)
     up_pre = widen(up_recv, up_out)
     sigmoid_gate = jax.nn.sigmoid(gate_pre)
@@ -88,7 +89,7 @@
     sizes = [lax.axis_size(name) for name in DP]
     summed = stacked.reshape(stacked.shape[0], *sizes, stacked.shape[2])
     for position in reversed(range(len(DP))):
-        wire = summed if position == len(DP) - 1 else summed.astype(jnp.bfloat16)
+        wire = summed.astype(jnp.bfloat16)
         summed = lax.all_to_all(
             wire, DP[position], split_axis=1 + position, concat_axis=1 + position, tiled=True
         ).astype(jnp.float32).sum(axis=1 + position, keepdims=True)

time: 196 us -> 201 us (1.026)
  local copies, waits for them, and re-layouts: 43.9 us -> 55.1 us
  blocking collectives: 55.2 us -> 45.1 us
  matrix products: 17.9 us -> 23.3 us
  waiting for transfers between devices: 35.5 us -> 30.3 us
  starting transfers between devices: 31.6 us -> 36.5 us
    all_to_all x2, blocking collectives: 55.2 us -> 45.1 us  [shards(): lax.all_to_all(wire, DP[position], split_axis=1 + position, concat_axis=1...]
    all_to_all x1 -> x2, waiting for transfers between devices: 23.5 us -> 17.6 us  [the longest x1 10.4 us: shards(): lax.all_to_all(jnp.stack([gate_mid, up_mid]), 'mp', split_axis=1, concat_...]
    all_to_all x1 -> x2, starting transfers between devices: 11.8 us -> 16.9 us  [the longest x1 11.6 us: shards(): lax.all_to_all(back_mid, 'mp', split_axis=0, concat_axis=1, tiled=True)]
    concatenate x8, local copies, waits for them, and re-layouts: 13.4 us -> 17.7 us  [shards(): stacked = jnp.concatenate(flat, axis=2)]
    all_to_all x1, starting transfers between devices: 4.09 us -> 7.54 us  [shards(): lax.all_to_all(down_mid, 'mp', split_axis=0, concat_axis=1, tiled=True)]
    all_to_all x1, starting transfers between devices: 7.98 us -> 5.15 us  [shards(): lax.all_to_all(wire, DP[position], split_axis=1 + position, concat_axis=1...]
    another operation x3 -> x4, local copies, waits for them, and re-layouts: 0.88 us -> 3.24 us  [shards(): jnp.stack([gate_mid, up_mid, back_mid])]
    unnamed x67 -> x57, local copies, waits for them, and re-layouts: 20.2 us -> 21.6 us
  transfers between devices with their start and end apart: 4 -> 5, of which waited for: 3 -> 4; matrix products, arithmetic and copies ran while one was open for 15% -> 21% of each run, Pallas kernels for 0% -> 0%
where the time goes in v6:
time: 201 us; the launch traced here: 200 us
  local copies, waits for them, and re-layouts  55.1 us (27%)
  blocking collectives  45.1 us (22%)
  starting transfers between devices  36.5 us (18%)
  waiting for transfers between devices  30.3 us (15%)
  matrix products  23.3 us (12%)
  other arithmetic  8.49 us (4%)
    all_to_all x2, blocking collectives, shards(): lax.all_to_all(wire, DP[position], split_axis=1 + position, concat_axis=1...  45.1 us
    unnamed x57, local copies, waits for them, and re-layouts  21.6 us
    concatenate x8, local copies, waits for them, and re-layouts, shards(): stacked = jnp.concatenate(flat, axis=2)  17.7 us
    all_to_all x1, starting transfers between devices, shards(): lax.all_to_all(back_mid, 'mp', split_axis=0, concat_axis=1, tiled=True)  11.6 us
    all_to_all x1, waiting for transfers between devices, shards(): lax.all_to_all(wire, DP[position], split_axis=1 + position, concat_axis=1...  10.6 us
    all_to_all x1, waiting for transfers between devices, shards(): lax.all_to_all(jnp.stack([gate_mid, up_mid]), 'mp', split_axis=1, concat_...  10.4 us
    all_to_all x1, starting transfers between devices, shards(): lax.all_to_all(down_mid, 'mp', split_axis=0, concat_axis=1, tiled=True)  7.54 us
    all_to_all x1, waiting for transfers between devices, shards(): lax.all_to_all(back_mid, 'mp', split_axis=0, concat_axis=1, tiled=True)  7.15 us
  transfers between devices with their start and end apart: 5, of which 4 were waited for; matrix products, arithmetic and copies ran while one was open for 21% of the time, Pallas kernels for 0%

profile of v6, /device:TPU:1, one launch (start us, length us, event | category | flops | bytes accessed | tf_op | source)
XLA Modules:
  0.0 199.9 jit_solution(17103162915054520713)
XLA Ops:
  4.3 11.6 %all-to-all-start = ((bf16[64,16,256]{2,1,0:T(8,128)(2,1)}), bf16[64,16,256]{2,1,0:T(8,128)(2,1)S(1)}, u32[]{:S(2)}, u32[]{:S(2)}) async-start(bf16[64,16,256]{2,1,0:T(8,128)(2,1)} %copy.93), calls=%async_computation | async-start | bytes 1048576 | tf_op jit(solution)/shard_map/all_to_all | solution.py:42
  20.4 7.1 %all-to-all-done = bf16[64,16,256]{2,1,0:T(8,128)(2,1)S(1)} async-done(((bf16[64,16,256]{2,1,0:T(8,128)(2,1)}), bf16[64,16,256]{2,1,0:T(8,128)(2,1)S(1)}, u32[]{:S(2)}, u32[]{:S(2)}) %all-to-all-start) | async-done | bytes 524320 | tf_op jit(solution)/shard_map/all_to_all | solution.py:42
  27.5 5.3 %all-to-all-start.1 = ((bf16[2,64,16,256]{3,2,0,1:T(8,128)(2,1)}), bf16[2,64,16,256]{3,2,0,1:T(8,128)(2,1)S(1)}, u32[]{:S(2)}, u32[]{:S(2)}) async-start(bf16[2,64,16,256]{3,2,0,1:T(8,128)(2,1)} %pad_maximum_fusion), calls=%async_computation.1 | async-start | bytes 2097152 | tf_op jit(solution)/shard_map/all_to_all | solution.py:38
  32.8 1.8 copy.117
  34.7 2.4 %fusion.45 = f32[8,256,448]{1,2,0:T(8,128)} fusion(bf16[8,448,128]{2,1,0:T(8,128)(2,1)S(1)} %copy-done.6, bf16[8,128,256]{2,1,0:T(8,128)(2,1)S(1)} %bitcast.173), kind=kOutput, calls=%fused_computation.72 | convolution fusion | flops 234881024 | bytes 5111808 | tf_op jit(solution)/shard_map/joq,jqt->jot/dot_general | solution.py:56
  37.1 10.4 %all-to-all-done.1 = bf16[2,64,16,256]{3,2,0,1:T(8,128)(2,1)S(1)} async-done(((bf16[2,64,16,256]{3,2,0,1:T(8,128)(2,1)}), bf16[2,64,16,256]{3,2,0,1:T(8,128)(2,1)S(1)}, u32[]{:S(2)}, u32[]{:S(2)}) %all-to-all-start.1) | async-done | bytes 1048608 | tf_op jit(solution)/shard_map/all_to_all | solution.py:38
  50.2 3.5 %fusion.7 = (bf16[8,448,256]{2,1,0:T(8,128)(2,1)S(1)}, bf16[8,448,256]{2,1,0:T(8,128)(2,1)}, bf16[8,448,256]{2,1,0:T(8,128)(2,1)}) fusion(f32[8,256,448]{1,2,0:T(8,128)S(1)} %fusion.46, f32[8,256,448]{1,2,0:T(8,128)S(1)} %copy-done.5, bf16[8,128,448]{1,2,0:T(8,128)(2,1)S(1)} %copy-done.21, bf16[8,128,256]{2,1,0:T(8,128)(2,1)S(1)} %bitcast.189), kind=kOutput, calls=%fused_computation.12 | convolution fusion | flops 248643584 | bytes 14286848 | tf_op jit(solution)/shard_map/jct,jco->jot/dot_general | solution.py:29
  56.8 7.5 %all-to-all-start.3 = ((bf16[64,16,256]{2,1,0:T(8,128)(2,1)}), bf16[64,16,256]{2,1,0:T(8,128)(2,1)S(1)}, u32[]{:S(2)}, u32[]{:S(2)}) async-start(bf16[64,16,256]{2,1,0:T(8,128)(2,1)} %copy.119), calls=%async_computation.3 | async-start | bytes 1048576 | tf_op jit(solution)/shard_map/all_to_all | solution.py:51
  64.4 1.8 copy.104
  66.2 1.9 copy.106
  68.1 2.7 %fusion.15 = bf16[8,256,64,2]{1,2,3,0:T(8,128)(2,1)S(1)} fusion(bf16[8,448,256]{2,1,0:T(8,128)(2,1)} %get-tuple-element.36, bf16[8,64,2,448]{3,0,2,1:T(8,128)(2,1)} %bitcast.204), kind=kOutput, calls=%fused_computation.25 | convolution fusion | flops 235143168 | bytes 3276800 | tf_op jit(solution)/shard_map/jot,jkpo->kjpt/dot_general | solution.py:68
  73.3 2.1 %all-to-all-done.3 = bf16[64,16,256]{2,1,0:T(8,128)(2,1)S(1)} async-done(((bf16[64,16,256]{2,1,0:T(8,128)(2,1)}), bf16[64,16,256]{2,1,0:T(8,128)(2,1)S(1)}, u32[]{:S(2)}, u32[]{:S(2)}) %all-to-all-start.3) | async-done | bytes 524320 | tf_op jit(solution)/shard_map/all_to_all | solution.py:51
  76.2 7.0 %all-to-all-start.2 = ((bf16[2,64,16,256]{3,2,0,1:T(8,128)(2,1)}), bf16[2,64,16,256]{3,2,0,1:T(8,128)(2,1)S(1)}, u32[]{:S(2)}, u32[]{:S(2)}) async-start(bf16[2,64,16,256]{3,2,0,1:T(8,128)(2,1)} %pad_maximum_fusion.1), calls=%async_computation.2 | async-start | bytes 2097152 | tf_op jit(solution)/shard_map/all_to_all | solution.py:71
  83.2 2.1 %convolution_convert_fusion.2 = bf16[8,128,448]{1,2,0:T(8,128)(2,1)S(1)} fusion(bf16[8,128,256]{2,1,0:T(8,128)(2,1)S(1)} %bitcast.176, bf16[8,448,256]{2,1,0:T(8,128)(2,1)} %get-tuple-element.36), kind=kOutput, calls=%fused_computation.23 | convolution fusion | flops 235339776 | bytes 3276800 | tf_op jit(solution)/shard_map/jct,jot->jco/dot_general | solution.py:61
  86.7 3.6 %concatenate.18 = bf16[8,4,4,2,1792]{4,3,2,1,0:T(2,128)(2,1)} reshape(bf16[8,128,448]{2,1,0:T(8,128)(2,1)} %copy.113) | data formatting | bytes 1835008 | tf_op jit(solution)/shard_map/concatenate | solution.py:88
  90.3 2.1 %convolution_convert_fusion.1 = bf16[8,128,448]{1,2,0:T(8,128)(2,1)S(1)} fusion(bf16[8,128,256]{2,1,0:T(8,128)(2,1)S(1)} %bitcast.190, bf16[8,448,256]{2,1,0:T(8,128)(2,1)} %get-tuple-element.37), kind=kOutput, calls=%fused_computation.22 | convolution fusion | flops 235339776 | bytes 3276800 | tf_op jit(solution)/shard_map/jct,jot->jco/dot_general | solution.py:64
  93.8 3.6 %concatenate.20 = bf16[8,4,4,2,1792]{4,3,2,1,0:T(2,128)(2,1)} reshape(bf16[8,128,448]{2,1,0:T(8,128)(2,1)} %copy.116) | data formatting | bytes 1835008 | tf_op jit(solution)/shard_map/concatenate | solution.py:88
  97.4 3.2 %convolution_convert_fusion = bf16[8,448,128]{2,1,0:T(8,128)(2,1)} fusion(bf16[8,448,256]{2,1,0:T(8,128)(2,1)} %copy-done.14, bf16[8,128,256]{2,1,0:T(8,128)(2,1)S(1)} %bitcast.174), kind=kOutput, calls=%fused_computation.21 | convolution fusion | flops 235339776 | bytes 3276800 | tf_op jit(solution)/shard_map/jot,jqt->joq/dot_general | solution.py:55
  100.6 2.4 %concatenate.21 = bf16[8,4,4,2,1792]{4,3,2,1,0:T(2,128)(2,1)S(1)} reshape(bf16[8,448,128]{2,1,0:T(8,128)(2,1)} %convolution_convert_fusion) | data formatting | bytes 1835008 | tf_op jit(solution)/shard_map/concatenate | solution.py:88
  108.8 1.9 copy.115
  110.7 1.8 concatenate.19
  114.1 1.9 constant_dynamic-update-slice_fusion.3
  116.0 1.7 constant_dynamic-update-slice_fusion.2
  117.8 1.7 constant_dynamic-update-slice_fusion.1
  119.5 1.9 constant_dynamic-update-slice_fusion
  121.4 3.4 %copy.122 = bf16[8,4,4,2,6912]{4,2,1,0,3:T(4,128)(2,1)S(1)} copy(bf16[8,4,4,2,6912]{4,3,2,1,0:T(2,128)(2,1)} %constant_dynamic-update-slice_fusion) | data formatting | bytes 7077888 | tf_op jit(solution)/shard_map/concatenate | solution.py:88
  124.7 18.9 %all_to_all.81 = bf16[8,4,4,2,6912]{4,2,1,0,3:T(4,128)(2,1)S(1)} all-to-all(bf16[8,4,4,2,6912]{4,2,1,0,3:T(4,128)(2,1)S(1)} %copy.122), channel_id=1, replica_groups=mesh['dz'=4,'dx'=4,'dc'=2,'mp'=8] {'dc'}, dimensions={3} | all-to-all | bytes 7077888 | tf_op jit(solution)/shard_map/all_to_all | solution.py:93
  143.6 4.4 %reduce_sum.33 = bf16[8,4,4,6912]{3,2,1,0:T(4,128)(2,1)} reduce(bf16[8,4,4,2,6912]{4,2,1,0,3:T(4,128)(2,1)S(1)} %all_to_all.81, bf16[]{:T(256)} %constant.2.clone.1), dimensions={3}, to_apply=%region_0.0 | reduce | flops 884736 | bytes 5308418 | tf_op jit(solution)/shard_map/reduce_sum | solution.py:95
  148.0 2.2 %copy.123 = bf16[8,4,4,1,6912]{4,1,0,3,2:T(4,128)(2,1)S(1)} copy(bf16[8,4,4,1,6912]{4,2,1,0,3:T(4,128)(2,1)} %bitcast.172) | data formatting | bytes 3538944 | tf_op jit(solution)/shard_map/convert_element_type | solution.py:92
  150.2 26.2 %all_to_all.82 = bf16[8,4,4,1,6912]{4,1,0,3,2:T(4,128)(2,1)S(1)} all-to-all(bf16[8,4,4,1,6912]{4,1,0,3,2:T(4,128)(2,1)S(1)} %copy.123), channel_id=1, replica_groups=mesh['dz'=4,'dx'=4,'dc'=2,'mp'=8] {'dx'}, dimensions={2} | all-to-all | bytes 3538944 | tf_op jit(solution)/shard_map/all_to_all | solution.py:93
  178.5 5.1 %all-to-all-start.6 = ((bf16[8,4,1,1,6912]{4,0,3,2,1:T(8,128)(2,1)}), bf16[8,4,1,1,6912]{4,0,3,2,1:T(8,128)(2,1)S(1)}, u32[]{:S(2)}, u32[]{:S(2)}) async-start(bf16[8,4,1,1,6912]{4,0,3,2,1:T(8,128)(2,1)} %copy.124), calls=%async_computation.6 | async-start | bytes 884736 | tf_op jit(solution)/shard_map/all_to_all | solution.py:93
  185.2 10.6 %all-to-all-done.6 = bf16[8,4,1,1,6912]{4,0,3,2,1:T(8,128)(2,1)S(1)} async-done(((bf16[8,4,1,1,6912]{4,0,3,2,1:T(8,128)(2,1)}), bf16[8,4,1,1,6912]{4,0,3,2,1:T(8,128)(2,1)S(1)}, u32[]{:S(2)}, u32[]{:S(2)}) %all-to-all-start.6) | async-done | bytes 442400 | tf_op jit(solution)/shard_map/all_to_all | solution.py:93
  (92 shorter events, 34.8 us)
Async XLA Ops:
  0.6 15.3 %copy-start = (bf16[256,1024]{1,0:T(8,128)(2,1)S(1)}, bf16[256,1024]{1,0:T(8,128)(2,1)}, u32[]{:S(2)}) copy-start(bf16[256,1024]{1,0:T(8,128)(2,1)} %param.8) | copy-start | bytes 1572868
  0.6 15.4 %copy-start.16 = (bf16[8,128,128]{2,1,0:T(8,128)(2,1)S(1)}, bf16[8,128,128]{2,1,0:T(8,128)(2,1)}, u32[]{:S(2)}) copy-start(bf16[8,128,128]{2,1,0:T(8,128)(2,1)} %param.10) | copy-start | bytes 786436
  1.9 15.0 %copy-start.18 = (bf16[8,128,128]{2,1,0:T(8,128)(2,1)S(1)}, bf16[8,128,128]{2,1,0:T(8,128)(2,1)}, u32[]{:S(2)}) copy-start(bf16[8,128,128]{2,1,0:T(8,128)(2,1)} %param.12) | copy-start | bytes 786436
  4.3 23.3 %all-to-all-start = ((bf16[64,16,256]{2,1,0:T(8,128)(2,1)}), bf16[64,16,256]{2,1,0:T(8,128)(2,1)S(1)}, u32[]{:S(2)}, u32[]{:S(2)}) async-start(bf16[64,16,256]{2,1,0:T(8,128)(2,1)} %copy.93), calls=%async_computation | async-start | bytes 1048576 | tf_op jit(solution)/shard_map/all_to_all | solution.py:42
  16.9 16.0 %copy-start.6 = (bf16[8,448,128]{2,1,0:T(8,128)(2,1)S(1)}, bf16[8,448,128]{2,1,0:T(8,128)(2,1)}, u32[]{:S(2)}) copy-start(bf16[8,448,128]{2,1,0:T(8,128)(2,1)} %param.14) | copy-start | bytes 2752516
  27.5 20.0 %all-to-all-start.1 = ((bf16[2,64,16,256]{3,2,0,1:T(8,128)(2,1)}), bf16[2,64,16,256]{3,2,0,1:T(8,128)(2,1)S(1)}, u32[]{:S(2)}, u32[]{:S(2)}) async-start(bf16[2,64,16,256]{3,2,0,1:T(8,128)(2,1)} %pad_maximum_fusion), calls=%async_computation.1 | async-start | bytes 2097152 | tf_op jit(solution)/shard_map/all_to_all | solution.py:38
  37.1 10.7 %copy-start.7 = (bf16[8,128,448]{1,2,0:T(8,128)(2,1)S(1)}, bf16[8,128,448]{1,2,0:T(8,128)(2,1)}, u32[]{:S(2)}) copy-start(bf16[8,128,448]{1,2,0:T(8,128)(2,1)} %param.11) | copy-start | bytes 2752516
  47.7 2.2 %copy-start.5 = (f32[8,256,448]{1,2,0:T(8,128)S(1)}, f32[8,256,448]{1,2,0:T(8,128)}, u32[]{:S(2)}) copy-start(f32[8,256,448]{1,2,0:T(8,128)} %fusion.45) | copy-start | bytes 11010052
  47.7 2.5 %copy-start.21 = (bf16[8,128,448]{1,2,0:T(8,128)(2,1)S(1)}, bf16[8,128,448]{1,2,0:T(8,128)(2,1)}, u32[]{:S(2)}) copy-start(bf16[8,128,448]{1,2,0:T(8,128)(2,1)} %param.13) | copy-start | bytes 2752516
  47.8 5.9 %copy-start.11 = (bf16[1,8,8,16,256]{4,3,2,1,0:T(8,128)(2,1)}, bf16[1,8,8,16,256]{4,3,2,1,0:T(8,128)(2,1)S(1)}, u32[]{:S(2)}) copy-start(bf16[1,8,8,16,256]{4,3,2,1,0:T(8,128)(2,1)S(1)} %get-tuple-element.40) | copy-start | bytes 1572868
  50.2 4.8 %copy-start.20 = (bf16[8,448,128]{1,0,2:T(8,128)(2,1)S(1)}, bf16[8,448,128]{1,0,2:T(8,128)(2,1)}, u32[]{:S(2)}) copy-start(bf16[8,448,128]{1,0,2:T(8,128)(2,1)} %copy.117) | copy-start | bytes 2752516
  53.7 1.3 copy-start.14
  56.8 18.6 %all-to-all-start.3 = ((bf16[64,16,256]{2,1,0:T(8,128)(2,1)}), bf16[64,16,256]{2,1,0:T(8,128)(2,1)S(1)}, u32[]{:S(2)}, u32[]{:S(2)}) async-start(bf16[64,16,256]{2,1,0:T(8,128)(2,1)} %copy.119), calls=%async_computation.3 | async-start | bytes 1048576 | tf_op jit(solution)/shard_map/all_to_all | solution.py:51
  68.1 3.0 %copy-start.15 = (bf16[8,448,256]{2,1,0:T(8,128)(2,1)S(1)}, bf16[8,448,256]{2,1,0:T(8,128)(2,1)}, u32[]{:S(2)}) copy-start(bf16[8,448,256]{2,1,0:T(8,128)(2,1)} %get-tuple-element.37) | copy-start | bytes 5505028
  75.4 0.8 copy-start.13
  76.2 29.0 %all-to-all-start.2 = ((bf16[2,64,16,256]{3,2,0,1:T(8,128)(2,1)}), bf16[2,64,16,256]{3,2,0,1:T(8,128)(2,1)S(1)}, u32[]{:S(2)}, u32[]{:S(2)}) async-start(bf16[2,64,16,256]{3,2,0,1:T(8,128)(2,1)} %pad_maximum_fusion.1), calls=%async_computation.2 | async-start | bytes 2097152 | tf_op jit(solution)/shard_map/all_to_all | solution.py:71
  85.3 5.0 %copy-start.12 = (bf16[1,8,8,16,256]{4,3,2,1,0:T(8,128)(2,1)S(1)}, bf16[1,8,8,16,256]{4,3,2,1,0:T(8,128)(2,1)}, u32[]{:S(2)}) copy-start(bf16[1,8,8,16,256]{4,3,2,1,0:T(8,128)(2,1)} %copy-done.11) | copy-start | bytes 1572868
  97.4 6.7 %copy-start.10 = (bf16[256,1024]{1,0:T(8,128)(2,1)S(1)}, bf16[256,1024]{1,0:T(8,128)(2,1)}, u32[]{:S(2)}) copy-start(bf16[256,1024]{1,0:T(8,128)(2,1)} %param.9) | copy-start | bytes 1572868
  105.3 7.1 %copy-start.8 = (bf16[8,4,4,2,1792]{4,3,2,1,0:T(2,128)(2,1)S(1)}, bf16[8,4,4,2,1792]{4,3,2,1,0:T(2,128)(2,1)}, u32[]{:S(2)}) copy-start(bf16[8,4,4,2,1792]{4,3,2,1,0:T(2,128)(2,1)} %concatenate.18) | copy-start | bytes 2752516
  105.4 0.8 copy-start.1
  105.5 8.7 %copy-start.3 = (bf16[1,8,8,16,256]{4,3,2,1,0:T(8,128)(2,1)}, bf16[1,8,8,16,256]{4,3,2,1,0:T(8,128)(2,1)S(1)}, u32[]{:S(2)}) copy-start(bf16[1,8,8,16,256]{4,3,2,1,0:T(8,128)(2,1)S(1)} %get-tuple-element.38) | copy-start | bytes 1572868
  108.8 7.2 %copy-start.9 = (bf16[8,4,4,2,1792]{4,3,2,1,0:T(2,128)(2,1)S(1)}, bf16[8,4,4,2,1792]{4,3,2,1,0:T(2,128)(2,1)}, u32[]{:S(2)}) copy-start(bf16[8,4,4,2,1792]{4,3,2,1,0:T(2,128)(2,1)} %concatenate.20) | copy-start | bytes 2752516
  150.2 33.5 %copy-start.2 = (bf16[1,8,8,16,256]{4,3,2,1,0:T(8,128)(2,1)S(1)}, bf16[1,8,8,16,256]{4,3,2,1,0:T(8,128)(2,1)}, u32[]{:S(2)}) copy-start(bf16[1,8,8,16,256]{4,3,2,1,0:T(8,128)(2,1)} %copy-done.1) | copy-start | bytes 1572868
  150.2 33.5 %copy-start.17 = (bf16[8,128,128]{2,1,0:T(8,128)(2,1)S(1)}, bf16[8,128,128]{2,1,0:T(8,128)(2,1)}, u32[]{:S(2)}) copy-start(bf16[8,128,128]{2,1,0:T(8,128)(2,1)} %param.10) | copy-start | bytes 786436
  176.4 7.5 %copy-start.4 = (bf16[1,8,8,16,256]{4,3,2,1,0:T(8,128)(2,1)S(1)}, bf16[1,8,8,16,256]{4,3,2,1,0:T(8,128)(2,1)}, u32[]{:S(2)}) copy-start(bf16[1,8,8,16,256]{4,3,2,1,0:T(8,128)(2,1)} %copy-done.3) | copy-start | bytes 1572868
  177.6 6.3 %copy-start.19 = (bf16[8,128,128]{2,1,0:T(8,128)(2,1)S(1)}, bf16[8,128,128]{2,1,0:T(8,128)(2,1)}, u32[]{:S(2)}) copy-start(bf16[8,128,128]{2,1,0:T(8,128)(2,1)} %param.12) | copy-start | bytes 786436
  178.5 17.4 %all-to-all-start.6 = ((bf16[8,4,1,1,6912]{4,0,3,2,1:T(8,128)(2,1)}), bf16[8,4,1,1,6912]{4,0,3,2,1:T(8,128)(2,1)S(1)}, u32[]{:S(2)}, u32[]{:S(2)}) async-start(bf16[8,4,1,1,6912]{4,0,3,2,1:T(8,128)(2,1)} %copy.124), calls=%async_computation.6 | async-start | bytes 884736 | tf_op jit(solution)/shard_map/all_to_all | solution.py:93

commit v7 on v4

--- a/solution.py
+++ b/solution.py
@@ -82,7 +82,7 @@
     term_up_in = jnp.einsum("tki,kot->kio", x_blocks, up_back, preferred_element_type=jnp.float32)
     grad_x = input_grad.astype(jnp.bfloat16).reshape(rows, local_blocks * BLK)
     terms = (term_gate_in, term_gate_out, term_up_in, term_up_out, term_down_in, term_down_out)
-    flat = [term.reshape(term.shape[0], groups, -1) for term in terms]
+    flat = [(term * scale).reshape(term.shape[0], groups, -1) for term in terms]
     widths = [piece.shape[2] for piece in flat]
     stacked = jnp.concatenate(flat, axis=2)
     sizes = [lax.axis_size(name) for name in DP]
@@ -98,7 +98,7 @@
     for term, width in zip(terms, widths):
         piece = summed[:, 0, start:start + width]
         start += width
-        outs.append(piece.reshape(term.shape[0], term.shape[1] // groups, term.shape[2]) * scale)
+        outs.append(piece.reshape(term.shape[0], term.shape[1] // groups, term.shape[2]))
     return (grad_x, *outs)
 
 

time: 196 us -> 196 us (level)
  blocking collectives: 55.2 us -> 51.2 us
  matrix products: 17.9 us -> 20.3 us
  local copies, waits for them, and re-layouts: 43.9 us -> 46.2 us
    all_to_all x2, blocking collectives: 55.2 us -> 51.2 us  [shards(): lax.all_to_all(wire, DP[position], split_axis=1 + position, concat_axis=1...]
    another operation x0 -> x6, local copies, waits for them, and re-layouts: none -> 3.96 us  [shards(): piece.reshape(term.shape[0], term.shape[1] // groups, term.shape[2])]
    mul x5 -> x4, local copies, waits for them, and re-layouts: 3.32 us -> 4.94 us  [shards(): flat = [(term * scale).reshape(term.shape[0], groups, -1) for term in terms]]
    unnamed x67 -> x61, local copies, waits for them, and re-layouts: 20.2 us -> 19.7 us
  transfers between devices with their start and end apart: 4 -> 4, of which waited for: 3 -> 3; matrix products, arithmetic and copies ran while one was open for 15% -> 18% of each run, Pallas kernels for 0% -> 0%
where the time goes in v7:
time: 196 us; the launch traced here: 195 us
  blocking collectives  51.2 us (26%)
  local copies, waits for them, and re-layouts  46.2 us (24%)
  waiting for transfers between devices  35.4 us (18%)
  starting transfers between devices  31.4 us (16%)
  matrix products  20.3 us (10%)
  other arithmetic  9.4 us (5%)
    all_to_all x2, blocking collectives, shards(): lax.all_to_all(wire, DP[position], split_axis=1 + position, concat_axis=1...  51.2 us
    all_to_all x1, waiting for transfers between devices, shards(): lax.all_to_all(jnp.stack([gate_mid, up_mid, back_mid]), 'mp', split_axis=...  23.5 us
    unnamed x61, local copies, waits for them, and re-layouts  19.7 us
    all_to_all x1, starting transfers between devices, shards(): lax.all_to_all(jnp.stack([gate_mid, up_mid, back_mid]), 'mp', split_axis=...  11.8 us
    concatenate x8, local copies, waits for them, and re-layouts, shards(): stacked = jnp.concatenate(flat, axis=2)  11.7 us
    all_to_all x1, waiting for transfers between devices, shards(): lax.all_to_all(wire, DP[position], split_axis=1 + position, concat_axis=1...  10.6 us
    all_to_all x1, starting transfers between devices, shards(): lax.all_to_all(jnp.stack([narrow(gate_grad, gate_out), narrow(up_grad, up...  7.88 us
    all_to_all x1, starting transfers between devices, shards(): lax.all_to_all(wire, DP[position], split_axis=1 + position, concat_axis=1...  7.69 us
  transfers between devices with their start and end apart: 4, of which 3 were waited for; matrix products, arithmetic and copies ran while one was open for 18% of the time, Pallas kernels for 0%

profile of v7, /device:TPU:1, one launch (start us, length us, event | category | flops | bytes accessed | tf_op | source)
XLA Modules:
  0.0 195.1 jit_solution(17881285959891780822)
XLA Ops:
  6.3 1.3 pad_maximum_fusion
  7.7 11.8 %all-to-all-start = ((bf16[3,64,16,256]{3,2,0,1:T(8,128)(2,1)}), bf16[3,64,16,256]{3,2,0,1:T(8,128)(2,1)S(1)}, u32[]{:S(2)}, u32[]{:S(2)}) async-start(bf16[3,64,16,256]{3,2,0,1:T(8,128)(2,1)} %pad_maximum_fusion), calls=%async_computation | async-start | bytes 3145728 | tf_op jit(solution)/shard_map/all_to_all | solution.py:38
  19.4 1.8 copy.113
  21.3 23.5 %all-to-all-done = bf16[3,64,16,256]{3,2,0,1:T(8,128)(2,1)S(1)} async-done(((bf16[3,64,16,256]{3,2,0,1:T(8,128)(2,1)}), bf16[3,64,16,256]{3,2,0,1:T(8,128)(2,1)S(1)}, u32[]{:S(2)}, u32[]{:S(2)}) %all-to-all-start) | async-done | bytes 1572896 | tf_op jit(solution)/shard_map/all_to_all | solution.py:38
  45.1 1.2 copy-done.9
  48.7 3.5 %fusion.7 = (bf16[8,448,256]{2,1,0:T(8,128)(2,1)S(1)}, bf16[8,448,256]{2,1,0:T(8,128)(2,1)}, bf16[8,448,256]{2,1,0:T(8,128)(2,1)}) fusion(f32[8,256,448]{1,2,0:T(8,128)S(1)} %fusion.46, f32[8,256,448]{1,2,0:T(8,128)S(1)} %fusion.45, bf16[8,128,448]{1,2,0:T(8,128)(2,1)S(1)} %copy-done.22, bf16[8,128,256]{2,1,0:T(8,128)(2,1)S(1)} %bitcast.194), kind=kOutput, calls=%fused_computation.12 | convolution fusion | flops 248643584 | bytes 14286848 | tf_op jit(solution)/shard_map/jct,jco->jot/dot_general | solution.py:29
  52.3 1.2 copy-done.17
  54.3 1.2 copy.115
  55.4 4.1 %all-to-all-start.2 = ((bf16[64,16,256]{2,1,0:T(8,128)(2,1)}), bf16[64,16,256]{2,1,0:T(8,128)(2,1)S(1)}, u32[]{:S(2)}, u32[]{:S(2)}) async-start(bf16[64,16,256]{2,1,0:T(8,128)(2,1)} %copy.115), calls=%async_computation.2 | async-start | bytes 1048576 | tf_op jit(solution)/shard_map/all_to_all | solution.py:50
  59.5 1.9 copy.100
  61.4 2.7 %copy.102 = bf16[8,128,448]{2,0,1:T(8,128)(2,1)} copy(bf16[8,128,448]{1,2,0:T(8,128)(2,1)} %param.13) | data formatting | bytes 1835008 | tf_op args[5]
  64.1 2.7 %fusion.15 = bf16[8,256,64,2]{1,2,3,0:T(8,128)(2,1)S(1)} fusion(bf16[8,448,256]{2,1,0:T(8,128)(2,1)} %get-tuple-element.36, bf16[8,64,2,448]{3,0,2,1:T(8,128)(2,1)} %bitcast.201), kind=kOutput, calls=%fused_computation.28 | convolution fusion | flops 235143168 | bytes 3276800 | tf_op jit(solution)/shard_map/jot,jkpo->kjpt/dot_general | solution.py:67
  68.2 1.2 pad_maximum_fusion.1
  69.4 1.2 all-to-all-done.2
  71.3 7.9 %all-to-all-start.1 = ((bf16[2,64,16,256]{3,2,0,1:T(8,128)(2,1)}), bf16[2,64,16,256]{3,2,0,1:T(8,128)(2,1)}, u32[]{:S(2)}, u32[]{:S(2)}) async-start(bf16[2,64,16,256]{3,2,0,1:T(8,128)(2,1)} %pad_maximum_fusion.1), calls=%async_computation.1 | async-start | bytes 2097152 | tf_op jit(solution)/shard_map/all_to_all | solution.py:70
  79.2 2.1 %convolution_multiply_fusion = f32[8,448,128]{2,1,0:T(8,128)S(1)} fusion(bf16[8,448,256]{2,1,0:T(8,128)(2,1)} %copy-done.17, bf16[8,128,256]{2,1,0:T(8,128)(2,1)S(1)} %bitcast.184), kind=kOutput, calls=%fused_computation.24 | convolution fusion | flops 235339776 | bytes 4194304 | tf_op jit(solution)/shard_map/jot,jqt->joq/dot_general | solution.py:54
  81.4 2.2 %concatenate.20 = f32[8,4,4,2,1792]{4,3,2,1,0:T(2,128)} reshape(f32[8,448,128]{2,1,0:T(8,128)S(1)} %convolution_multiply_fusion) | data formatting | bytes 3670016 | tf_op jit(solution)/shard_map/concatenate | solution.py:87
  83.5 3.4 %convolution_multiply_fusion.2 = f32[8,128,448]{1,2,0:T(8,128)} fusion(bf16[8,128,256]{2,1,0:T(8,128)(2,1)S(1)} %bitcast.182, bf16[8,448,256]{2,1,0:T(8,128)(2,1)} %get-tuple-element.36), kind=kOutput, calls=%fused_computation.26 | convolution fusion | flops 235339776 | bytes 4194304 | tf_op jit(solution)/shard_map/jct,jot->jco/dot_general | solution.py:60
  86.9 1.9 copy.109
  88.8 2.9 %concatenate.17 = f32[8,4,4,2,1792]{4,3,2,1,0:T(2,128)} reshape(f32[8,128,448]{2,1,0:T(8,128)S(1)} %copy.109) | data formatting | bytes 3670016 | tf_op jit(solution)/shard_map/concatenate | solution.py:87
  91.7 3.4 %convolution_multiply_fusion.1 = f32[8,128,448]{1,2,0:T(8,128)} fusion(bf16[8,128,256]{2,1,0:T(8,128)(2,1)S(1)} %bitcast.195, bf16[8,448,256]{2,1,0:T(8,128)(2,1)} %get-tuple-element.37), kind=kOutput, calls=%fused_computation.25 | convolution fusion | flops 235339776 | bytes 4194304 | tf_op jit(solution)/shard_map/jct,jot->jco/dot_general | solution.py:63
  95.1 1.9 copy.112
  97.0 2.9 %concatenate.19 = f32[8,4,4,2,1792]{4,3,2,1,0:T(2,128)} reshape(f32[8,128,448]{2,1,0:T(8,128)S(1)} %copy.112) | data formatting | bytes 3670016 | tf_op jit(solution)/shard_map/concatenate | solution.py:87
  100.6 1.4 copy.171
  104.9 1.3 concatenate.18
  109.7 1.8 copy.118
  111.5 25.1 %all_to_all.63 = f32[8,4,4,2,6912]{4,2,1,0,3:T(4,128)} all-to-all(f32[8,4,4,2,6912]{4,2,1,0,3:T(4,128)S(1)} %copy.118), channel_id=1, replica_groups=mesh['dz'=4,'dx'=4,'dc'=2,'mp'=8] {'dc'}, dimensions={3} | all-to-all | bytes 14155776 | tf_op jit(solution)/shard_map/all_to_all | solution.py:92
  136.6 5.6 %reduce_sum.30 = bf16[8,4,4,6912]{3,2,1,0:T(4,128)(2,1)S(1)} reduce(f32[8,4,4,2,6912]{4,2,1,0,3:T(4,128)} %all_to_all.63, f32[]{:T(128)} %constant.2.clone.1), dimensions={3}, to_apply=%region_0.0 | reduce | flops 884736 | bytes 8847364 | tf_op jit(solution)/shard_map/reduce_sum | solution.py:94
  142.9 26.1 %all_to_all.64 = bf16[8,4,4,1,6912]{4,1,0,3,2:T(4,128)(2,1)S(1)} all-to-all(bf16[8,4,4,1,6912]{4,1,0,3,2:T(4,128)(2,1)S(1)} %copy.119), channel_id=1, replica_groups=mesh['dz'=4,'dx'=4,'dc'=2,'mp'=8] {'dx'}, dimensions={2} | all-to-all | bytes 3538944 | tf_op jit(solution)/shard_map/all_to_all | solution.py:92
  169.0 1.2 reduce_sum.31
  171.1 7.7 %all-to-all-start.5 = ((bf16[8,4,1,1,6912]{4,0,3,2,1:T(8,128)(2,1)}), bf16[8,4,1,1,6912]{4,0,3,2,1:T(8,128)(2,1)S(1)}, u32[]{:S(2)}, u32[]{:S(2)}) async-start(bf16[8,4,1,1,6912]{4,0,3,2,1:T(8,128)(2,1)} %copy.120), calls=%async_computation.5 | async-start | bytes 884736 | tf_op jit(solution)/shard_map/all_to_all | solution.py:92
  180.4 10.6 %all-to-all-done.5 = bf16[8,4,1,1,6912]{4,0,3,2,1:T(8,128)(2,1)S(1)} async-done(((bf16[8,4,1,1,6912]{4,0,3,2,1:T(8,128)(2,1)}), bf16[8,4,1,1,6912]{4,0,3,2,1:T(8,128)(2,1)S(1)}, u32[]{:S(2)}, u32[]{:S(2)}) %all-to-all-start.5) | async-done | bytes 442400 | tf_op jit(solution)/shard_map/all_to_all | solution.py:92
  (93 shorter events, 25.2 us)
Async XLA Ops:
  4.4 1.0 copy-start.11
  4.7 1.0 copy-start.23
  7.7 11.8 %copy-start.8 = (bf16[8,448,128]{2,1,0:T(8,128)(2,1)S(1)}, bf16[8,448,128]{2,1,0:T(8,128)(2,1)}, u32[]{:S(2)}) copy-start(bf16[8,448,128]{2,1,0:T(8,128)(2,1)} %param.14) | copy-start | bytes 2752516
  7.7 37.2 %all-to-all-start = ((bf16[3,64,16,256]{3,2,0,1:T(8,128)(2,1)}), bf16[3,64,16,256]{3,2,0,1:T(8,128)(2,1)S(1)}, u32[]{:S(2)}, u32[]{:S(2)}) async-start(bf16[3,64,16,256]{3,2,0,1:T(8,128)(2,1)} %pad_maximum_fusion), calls=%async_computation | async-start | bytes 3145728 | tf_op jit(solution)/shard_map/all_to_all | solution.py:38
  45.0 1.4 copy-start.9
  45.1 3.1 %copy-start.14 = (bf16[1,8,8,16,256]{4,3,2,1,0:T(8,128)(2,1)}, bf16[1,8,8,16,256]{4,3,2,1,0:T(8,128)(2,1)S(1)}, u32[]{:S(2)}) copy-start(bf16[1,8,8,16,256]{4,3,2,1,0:T(8,128)(2,1)S(1)} %get-tuple-element.38) | copy-start | bytes 1572868
  46.4 1.2 copy-start.10
  47.5 1.2 copy-start.22
  48.7 4.7 %copy-start.20 = (bf16[8,448,128]{1,0,2:T(8,128)(2,1)S(1)}, bf16[8,448,128]{1,0,2:T(8,128)(2,1)}, u32[]{:S(2)}) copy-start(bf16[8,448,128]{1,0,2:T(8,128)(2,1)} %copy.113) | copy-start | bytes 2752516
  52.3 1.2 copy-start.17
  55.4 15.1 %all-to-all-start.2 = ((bf16[64,16,256]{2,1,0:T(8,128)(2,1)}), bf16[64,16,256]{2,1,0:T(8,128)(2,1)S(1)}, u32[]{:S(2)}, u32[]{:S(2)}) async-start(bf16[64,16,256]{2,1,0:T(8,128)(2,1)} %copy.115), calls=%async_computation.2 | async-start | bytes 1048576 | tf_op jit(solution)/shard_map/all_to_all | solution.py:50
  64.1 3.0 %copy-start.16 = (bf16[8,448,256]{2,1,0:T(8,128)(2,1)S(1)}, bf16[8,448,256]{2,1,0:T(8,128)(2,1)}, u32[]{:S(2)}) copy-start(bf16[8,448,256]{2,1,0:T(8,128)(2,1)} %get-tuple-element.37) | copy-start | bytes 5505028
  64.1 3.0 %copy-start.21 = (bf16[8,128,448]{2,0,1:T(8,128)(2,1)S(1)}, bf16[8,128,448]{2,0,1:T(8,128)(2,1)}, u32[]{:S(2)}) copy-start(bf16[8,128,448]{2,0,1:T(8,128)(2,1)} %copy.102) | copy-start | bytes 2752516
  70.5 0.8 copy-start.12
  71.3 29.2 %all-to-all-start.1 = ((bf16[2,64,16,256]{3,2,0,1:T(8,128)(2,1)}), bf16[2,64,16,256]{3,2,0,1:T(8,128)(2,1)}, u32[]{:S(2)}, u32[]{:S(2)}) async-start(bf16[2,64,16,256]{3,2,0,1:T(8,128)(2,1)} %pad_maximum_fusion.1), calls=%async_computation.1 | async-start | bytes 2097152 | tf_op jit(solution)/shard_map/all_to_all | solution.py:70
  88.8 2.9 %copy-start.15 = (bf16[1,8,8,16,256]{4,3,2,1,0:T(8,128)(2,1)S(1)}, bf16[1,8,8,16,256]{4,3,2,1,0:T(8,128)(2,1)}, u32[]{:S(2)}) copy-start(bf16[1,8,8,16,256]{4,3,2,1,0:T(8,128)(2,1)} %copy-done.14) | copy-start | bytes 1572868
  97.0 2.9 %copy-start.13 = (bf16[64,16,256]{2,1,0:T(8,128)(2,1)S(1)}, bf16[64,16,256]{2,1,0:T(8,128)(2,1)}, u32[]{:S(2)}) copy-start(bf16[64,16,256]{2,1,0:T(8,128)(2,1)} %copy-done.12) | copy-start | bytes 1572868
  100.6 2.3 %copy-start.3 = (bf16[256,1024]{1,0:T(8,128)(2,1)S(1)}, bf16[256,1024]{1,0:T(8,128)(2,1)}, u32[]{:S(2)}) copy-start(bf16[256,1024]{1,0:T(8,128)(2,1)} %param.8) | copy-start | bytes 1572868
  102.1 0.8 copy-start.4
  102.1 1.6 copy-start.6
  103.9 2.4 %copy-start.1 = (f32[8,4,4,2,1792]{4,3,2,1,0:T(2,128)S(1)}, f32[8,4,4,2,1792]{4,3,2,1,0:T(2,128)}, u32[]{:S(2)}) copy-start(f32[8,4,4,2,1792]{4,3,2,1,0:T(2,128)} %concatenate.17) | copy-start | bytes 5505028
  106.3 1.5 copy-start.2
  107.8 1.5 copy-start
  169.0 9.8 %copy-start.5 = (bf16[1,8,8,16,256]{4,3,2,1,0:T(8,128)(2,1)S(1)}, bf16[1,8,8,16,256]{4,3,2,1,0:T(8,128)(2,1)}, u32[]{:S(2)}) copy-start(bf16[1,8,8,16,256]{4,3,2,1,0:T(8,128)(2,1)} %copy-done.4) | copy-start | bytes 1572868
  169.0 9.8 %copy-start.18 = (bf16[8,128,128]{2,1,0:T(8,128)(2,1)S(1)}, bf16[8,128,128]{2,1,0:T(8,128)(2,1)}, u32[]{:S(2)}) copy-start(bf16[8,128,128]{2,1,0:T(8,128)(2,1)} %param.10) | copy-start | bytes 786436
  170.2 8.8 %copy-start.7 = (bf16[1,8,8,16,256]{4,3,2,1,0:T(8,128)(2,1)S(1)}, bf16[1,8,8,16,256]{4,3,2,1,0:T(8,128)(2,1)}, u32[]{:S(2)}) copy-start(bf16[1,8,8,16,256]{4,3,2,1,0:T(8,128)(2,1)} %copy-done.6) | copy-start | bytes 1572868
  170.3 8.8 %copy-start.19 = (bf16[8,128,128]{2,1,0:T(8,128)(2,1)S(1)}, bf16[8,128,128]{2,1,0:T(8,128)(2,1)}, u32[]{:S(2)}) copy-start(bf16[8,128,128]{2,1,0:T(8,128)(2,1)} %param.12) | copy-start | bytes 786436
  171.1 19.9 %all-to-all-start.5 = ((bf16[8,4,1,1,6912]{4,0,3,2,1:T(8,128)(2,1)}), bf16[8,4,1,1,6912]{4,0,3,2,1:T(8,128)(2,1)S(1)}, u32[]{:S(2)}, u32[]{:S(2)}) async-start(bf16[8,4,1,1,6912]{4,0,3,2,1:T(8,128)(2,1)} %copy.120), calls=%async_computation.5 | async-start | bytes 884736 | tf_op jit(solution)/shard_map/all_to_all | solution.py:92

commit v8 on v4

--- a/solution.py
+++ b/solution.py
@@ -10,6 +10,26 @@
 PAIR = 2
 FBLK = 448
 DP = ("dz", "dx", "dc")
+
+
+def ring_scatter(summed, name, dim):
+    count = lax.axis_size(name)
+    me = lax.axis_index(name)
+    half = summed.shape[-1] // 2
+    ahead, behind = summed[..., :half], summed[..., half:]
+    clockwise = [(j, (j + 1) % count) for j in range(count)]
+    counter = [(j, (j - 1) % count) for j in range(count)]
+
+    def take(values, shift):
+        return lax.dynamic_index_in_dim(values, (me + 2 * count + shift) % count, axis=dim)
+
+    carry_a, carry_b = take(ahead, -1), take(behind, 1)
+    for step in range(count - 1):
+        got_a = lax.ppermute(carry_a.astype(jnp.bfloat16), name, clockwise).astype(jnp.float32)
+        got_b = lax.ppermute(carry_b.astype(jnp.bfloat16), name, counter).astype(jnp.float32)
+        carry_a = got_a + take(ahead, -step - 2)
+        carry_b = got_b + take(behind, step + 2)
+    return jnp.concatenate([carry_a, carry_b], axis=-1)
 
 
 def shards(tokens_in, grad_out, gate_in, gate_out, up_in, up_out, down_in, down_out):
@@ -88,6 +108,9 @@
     sizes = [lax.axis_size(name) for name in DP]
     summed = stacked.reshape(stacked.shape[0], *sizes, stacked.shape[2])
     for position in reversed(range(len(DP))):
+        if position == 1:
+            summed = ring_scatter(summed, DP[position], 1 + position)
+            continue
         wire = summed if position == len(DP) - 1 else summed.astype(jnp.bfloat16)
         summed = lax.all_to_all(
             wire, DP[position], split_axis=1 + position, concat_axis=1 + position, tiled=True

time: 196 us -> 208 us (1.061); the launches traced: 195 us -> 205 us
  blocking collectives: 55.2 us -> 28.5 us
  waiting for transfers between devices: 35.5 us -> 60.3 us
  starting transfers between devices: 31.6 us -> 42.2 us
  other arithmetic: 9.93 us -> 13.3 us
  local copies, waits for them, and re-layouts: 43.9 us -> 41.6 us
    all_to_all x2 -> x1, blocking collectives: 55.2 us -> 28.5 us  [shards(): lax.all_to_all(wire, DP[position], split_axis=1 + position, concat_axis=1...]
    ppermute x0 -> x6, waiting for transfers between devices: none -> 26.5 us  [the longest x3 23 us: ring_scatter(): lax.ppermute(carry_b.astype(jnp.bfloat16), name, counter)]
    ppermute x0 -> x6, starting transfers between devices: none -> 10 us  [the longest x3 9.51 us: ring_scatter(): lax.ppermute(carry_b.astype(jnp.bfloat16), name, counter)]
    all_to_all x1, waiting for transfers between devices: 10.6 us -> 8.15 us  [shards(): lax.all_to_all(wire, DP[position], split_axis=1 + position, concat_axis=1...]
    convert_element_type x0 -> x4, other arithmetic: none -> 2.45 us  [the longest x2 1.22 us: ring_scatter(): carry_b.astype(jnp.bfloat16)]
    reduce_sum x3 -> x2, other arithmetic: 6.85 us -> 5.61 us  [shards(): summed = lax.all_to_all(wire, DP[position], split_axis=1 + position, conc...]
    unnamed x67 -> x63, local copies, waits for them, and re-layouts: 20.2 us -> 19 us
  transfers between devices with their start and end apart: 4 -> 10, of which waited for: 3 -> 8; matrix products, arithmetic and copies ran while one was open for 15% -> 15% of each run, Pallas kernels for 0% -> 0%
where the time goes in v8:
time: 208 us; the launch traced here: 205 us
  waiting for transfers between devices  60.3 us (29%)
  starting transfers between devices  42.2 us (20%)
  local copies, waits for them, and re-layouts  41.6 us (20%)
  blocking collectives  28.5 us (14%)
  matrix products  17.9 us (9%)
  other arithmetic  13.3 us (6%)
    all_to_all x1, blocking collectives, shards(): lax.all_to_all(wire, DP[position], split_axis=1 + position, concat_axis=1...  28.5 us
    all_to_all x1, waiting for transfers between devices, shards(): lax.all_to_all(jnp.stack([gate_mid, up_mid, back_mid]), 'mp', split_axis=...  23.5 us
    ppermute x3, waiting for transfers between devices, ring_scatter(): lax.ppermute(carry_b.astype(jnp.bfloat16), name, counter)  23 us
    unnamed x63, local copies, waits for them, and re-layouts  19 us
    all_to_all x1, starting transfers between devices, shards(): lax.all_to_all(jnp.stack([gate_mid, up_mid, back_mid]), 'mp', split_axis=...  11.8 us
    concatenate x8, local copies, waits for them, and re-layouts, shards(): stacked = jnp.concatenate(flat, axis=2)  11.8 us
    ppermute x3, starting transfers between devices, ring_scatter(): lax.ppermute(carry_b.astype(jnp.bfloat16), name, counter)  9.51 us
    all_to_all x1, starting transfers between devices, shards(): lax.all_to_all(wire, DP[position], split_axis=1 + position, concat_axis=1...  8.53 us
  transfers between devices with their start and end apart: 10, of which 8 were waited for; matrix products, arithmetic and copies ran while one was open for 15% of the time, Pallas kernels for 0%

profile of v8, /device:TPU:1, one launch (start us, length us, event | category | flops | bytes accessed | tf_op | source)
XLA Modules:
  0.0 205.0 jit_solution(17813449140059260761)
XLA Ops:
  6.3 1.4 pad_maximum_fusion
  7.7 11.8 %all-to-all-start = ((bf16[3,64,16,256]{3,2,0,1:T(8,128)(2,1)}), bf16[3,64,16,256]{3,2,0,1:T(8,128)(2,1)S(1)}, u32[]{:S(2)}, u32[]{:S(2)}) async-start(bf16[3,64,16,256]{3,2,0,1:T(8,128)(2,1)} %pad_maximum_fusion), calls=%async_computation | async-start | bytes 3145728 | tf_op jit(solution)/shard_map/all_to_all | solution.py:58
  19.5 1.9 copy.113
  21.3 23.5 %all-to-all-done = bf16[3,64,16,256]{3,2,0,1:T(8,128)(2,1)S(1)} async-done(((bf16[3,64,16,256]{3,2,0,1:T(8,128)(2,1)}), bf16[3,64,16,256]{3,2,0,1:T(8,128)(2,1)S(1)}, u32[]{:S(2)}, u32[]{:S(2)}) %all-to-all-start) | async-done | bytes 1572896 | tf_op jit(solution)/shard_map/all_to_all | solution.py:58
  48.7 3.5 %fusion.7 = (bf16[8,448,256]{2,1,0:T(8,128)(2,1)S(1)}, bf16[8,448,256]{2,1,0:T(8,128)(2,1)}, bf16[8,448,256]{2,1,0:T(8,128)(2,1)}) fusion(f32[8,256,448]{1,2,0:T(8,128)S(1)} %fusion.49, f32[8,256,448]{1,2,0:T(8,128)S(1)} %fusion.48, bf16[8,128,448]{1,2,0:T(8,128)(2,1)S(1)} %copy-done.23, bf16[8,128,256]{2,1,0:T(8,128)(2,1)S(1)} %bitcast.185), kind=kOutput, calls=%fused_computation.12 | convolution fusion | flops 248643584 | bytes 14286848 | tf_op jit(solution)/shard_map/jct,jco->jot/dot_general | solution.py:49
  52.3 1.3 copy-done.18
  55.5 4.1 %all-to-all-start.2 = ((bf16[64,16,256]{2,1,0:T(8,128)(2,1)}), bf16[64,16,256]{2,1,0:T(8,128)(2,1)S(1)}, u32[]{:S(2)}, u32[]{:S(2)}) async-start(bf16[64,16,256]{2,1,0:T(8,128)(2,1)} %copy.115), calls=%async_computation.2 | async-start | bytes 1048576 | tf_op jit(solution)/shard_map/all_to_all | solution.py:70
  59.6 1.9 copy.100
  61.4 2.7 %copy.102 = bf16[8,128,448]{2,0,1:T(8,128)(2,1)} copy(bf16[8,128,448]{1,2,0:T(8,128)(2,1)} %param.13) | data formatting | bytes 1835008 | tf_op args[5]
  64.1 2.7 %fusion.15 = bf16[8,256,64,2]{1,2,3,0:T(8,128)(2,1)S(1)} fusion(bf16[8,448,256]{2,1,0:T(8,128)(2,1)} %get-tuple-element.36, bf16[8,64,2,448]{3,0,2,1:T(8,128)(2,1)} %bitcast.197), kind=kOutput, calls=%fused_computation.24 | convolution fusion | flops 235143168 | bytes 3276800 | tf_op jit(solution)/shard_map/jot,jkpo->kjpt/dot_general | solution.py:87
  69.3 1.3 all-to-all-done.2
  70.6 7.8 %all-to-all-start.1 = ((bf16[2,64,16,256]{3,2,0,1:T(8,128)(2,1)}), bf16[2,64,16,256]{3,2,0,1:T(8,128)(2,1)}, u32[]{:S(2)}, u32[]{:S(2)}) async-start(bf16[2,64,16,256]{3,2,0,1:T(8,128)(2,1)} %pad_maximum_fusion.1), calls=%async_computation.1 | async-start | bytes 2097152 | tf_op jit(solution)/shard_map/all_to_all | solution.py:90
  78.4 2.1 %fusion.47 = f32[8,448,128]{2,1,0:T(8,128)S(1)} fusion(bf16[8,448,256]{2,1,0:T(8,128)(2,1)} %copy-done.18, bf16[8,128,256]{2,1,0:T(8,128)(2,1)S(1)} %bitcast.181), kind=kOutput, calls=%fused_computation.79 | convolution fusion | flops 234881024 | bytes 4194304 | tf_op jit(solution)/shard_map/jot,jqt->joq/dot_general | solution.py:74
  80.5 2.2 %concatenate.32 = f32[8,4,4,2,1792]{4,3,2,1,0:T(2,128)} reshape(f32[8,448,128]{2,1,0:T(8,128)S(1)} %fusion.47) | data formatting | bytes 3670016 | tf_op jit(solution)/shard_map/concatenate | solution.py:107
  82.7 2.2 %fusion.45 = f32[8,128,448]{2,1,0:T(8,128)S(1)} fusion(bf16[8,128,256]{2,1,0:T(8,128)(2,1)S(1)} %bitcast.173, bf16[8,448,256]{2,1,0:T(8,128)(2,1)} %get-tuple-element.36), kind=kOutput, calls=%fused_computation.77 | convolution fusion | flops 234881024 | bytes 4194304 | tf_op jit(solution)/shard_map/jct,jot->jco/dot_general | solution.py:80
  84.9 2.9 %concatenate.29 = f32[8,4,4,2,1792]{4,3,2,1,0:T(2,128)} reshape(f32[8,128,448]{2,1,0:T(8,128)S(1)} %fusion.45) | data formatting | bytes 3670016 | tf_op jit(solution)/shard_map/concatenate | solution.py:107
  87.8 2.2 %fusion.46 = f32[8,128,448]{2,1,0:T(8,128)S(1)} fusion(bf16[8,128,256]{2,1,0:T(8,128)(2,1)S(1)} %bitcast.186, bf16[8,448,256]{2,1,0:T(8,128)(2,1)} %get-tuple-element.37), kind=kOutput, calls=%fused_computation.78 | convolution fusion | flops 234881024 | bytes 4194304 | tf_op jit(solution)/shard_map/jct,jot->jco/dot_general | solution.py:83
  90.0 2.9 %concatenate.31 = f32[8,4,4,2,1792]{4,3,2,1,0:T(2,128)} reshape(f32[8,128,448]{2,1,0:T(8,128)S(1)} %fusion.46) | data formatting | bytes 3670016 | tf_op jit(solution)/shard_map/concatenate | solution.py:107
  94.4 1.4 copy.172
  98.8 1.3 concatenate.30
  103.6 1.8 copy.118
  105.4 28.5 %all_to_all.58 = f32[8,4,4,2,6912]{4,2,1,0,3:T(4,128)} all-to-all(f32[8,4,4,2,6912]{4,2,1,0,3:T(4,128)S(1)} %copy.118), channel_id=1, replica_groups=mesh['dz'=4,'dx'=4,'dc'=2,'mp'=8] {'dc'}, dimensions={3} | all-to-all | bytes 14155776 | tf_op jit(solution)/shard_map/all_to_all | solution.py:115
  134.0 5.6 %reduce_sum.18 = f32[8,4,4,6912]{3,2,1,0:T(4,128)S(1)} reduce(f32[8,4,4,2,6912]{4,2,1,0,3:T(4,128)} %all_to_all.58, f32[]{:T(128)} %constant.82.clone.1), dimensions={3}, to_apply=%region_0.0 | reduce | flops 884736 | bytes 10616836 | tf_op jit(solution)/shard_map/reduce_sum | solution.py:117
  140.2 2.5 %collective-permute-start.3 = (bf16[8,4,1,1,3456]{4,2,1,0,3:T(2,128)(2,1)S(1)}, bf16[8,4,1,1,3456]{4,2,1,0,3:T(2,128)(2,1)S(1)}, u32[]{:S(2)}, u32[]{:S(2)}) collective-permute-start(bf16[8,4,1,1,3456]{4,2,1,0,3:T(2,128)(2,1)S(1)} %dynamic-slice_convert_fusion), channel_id=1, source_target_pairs={{0,48},{16,0},{32,16},{48,32},{1,49},{17,1},{33,17},{49,33},{2,50}... | collective-permute-start | bytes 663560 | tf_op jit(solution)/shard_map/ppermute | solution.py:29
  143.2 8.8 %collective-permute-done.3 = bf16[8,4,1,1,3456]{4,2,1,0,3:T(2,128)(2,1)S(1)} collective-permute-done((bf16[8,4,1,1,3456]{4,2,1,0,3:T(2,128)(2,1)S(1)}, bf16[8,4,1,1,3456]{4,2,1,0,3:T(2,128)(2,1)S(1)}, u32[]{:S(2)}, u32[]{:S(2)}) %collective-permute-start.3) | collective-permute-done | bytes 221216 | tf_op jit(solution)/shard_map/ppermute | solution.py:29
  152.6 3.5 %collective-permute-start.4 = (bf16[8,4,1,1,3456]{4,2,1,0,3:T(2,128)(2,1)S(1)}, bf16[8,4,1,1,3456]{4,2,1,0,3:T(2,128)(2,1)S(1)}, u32[]{:S(2)}, u32[]{:S(2)}) collective-permute-start(bf16[8,4,1,1,3456]{4,2,1,0,3:T(2,128)(2,1)S(1)} %add_convert_fusion.2), channel_id=1, source_target_pairs={{0,48},{16,0},{32,16},{48,32},{1,49},{17,1},{33,17},{49,33},{2,50}... | collective-permute-start | bytes 663560 | tf_op jit(solution)/shard_map/ppermute | solution.py:29
  156.8 7.7 %collective-permute-done.4 = bf16[8,4,1,1,3456]{4,2,1,0,3:T(2,128)(2,1)S(1)} collective-permute-done((bf16[8,4,1,1,3456]{4,2,1,0,3:T(2,128)(2,1)S(1)}, bf16[8,4,1,1,3456]{4,2,1,0,3:T(2,128)(2,1)S(1)}, u32[]{:S(2)}, u32[]{:S(2)}) %collective-permute-start.4) | collective-permute-done | bytes 221216 | tf_op jit(solution)/shard_map/ppermute | solution.py:29
  165.1 3.5 %collective-permute-start.5 = (bf16[8,4,1,1,3456]{4,2,1,0,3:T(2,128)(2,1)S(1)}, bf16[8,4,1,1,3456]{4,2,1,0,3:T(2,128)(2,1)S(1)}, u32[]{:S(2)}, u32[]{:S(2)}) collective-permute-start(bf16[8,4,1,1,3456]{4,2,1,0,3:T(2,128)(2,1)S(1)} %add_convert_fusion.1), channel_id=1, source_target_pairs={{0,48},{16,0},{32,16},{48,32},{1,49},{17,1},{33,17},{49,33},{2,50}... | collective-permute-start | bytes 663560 | tf_op jit(solution)/shard_map/ppermute | solution.py:29
  169.6 6.6 %collective-permute-done.5 = bf16[8,4,1,1,3456]{4,2,1,0,3:T(2,128)(2,1)S(1)} collective-permute-done((bf16[8,4,1,1,3456]{4,2,1,0,3:T(2,128)(2,1)S(1)}, bf16[8,4,1,1,3456]{4,2,1,0,3:T(2,128)(2,1)S(1)}, u32[]{:S(2)}, u32[]{:S(2)}) %collective-permute-start.5) | collective-permute-done | bytes 221216 | tf_op jit(solution)/shard_map/ppermute | solution.py:29
  176.8 3.5 %collective-permute-done.2 = bf16[8,4,1,1,3456]{4,2,1,0,3:T(2,128)(2,1)S(1)} collective-permute-done((bf16[8,4,1,1,3456]{4,2,1,0,3:T(2,128)(2,1)S(1)}, bf16[8,4,1,1,3456]{4,2,1,0,3:T(2,128)(2,1)S(1)}, u32[]{:S(2)}, u32[]{:S(2)}) %collective-permute-start.2) | collective-permute-done | bytes 221216 | tf_op jit(solution)/shard_map/ppermute | solution.py:28
  182.7 8.5 %all-to-all-start.4 = ((bf16[8,4,1,1,6912]{4,0,3,2,1:T(8,128)(2,1)}), bf16[8,4,1,1,6912]{4,0,3,2,1:T(8,128)(2,1)S(1)}, u32[]{:S(2)}, u32[]{:S(2)}) async-start(bf16[8,4,1,1,6912]{4,0,3,2,1:T(8,128)(2,1)} %copy.119), calls=%async_computation.4 | async-start | bytes 884736 | tf_op jit(solution)/shard_map/all_to_all | solution.py:115
  192.9 8.2 %all-to-all-done.4 = bf16[8,4,1,1,6912]{4,0,3,2,1:T(8,128)(2,1)S(1)} async-done(((bf16[8,4,1,1,6912]{4,0,3,2,1:T(8,128)(2,1)}), bf16[8,4,1,1,6912]{4,0,3,2,1:T(8,128)(2,1)S(1)}, u32[]{:S(2)}, u32[]{:S(2)}) %all-to-all-start.4) | async-done | bytes 442400 | tf_op jit(solution)/shard_map/all_to_all | solution.py:115
  (112 shorter events, 34.3 us)
Async XLA Ops:
  7.7 11.8 %copy-start.8 = (bf16[8,448,128]{2,1,0:T(8,128)(2,1)S(1)}, bf16[8,448,128]{2,1,0:T(8,128)(2,1)}, u32[]{:S(2)}) copy-start(bf16[8,448,128]{2,1,0:T(8,128)(2,1)} %param.14) | copy-start | bytes 2752516
  7.7 37.2 %all-to-all-start = ((bf16[3,64,16,256]{3,2,0,1:T(8,128)(2,1)}), bf16[3,64,16,256]{3,2,0,1:T(8,128)(2,1)S(1)}, u32[]{:S(2)}, u32[]{:S(2)}) async-start(bf16[3,64,16,256]{3,2,0,1:T(8,128)(2,1)} %pad_maximum_fusion), calls=%async_computation | async-start | bytes 3145728 | tf_op jit(solution)/shard_map/all_to_all | solution.py:58
  45.0 1.4 copy-start.9
  45.1 3.1 %copy-start.13 = (bf16[1,8,8,16,256]{4,3,2,1,0:T(8,128)(2,1)}, bf16[1,8,8,16,256]{4,3,2,1,0:T(8,128)(2,1)S(1)}, u32[]{:S(2)}) copy-start(bf16[1,8,8,16,256]{4,3,2,1,0:T(8,128)(2,1)S(1)} %get-tuple-element.40) | copy-start | bytes 1572868
  46.4 1.2 copy-start.10
  47.6 1.2 copy-start.23
  48.7 4.8 %copy-start.21 = (bf16[8,448,128]{1,0,2:T(8,128)(2,1)S(1)}, bf16[8,448,128]{1,0,2:T(8,128)(2,1)}, u32[]{:S(2)}) copy-start(bf16[8,448,128]{1,0,2:T(8,128)(2,1)} %copy.113) | copy-start | bytes 2752516
  52.3 1.3 copy-start.18
  55.5 15.1 %all-to-all-start.2 = ((bf16[64,16,256]{2,1,0:T(8,128)(2,1)}), bf16[64,16,256]{2,1,0:T(8,128)(2,1)S(1)}, u32[]{:S(2)}, u32[]{:S(2)}) async-start(bf16[64,16,256]{2,1,0:T(8,128)(2,1)} %copy.115), calls=%async_computation.2 | async-start | bytes 1048576 | tf_op jit(solution)/shard_map/all_to_all | solution.py:70
  64.1 3.0 %copy-start.17 = (bf16[8,448,256]{2,1,0:T(8,128)(2,1)S(1)}, bf16[8,448,256]{2,1,0:T(8,128)(2,1)}, u32[]{:S(2)}) copy-start(bf16[8,448,256]{2,1,0:T(8,128)(2,1)} %get-tuple-element.37) | copy-start | bytes 5505028
  64.1 3.0 %copy-start.22 = (bf16[8,128,448]{2,0,1:T(8,128)(2,1)S(1)}, bf16[8,128,448]{2,0,1:T(8,128)(2,1)}, u32[]{:S(2)}) copy-start(bf16[8,128,448]{2,0,1:T(8,128)(2,1)} %copy.102) | copy-start | bytes 2752516
  70.6 7.8 %copy-start.15 = (bf16[64,16,256]{2,1,0:T(8,128)(2,1)}, bf16[64,16,256]{2,1,0:T(8,128)(2,1)S(1)}, u32[]{:S(2)}) copy-start(bf16[64,16,256]{2,1,0:T(8,128)(2,1)S(1)} %all-to-all-done.2) | copy-start | bytes 1572868
  70.6 23.8 %all-to-all-start.1 = ((bf16[2,64,16,256]{3,2,0,1:T(8,128)(2,1)}), bf16[2,64,16,256]{3,2,0,1:T(8,128)(2,1)}, u32[]{:S(2)}, u32[]{:S(2)}) async-start(bf16[2,64,16,256]{3,2,0,1:T(8,128)(2,1)} %pad_maximum_fusion.1), calls=%async_computation.1 | async-start | bytes 2097152 | tf_op jit(solution)/shard_map/all_to_all | solution.py:90
  84.9 2.9 %copy-start.14 = (bf16[1,8,8,16,256]{4,3,2,1,0:T(8,128)(2,1)S(1)}, bf16[1,8,8,16,256]{4,3,2,1,0:T(8,128)(2,1)}, u32[]{:S(2)}) copy-start(bf16[1,8,8,16,256]{4,3,2,1,0:T(8,128)(2,1)} %copy-done.13) | copy-start | bytes 1572868
  90.0 2.9 %copy-start.16 = (bf16[64,16,256]{2,1,0:T(8,128)(2,1)S(1)}, bf16[64,16,256]{2,1,0:T(8,128)(2,1)}, u32[]{:S(2)}) copy-start(bf16[64,16,256]{2,1,0:T(8,128)(2,1)} %copy-done.15) | copy-start | bytes 1572868
  90.0 3.0 %copy-start.12 = (bf16[256,1024]{1,0:T(8,128)(2,1)S(1)}, bf16[256,1024]{1,0:T(8,128)(2,1)}, u32[]{:S(2)}) copy-start(bf16[256,1024]{1,0:T(8,128)(2,1)} %param.9) | copy-start | bytes 1572868
  94.4 2.3 %copy-start.3 = (bf16[256,1024]{1,0:T(8,128)(2,1)S(1)}, bf16[256,1024]{1,0:T(8,128)(2,1)}, u32[]{:S(2)}) copy-start(bf16[256,1024]{1,0:T(8,128)(2,1)} %param.8) | copy-start | bytes 1572868
  95.9 1.6 copy-start.6
  97.8 2.4 %copy-start.2 = (f32[8,4,4,2,1792]{4,3,2,1,0:T(2,128)S(1)}, f32[8,4,4,2,1792]{4,3,2,1,0:T(2,128)}, u32[]{:S(2)}) copy-start(f32[8,4,4,2,1792]{4,3,2,1,0:T(2,128)} %concatenate.29) | copy-start | bytes 5505028
  100.2 1.5 copy-start.1
  101.7 1.5 copy-start
  140.2 11.8 %collective-permute-start.3 = (bf16[8,4,1,1,3456]{4,2,1,0,3:T(2,128)(2,1)S(1)}, bf16[8,4,1,1,3456]{4,2,1,0,3:T(2,128)(2,1)S(1)}, u32[]{:S(2)}, u32[]{:S(2)}) collective-permute-start(bf16[8,4,1,1,3456]{4,2,1,0,3:T(2,128)(2,1)S(1)} %dynamic-slice_convert_fusion), channel_id=1, source_target_pairs={{0,48},{16,0},{32,16},{48,32},{1,49},{17,1},{33,17},{49,33},{2,50}... | collective-permute-start | bytes 663560 | tf_op jit(solution)/shard_map/ppermute | solution.py:29
  143.1 13.0 %collective-permute-start = (bf16[8,4,1,1,3456]{4,2,1,0,3:T(2,128)(2,1)S(1)}, bf16[8,4,1,1,3456]{4,2,1,0,3:T(2,128)(2,1)S(1)}, u32[]{:S(2)}, u32[]{:S(2)}) collective-permute-start(bf16[8,4,1,1,3456]{4,2,1,0,3:T(2,128)(2,1)S(1)} %dynamic-slice_convert_fusion.1), channel_id=1, source_target_pairs={{0,16},{16,32},{32,48},{48,0},{1,17},{17,33},{33,49},{49,1},{2,18}... | collective-permute-start | bytes 663560 | tf_op jit(solution)/shard_map/ppermute | solution.py:28
  152.6 11.9 %collective-permute-start.4 = (bf16[8,4,1,1,3456]{4,2,1,0,3:T(2,128)(2,1)S(1)}, bf16[8,4,1,1,3456]{4,2,1,0,3:T(2,128)(2,1)S(1)}, u32[]{:S(2)}, u32[]{:S(2)}) collective-permute-start(bf16[8,4,1,1,3456]{4,2,1,0,3:T(2,128)(2,1)S(1)} %add_convert_fusion.2), channel_id=1, source_target_pairs={{0,48},{16,0},{32,16},{48,32},{1,49},{17,1},{33,17},{49,33},{2,50}... | collective-permute-start | bytes 663560 | tf_op jit(solution)/shard_map/ppermute | solution.py:29
  156.7 11.9 %collective-permute-start.1 = (bf16[8,4,1,1,3456]{4,2,1,0,3:T(2,128)(2,1)S(1)}, bf16[8,4,1,1,3456]{4,2,1,0,3:T(2,128)(2,1)S(1)}, u32[]{:S(2)}, u32[]{:S(2)}) collective-permute-start(bf16[8,4,1,1,3456]{4,2,1,0,3:T(2,128)(2,1)S(1)} %add_convert_fusion.5), channel_id=1, source_target_pairs={{0,16},{16,32},{32,48},{48,0},{1,17},{17,33},{33,49},{49,1},{2,18}... | collective-permute-start | bytes 663560 | tf_op jit(solution)/shard_map/ppermute | solution.py:28
  165.1 11.0 %collective-permute-start.5 = (bf16[8,4,1,1,3456]{4,2,1,0,3:T(2,128)(2,1)S(1)}, bf16[8,4,1,1,3456]{4,2,1,0,3:T(2,128)(2,1)S(1)}, u32[]{:S(2)}, u32[]{:S(2)}) collective-permute-start(bf16[8,4,1,1,3456]{4,2,1,0,3:T(2,128)(2,1)S(1)} %add_convert_fusion.1), channel_id=1, source_target_pairs={{0,48},{16,0},{32,16},{48,32},{1,49},{17,1},{33,17},{49,33},{2,50}... | collective-permute-start | bytes 663560 | tf_op jit(solution)/shard_map/ppermute | solution.py:29
  169.2 11.0 %collective-permute-start.2 = (bf16[8,4,1,1,3456]{4,2,1,0,3:T(2,128)(2,1)S(1)}, bf16[8,4,1,1,3456]{4,2,1,0,3:T(2,128)(2,1)S(1)}, u32[]{:S(2)}, u32[]{:S(2)}) collective-permute-start(bf16[8,4,1,1,3456]{4,2,1,0,3:T(2,128)(2,1)S(1)} %add_convert_fusion.4), channel_id=1, source_target_pairs={{0,16},{16,32},{32,48},{48,0},{1,17},{17,33},{33,49},{49,1},{2,18}... | collective-permute-start | bytes 663560 | tf_op jit(solution)/shard_map/ppermute | solution.py:28
  180.8 10.4 %copy-start.5 = (bf16[1,8,8,16,256]{4,3,2,1,0:T(8,128)(2,1)S(1)}, bf16[1,8,8,16,256]{4,3,2,1,0:T(8,128)(2,1)}, u32[]{:S(2)}) copy-start(bf16[1,8,8,16,256]{4,3,2,1,0:T(8,128)(2,1)} %copy-done.4) | copy-start | bytes 1572868
  180.9 10.4 %copy-start.19 = (bf16[8,128,128]{2,1,0:T(8,128)(2,1)S(1)}, bf16[8,128,128]{2,1,0:T(8,128)(2,1)}, u32[]{:S(2)}) copy-start(bf16[8,128,128]{2,1,0:T(8,128)(2,1)} %param.10) | copy-start | bytes 786436
  181.8 9.7 %copy-start.7 = (bf16[1,8,8,16,256]{4,3,2,1,0:T(8,128)(2,1)S(1)}, bf16[1,8,8,16,256]{4,3,2,1,0:T(8,128)(2,1)}, u32[]{:S(2)}) copy-start(bf16[1,8,8,16,256]{4,3,2,1,0:T(8,128)(2,1)} %copy-done.6) | copy-start | bytes 1572868
  181.8 9.7 %copy-start.20 = (bf16[8,128,128]{2,1,0:T(8,128)(2,1)S(1)}, bf16[8,128,128]{2,1,0:T(8,128)(2,1)}, u32[]{:S(2)}) copy-start(bf16[8,128,128]{2,1,0:T(8,128)(2,1)} %param.12) | copy-start | bytes 786436
  182.7 18.3 %all-to-all-start.4 = ((bf16[8,4,1,1,6912]{4,0,3,2,1:T(8,128)(2,1)}), bf16[8,4,1,1,6912]{4,0,3,2,1:T(8,128)(2,1)S(1)}, u32[]{:S(2)}, u32[]{:S(2)}) async-start(bf16[8,4,1,1,6912]{4,0,3,2,1:T(8,128)(2,1)} %copy.119), calls=%async_computation.4 | async-start | bytes 884736 | tf_op jit(solution)/shard_map/all_to_all | solution.py:115
  (3 other events, 2.8 us)

commit v9 on v4

--- a/solution.py
+++ b/solution.py
@@ -72,15 +72,10 @@
         "mp", split_axis=1, concat_axis=2, tiled=True,
     )
     gate_back, up_back = back_recv2[0], back_recv2[1]
-    input_grad = jnp.einsum("kio,kot->tki", gate_in, gate_back, preferred_element_type=jnp.float32)
-    input_grad = input_grad + jnp.einsum(
-        "kio,kot->tki", up_in, up_back, preferred_element_type=jnp.float32
-    )
     term_gate_in = jnp.einsum(
         "tki,kot->kio", x_blocks, gate_back, preferred_element_type=jnp.float32
     )
     term_up_in = jnp.einsum("tki,kot->kio", x_blocks, up_back, preferred_element_type=jnp.float32)
-    grad_x = input_grad.astype(jnp.bfloat16).reshape(rows, local_blocks * BLK)
     terms = (term_gate_in, term_gate_out, term_up_in, term_up_out, term_down_in, term_down_out)
     flat = [term.reshape(term.shape[0], groups, -1) for term in terms]
     widths = [piece.shape[2] for piece in flat]
@@ -89,6 +84,8 @@
     summed = stacked.reshape(stacked.shape[0], *sizes, stacked.shape[2])
     for position in reversed(range(len(DP))):
         wire = summed if position == len(DP) - 1 else summed.astype(jnp.bfloat16)
+        if position == 0:
+            wire, gate_back, up_back = lax.optimization_barrier((wire, gate_back, up_back))
         summed = lax.all_to_all(
             wire, DP[position], split_axis=1 + position, concat_axis=1 + position, tiled=True
         ).astype(jnp.float32).sum(axis=1 + position, keepdims=True)
@@ -99,6 +96,11 @@
         piece = summed[:, 0, start:start + width]
         start += width
         outs.append(piece.reshape(term.shape[0], term.shape[1] // groups, term.shape[2]) * scale)
+    input_grad = jnp.einsum("kio,kot->tki", gate_in, gate_back, preferred_element_type=jnp.float32)
+    input_grad = input_grad + jnp.einsum(
+        "kio,kot->tki", up_in, up_back, preferred_element_type=jnp.float32
+    )
+    grad_x = input_grad.astype(jnp.bfloat16).reshape(rows, local_blocks * BLK)
     return (grad_x, *outs)
 
 

time: 196 us -> 196 us (level)
  no operation moved by 1% of the time
where the time goes in v9:
time: 196 us; the launch traced here: 195 us
  blocking collectives  55.2 us (28%)
  local copies, waits for them, and re-layouts  43.9 us (22%)
  waiting for transfers between devices  35.5 us (18%)
  starting transfers between devices  31.6 us (16%)
  matrix products  17.9 us (9%)
  other arithmetic  9.93 us (5%)
    all_to_all x2, blocking collectives, shards(): lax.all_to_all(wire, DP[position], split_axis=1 + position, concat_axis=1...  55.2 us
    all_to_all x1, waiting for transfers between devices, shards(): lax.all_to_all(jnp.stack([gate_mid, up_mid, back_mid]), 'mp', split_axis=...  23.5 us
    unnamed x67, local copies, waits for them, and re-layouts  20.2 us
    concatenate x8, local copies, waits for them, and re-layouts, shards(): stacked = jnp.concatenate(flat, axis=2)  13.4 us
    all_to_all x1, starting transfers between devices, shards(): lax.all_to_all(jnp.stack([gate_mid, up_mid, back_mid]), 'mp', split_axis=...  11.8 us
    all_to_all x1, waiting for transfers between devices, shards(): lax.all_to_all(wire, DP[position], split_axis=1 + position, concat_axis=1...  10.6 us
    all_to_all x1, starting transfers between devices, shards(): lax.all_to_all(wire, DP[position], split_axis=1 + position, concat_axis=1...  7.98 us
    all_to_all x1, starting transfers between devices, shards(): lax.all_to_all(jnp.stack([narrow(gate_grad, gate_out), narrow(up_grad, up...  7.72 us
  transfers between devices with their start and end apart: 4, of which 3 were waited for; matrix products, arithmetic and copies ran while one was open for 15% of the time, Pallas kernels for 0%

profile of v9, /device:TPU:1, one launch (start us, length us, event | category | flops | bytes accessed | tf_op | source)
XLA Modules:
  0.0 195.2 jit_solution(11559601574837449792)
XLA Ops:
  0.6 1.1 copy.88
  2.9 1.1 copy.138
  6.1 1.4 pad_maximum_fusion
  7.4 11.8 %all-to-all-start = ((bf16[3,64,16,256]{3,2,0,1:T(8,128)(2,1)}), bf16[3,64,16,256]{3,2,0,1:T(8,128)(2,1)S(1)}, u32[]{:S(2)}, u32[]{:S(2)}) async-start(bf16[3,64,16,256]{3,2,0,1:T(8,128)(2,1)} %pad_maximum_fusion), calls=%async_computation | async-start | bytes 3145728 | tf_op jit(solution)/shard_map/all_to_all | solution.py:38
  19.2 1.8 copy.113
  21.0 23.5 %all-to-all-done = bf16[3,64,16,256]{3,2,0,1:T(8,128)(2,1)S(1)} async-done(((bf16[3,64,16,256]{3,2,0,1:T(8,128)(2,1)}), bf16[3,64,16,256]{3,2,0,1:T(8,128)(2,1)S(1)}, u32[]{:S(2)}, u32[]{:S(2)}) %all-to-all-start) | async-done | bytes 1572896 | tf_op jit(solution)/shard_map/all_to_all | solution.py:38
  44.9 1.2 copy-done.9
  48.5 3.5 %fusion.7 = (bf16[8,448,256]{2,1,0:T(8,128)(2,1)S(1)}, bf16[8,448,256]{2,1,0:T(8,128)(2,1)}, bf16[8,448,256]{2,1,0:T(8,128)(2,1)}) fusion(f32[8,256,448]{1,2,0:T(8,128)S(1)} %fusion.48, f32[8,256,448]{1,2,0:T(8,128)S(1)} %fusion.47, bf16[8,128,448]{1,2,0:T(8,128)(2,1)S(1)} %copy-done.25, bf16[8,128,256]{2,1,0:T(8,128)(2,1)S(1)} %bitcast.188), kind=kOutput, calls=%fused_computation.12 | convolution fusion | flops 248643584 | bytes 14286848 | tf_op jit(solution)/shard_map/jct,jco->jot/dot_general | solution.py:29
  52.0 1.2 copy-done.20
  54.0 1.1 copy.115
  55.2 4.1 %all-to-all-start.2 = ((bf16[64,16,256]{2,1,0:T(8,128)(2,1)}), bf16[64,16,256]{2,1,0:T(8,128)(2,1)S(1)}, u32[]{:S(2)}, u32[]{:S(2)}) async-start(bf16[64,16,256]{2,1,0:T(8,128)(2,1)} %copy.115), calls=%async_computation.2 | async-start | bytes 1048576 | tf_op jit(solution)/shard_map/all_to_all | solution.py:50
  59.3 1.9 copy.100
  61.1 2.7 %copy.102 = bf16[8,128,448]{2,0,1:T(8,128)(2,1)} copy(bf16[8,128,448]{1,2,0:T(8,128)(2,1)} %param.13) | data formatting | bytes 1835008 | tf_op args[5]
  63.8 2.7 %fusion.15 = bf16[8,256,64,2]{1,2,3,0:T(8,128)(2,1)S(1)} fusion(bf16[8,448,256]{2,1,0:T(8,128)(2,1)} %get-tuple-element.42, bf16[8,64,2,448]{3,0,2,1:T(8,128)(2,1)} %bitcast.201), kind=kOutput, calls=%fused_computation.25 | convolution fusion | flops 235143168 | bytes 3276800 | tf_op jit(solution)/shard_map/jot,jkpo->kjpt/dot_general | solution.py:67
  69.0 1.3 all-to-all-done.2
  71.1 7.7 %all-to-all-start.1 = ((bf16[2,64,16,256]{3,2,0,1:T(8,128)(2,1)}), bf16[2,64,16,256]{3,2,0,1:T(8,128)(2,1)}, u32[]{:S(2)}, u32[]{:S(2)}) async-start(bf16[2,64,16,256]{3,2,0,1:T(8,128)(2,1)} %pad_maximum_fusion.1), calls=%async_computation.1 | async-start | bytes 2097152 | tf_op jit(solution)/shard_map/all_to_all | solution.py:70
  78.9 2.1 %fusion.46 = f32[8,448,128]{2,1,0:T(8,128)S(1)} fusion(bf16[8,448,256]{2,1,0:T(8,128)(2,1)} %copy-done.20, bf16[8,128,256]{2,1,0:T(8,128)(2,1)S(1)} %bitcast.184), kind=kOutput, calls=%fused_computation.70 | convolution fusion | flops 234881024 | bytes 4194304 | tf_op jit(solution)/shard_map/jot,jqt->joq/dot_general | solution.py:54
  81.0 2.2 %concatenate.20 = f32[8,4,4,2,1792]{4,3,2,1,0:T(2,128)} reshape(f32[8,448,128]{2,1,0:T(8,128)S(1)} %fusion.46) | data formatting | bytes 3670016 | tf_op jit(solution)/shard_map/concatenate | solution.py:82
  83.2 2.2 %fusion.44 = f32[8,128,448]{2,1,0:T(8,128)S(1)} fusion(bf16[8,128,256]{2,1,0:T(8,128)(2,1)S(1)} %bitcast.178, bf16[8,448,256]{2,1,0:T(8,128)(2,1)} %get-tuple-element.42), kind=kOutput, calls=%fused_computation.68 | convolution fusion | flops 234881024 | bytes 4194304 | tf_op jit(solution)/shard_map/jct,jot->jco/dot_general | solution.py:60
  85.4 2.9 %concatenate.17 = f32[8,4,4,2,1792]{4,3,2,1,0:T(2,128)} reshape(f32[8,128,448]{2,1,0:T(8,128)S(1)} %fusion.44) | data formatting | bytes 3670016 | tf_op jit(solution)/shard_map/concatenate | solution.py:82
  88.3 2.2 %fusion.45 = f32[8,128,448]{2,1,0:T(8,128)S(1)} fusion(bf16[8,128,256]{2,1,0:T(8,128)(2,1)S(1)} %bitcast.189, bf16[8,448,256]{2,1,0:T(8,128)(2,1)} %get-tuple-element.43), kind=kOutput, calls=%fused_computation.69 | convolution fusion | flops 234881024 | bytes 4194304 | tf_op jit(solution)/shard_map/jct,jot->jco/dot_general | solution.py:63
  90.5 2.9 %concatenate.19 = f32[8,4,4,2,1792]{4,3,2,1,0:T(2,128)} reshape(f32[8,128,448]{2,1,0:T(8,128)S(1)} %fusion.45) | data formatting | bytes 3670016 | tf_op jit(solution)/shard_map/concatenate | solution.py:82
  94.9 1.4 copy.173
  100.1 1.3 concatenate.18
  103.2 1.2 copy-done
  105.6 1.8 copy.118
  107.4 29.3 %all_to_all.63 = f32[8,4,4,2,6912]{4,2,1,0,3:T(4,128)} all-to-all(f32[8,4,4,2,6912]{4,2,1,0,3:T(4,128)S(1)} %copy.118), channel_id=1, replica_groups=mesh['dz'=4,'dx'=4,'dc'=2,'mp'=8] {'dc'}, dimensions={3} | all-to-all | bytes 14155776 | tf_op jit(solution)/shard_map/all_to_all | solution.py:89
  136.7 5.6 %reduce_sum.30 = bf16[8,4,4,6912]{3,2,1,0:T(4,128)(2,1)S(1)} reduce(f32[8,4,4,2,6912]{4,2,1,0,3:T(4,128)} %all_to_all.63, f32[]{:T(128)} %constant.1.clone.1), dimensions={3}, to_apply=%region_0.0 | reduce | flops 884736 | bytes 8847364 | tf_op jit(solution)/shard_map/reduce_sum | solution.py:91
  143.0 25.9 %all_to_all.64 = bf16[8,4,4,1,6912]{4,1,0,3,2:T(4,128)(2,1)S(1)} all-to-all(bf16[8,4,4,1,6912]{4,1,0,3,2:T(4,128)(2,1)S(1)} %copy.119), channel_id=1, replica_groups=mesh['dz'=4,'dx'=4,'dc'=2,'mp'=8] {'dx'}, dimensions={2} | all-to-all | bytes 3538944 | tf_op jit(solution)/shard_map/all_to_all | solution.py:89
  168.8 1.2 reduce_sum.31
  170.9 8.0 %all-to-all-start.5 = ((bf16[8,4,1,1,6912]{4,0,3,2,1:T(8,128)(2,1)}), bf16[8,4,1,1,6912]{4,0,3,2,1:T(8,128)(2,1)S(1)}, u32[]{:S(2)}, u32[]{:S(2)}) async-start(bf16[8,4,1,1,6912]{4,0,3,2,1:T(8,128)(2,1)} %copy.120), calls=%async_computation.5 | async-start | bytes 884736 | tf_op jit(solution)/shard_map/all_to_all | solution.py:89
  180.5 10.6 %all-to-all-done.5 = bf16[8,4,1,1,6912]{4,0,3,2,1:T(8,128)(2,1)S(1)} async-done(((bf16[8,4,1,1,6912]{4,0,3,2,1:T(8,128)(2,1)}), bf16[8,4,1,1,6912]{4,0,3,2,1:T(8,128)(2,1)S(1)}, u32[]{:S(2)}, u32[]{:S(2)}) %all-to-all-start.5) | async-done | bytes 442400 | tf_op jit(solution)/shard_map/all_to_all | solution.py:89
  (97 shorter events, 24.9 us)
Async XLA Ops:
  4.1 1.3 copy-start.11
  4.4 1.1 copy-start.26
  7.4 11.8 %copy-start.8 = (bf16[8,448,128]{2,1,0:T(8,128)(2,1)S(1)}, bf16[8,448,128]{2,1,0:T(8,128)(2,1)}, u32[]{:S(2)}) copy-start(bf16[8,448,128]{2,1,0:T(8,128)(2,1)} %param.14) | copy-start | bytes 2752516
  7.4 37.2 %all-to-all-start = ((bf16[3,64,16,256]{3,2,0,1:T(8,128)(2,1)}), bf16[3,64,16,256]{3,2,0,1:T(8,128)(2,1)S(1)}, u32[]{:S(2)}, u32[]{:S(2)}) async-start(bf16[3,64,16,256]{3,2,0,1:T(8,128)(2,1)} %pad_maximum_fusion), calls=%async_computation | async-start | bytes 3145728 | tf_op jit(solution)/shard_map/all_to_all | solution.py:38
  44.8 1.4 copy-start.9
  44.9 3.1 %copy-start.13 = (bf16[1,8,8,16,256]{4,3,2,1,0:T(8,128)(2,1)}, bf16[1,8,8,16,256]{4,3,2,1,0:T(8,128)(2,1)S(1)}, u32[]{:S(2)}) copy-start(bf16[1,8,8,16,256]{4,3,2,1,0:T(8,128)(2,1)S(1)} %get-tuple-element.44) | copy-start | bytes 1572868
  46.1 1.2 copy-start.10
  47.3 1.2 copy-start.25
  48.5 4.8 %copy-start.23 = (bf16[8,448,128]{1,0,2:T(8,128)(2,1)S(1)}, bf16[8,448,128]{1,0,2:T(8,128)(2,1)}, u32[]{:S(2)}) copy-start(bf16[8,448,128]{1,0,2:T(8,128)(2,1)} %copy.113) | copy-start | bytes 2752516
  52.0 1.2 copy-start.20
  55.2 15.1 %all-to-all-start.2 = ((bf16[64,16,256]{2,1,0:T(8,128)(2,1)}), bf16[64,16,256]{2,1,0:T(8,128)(2,1)S(1)}, u32[]{:S(2)}, u32[]{:S(2)}) async-start(bf16[64,16,256]{2,1,0:T(8,128)(2,1)} %copy.115), calls=%async_computation.2 | async-start | bytes 1048576 | tf_op jit(solution)/shard_map/all_to_all | solution.py:50
  63.8 3.0 %copy-start.19 = (bf16[8,448,256]{2,1,0:T(8,128)(2,1)S(1)}, bf16[8,448,256]{2,1,0:T(8,128)(2,1)}, u32[]{:S(2)}) copy-start(bf16[8,448,256]{2,1,0:T(8,128)(2,1)} %get-tuple-element.43) | copy-start | bytes 5505028
  63.8 3.0 %copy-start.24 = (bf16[8,128,448]{2,0,1:T(8,128)(2,1)S(1)}, bf16[8,128,448]{2,0,1:T(8,128)(2,1)}, u32[]{:S(2)}) copy-start(bf16[8,128,448]{2,0,1:T(8,128)(2,1)} %copy.102) | copy-start | bytes 2752516
  70.3 0.8 copy-start.15
  71.1 23.8 %all-to-all-start.1 = ((bf16[2,64,16,256]{3,2,0,1:T(8,128)(2,1)}), bf16[2,64,16,256]{3,2,0,1:T(8,128)(2,1)}, u32[]{:S(2)}, u32[]{:S(2)}) async-start(bf16[2,64,16,256]{3,2,0,1:T(8,128)(2,1)} %pad_maximum_fusion.1), calls=%async_computation.1 | async-start | bytes 2097152 | tf_op jit(solution)/shard_map/all_to_all | solution.py:70
  85.4 2.9 %copy-start.14 = (bf16[1,8,8,16,256]{4,3,2,1,0:T(8,128)(2,1)S(1)}, bf16[1,8,8,16,256]{4,3,2,1,0:T(8,128)(2,1)}, u32[]{:S(2)}) copy-start(bf16[1,8,8,16,256]{4,3,2,1,0:T(8,128)(2,1)} %copy-done.13) | copy-start | bytes 1572868
  90.5 2.9 %copy-start.16 = (bf16[64,16,256]{2,1,0:T(8,128)(2,1)S(1)}, bf16[64,16,256]{2,1,0:T(8,128)(2,1)}, u32[]{:S(2)}) copy-start(bf16[64,16,256]{2,1,0:T(8,128)(2,1)} %copy-done.15) | copy-start | bytes 1572868
  90.5 3.0 %copy-start.12 = (bf16[256,1024]{1,0:T(8,128)(2,1)S(1)}, bf16[256,1024]{1,0:T(8,128)(2,1)}, u32[]{:S(2)}) copy-start(bf16[256,1024]{1,0:T(8,128)(2,1)} %param.9) | copy-start | bytes 1572868
  94.9 2.3 %copy-start.3 = (bf16[256,1024]{1,0:T(8,128)(2,1)S(1)}, bf16[256,1024]{1,0:T(8,128)(2,1)}, u32[]{:S(2)}) copy-start(bf16[256,1024]{1,0:T(8,128)(2,1)} %param.8) | copy-start | bytes 1572868
  96.4 0.8 copy-start.4
  96.4 2.6 %copy-start.6 = (bf16[1,8,8,16,256]{4,3,2,1,0:T(8,128)(2,1)}, bf16[1,8,8,16,256]{4,3,2,1,0:T(8,128)(2,1)S(1)}, u32[]{:S(2)}) copy-start(bf16[1,8,8,16,256]{4,3,2,1,0:T(8,128)(2,1)S(1)} %get-tuple-element.47) | copy-start | bytes 1572868
  98.8 2.7 %copy-start.2 = (f32[8,4,4,2,1792]{4,3,2,1,0:T(2,128)S(1)}, f32[8,4,4,2,1792]{4,3,2,1,0:T(2,128)}, u32[]{:S(2)}) copy-start(f32[8,4,4,2,1792]{4,3,2,1,0:T(2,128)} %concatenate.17) | copy-start | bytes 5505028
  99.1 2.3 %copy-start.18 = (f32[8,4,4,2,512]{4,3,2,1,0:T(2,128)S(1)}, f32[8,4,4,2,512]{4,3,2,1,0:T(2,128)}, u32[]{:S(2)}) copy-start(f32[8,4,4,2,512]{4,3,2,1,0:T(2,128)} %concatenate.16) | copy-start | bytes 1572868
  101.4 1.5 copy-start.1
  102.9 1.5 copy-start
  104.4 1.0 copy-start.17
  168.8 10.1 %copy-start.5 = (bf16[1,8,8,16,256]{4,3,2,1,0:T(8,128)(2,1)S(1)}, bf16[1,8,8,16,256]{4,3,2,1,0:T(8,128)(2,1)}, u32[]{:S(2)}) copy-start(bf16[1,8,8,16,256]{4,3,2,1,0:T(8,128)(2,1)} %copy-done.4) | copy-start | bytes 1572868
  168.8 10.1 %copy-start.21 = (bf16[8,128,128]{2,1,0:T(8,128)(2,1)S(1)}, bf16[8,128,128]{2,1,0:T(8,128)(2,1)}, u32[]{:S(2)}) copy-start(bf16[8,128,128]{2,1,0:T(8,128)(2,1)} %param.10) | copy-start | bytes 786436
  170.1 9.1 %copy-start.7 = (bf16[1,8,8,16,256]{4,3,2,1,0:T(8,128)(2,1)S(1)}, bf16[1,8,8,16,256]{4,3,2,1,0:T(8,128)(2,1)}, u32[]{:S(2)}) copy-start(bf16[1,8,8,16,256]{4,3,2,1,0:T(8,128)(2,1)} %copy-done.6) | copy-start | bytes 1572868
  170.1 9.1 %copy-start.22 = (bf16[8,128,128]{2,1,0:T(8,128)(2,1)S(1)}, bf16[8,128,128]{2,1,0:T(8,128)(2,1)}, u32[]{:S(2)}) copy-start(bf16[8,128,128]{2,1,0:T(8,128)(2,1)} %param.12) | copy-start | bytes 786436
  170.9 20.2 %all-to-all-start.5 = ((bf16[8,4,1,1,6912]{4,0,3,2,1:T(8,128)(2,1)}), bf16[8,4,1,1,6912]{4,0,3,2,1:T(8,128)(2,1)S(1)}, u32[]{:S(2)}, u32[]{:S(2)}) async-start(bf16[8,4,1,1,6912]{4,0,3,2,1:T(8,128)(2,1)} %copy.120), calls=%async_computation.5 | async-start | bytes 884736 | tf_op jit(solution)/shard_map/all_to_all | solution.py:89

commit v10 on v4

--- a/solution.py
+++ b/solution.py
@@ -88,6 +88,12 @@
     sizes = [lax.axis_size(name) for name in DP]
     summed = stacked.reshape(stacked.shape[0], *sizes, stacked.shape[2])
     for position in reversed(range(len(DP))):
+        if position == len(DP) - 1 and sizes[position] == 2:
+            me = lax.axis_index(DP[position])
+            own = lax.dynamic_index_in_dim(summed, me, axis=1 + position)
+            other = lax.dynamic_index_in_dim(summed, 1 - me, axis=1 + position)
+            summed = own + lax.ppermute(other, DP[position], [(0, 1), (1, 0)])
+            continue
         wire = summed if position == len(DP) - 1 else summed.astype(jnp.bfloat16)
         summed = lax.all_to_all(
             wire, DP[position], split_axis=1 + position, concat_axis=1 + position, tiled=True

time: 196 us -> 191 us (0.974)
  blocking collectives: 55.2 us -> 26.1 us
  starting transfers between devices: 31.6 us -> 49.2 us
  waiting for transfers between devices: 35.5 us -> 42.9 us
  other arithmetic: 9.93 us -> 7.7 us
    all_to_all x2 -> x1, blocking collectives: 55.2 us -> 26.1 us  [shards(): lax.all_to_all(wire, DP[position], split_axis=1 + position, concat_axis=1...]
    ppermute x0 -> x1, starting transfers between devices: none -> 23 us  [shards(): summed = own + lax.ppermute(other, DP[position], [(0, 1), (1, 0)])]
    ppermute x0 -> x1, waiting for transfers between devices: none -> 6.19 us  [shards(): summed = own + lax.ppermute(other, DP[position], [(0, 1), (1, 0)])]
    reduce_sum x3 -> x2, other arithmetic: 6.85 us -> 1.2 us  [shards(): summed = lax.all_to_all(wire, DP[position], split_axis=1 + position, conc...]
    all_to_all x1, starting transfers between devices: 7.98 us -> 3.47 us  [shards(): lax.all_to_all(wire, DP[position], split_axis=1 + position, concat_axis=1...]
    convert_element_type x0 -> x1, other arithmetic: none -> 3.39 us  [shards(): wire = summed if position == len(DP) - 1 else summed.astype(jnp.bfloat16)]
    dynamic_slice x0 -> x1, local copies, waits for them, and re-layouts: none -> 2.34 us  [shards(): other = lax.dynamic_index_in_dim(summed, 1 - me, axis=1 + position)]
    concatenate x8 -> x7, local copies, waits for them, and re-layouts: 13.4 us -> 12.6 us  [shards(): stacked = jnp.concatenate(flat, axis=2)]
  transfers between devices with their start and end apart: 4 -> 5, of which waited for: 3 -> 5; matrix products, arithmetic and copies ran while one was open for 15% -> 15% of each run, Pallas kernels for 0% -> 0%
where the time goes in v10:
time: 191 us
  starting transfers between devices  49.2 us (26%)
  local copies, waits for them, and re-layouts  44.8 us (23%)
  waiting for transfers between devices  42.9 us (22%)
  blocking collectives  26.1 us (14%)
  matrix products  18.7 us (10%)
  other arithmetic  7.7 us (4%)
    all_to_all x1, blocking collectives, shards(): lax.all_to_all(wire, DP[position], split_axis=1 + position, concat_axis=1...  26.1 us
    all_to_all x1, waiting for transfers between devices, shards(): lax.all_to_all(jnp.stack([gate_mid, up_mid, back_mid]), 'mp', split_axis=...  23.5 us
    ppermute x1, starting transfers between devices, shards(): summed = own + lax.ppermute(other, DP[position], [(0, 1), (1, 0)])  23 us
    unnamed x57, local copies, waits for them, and re-layouts  19.8 us
    concatenate x7, local copies, waits for them, and re-layouts, shards(): stacked = jnp.concatenate(flat, axis=2)  12.6 us
    all_to_all x1, starting transfers between devices, shards(): lax.all_to_all(jnp.stack([gate_mid, up_mid, back_mid]), 'mp', split_axis=...  11.8 us
    all_to_all x1, waiting for transfers between devices, shards(): lax.all_to_all(wire, DP[position], split_axis=1 + position, concat_axis=1...  10.6 us
    all_to_all x1, starting transfers between devices, shards(): lax.all_to_all(jnp.stack([narrow(gate_grad, gate_out), narrow(up_grad, up...  6.92 us
  transfers between devices with their start and end apart: 5, of which 5 were waited for; matrix products, arithmetic and copies ran while one was open for 15% of the time, Pallas kernels for 0%

profile of v10, /device:TPU:1, one launch (start us, length us, event | category | flops | bytes accessed | tf_op | source)
XLA Modules:
  0.0 190.5 jit_solution(4939722690720898128)
XLA Ops:
  2.9 1.1 copy.178
  6.1 1.4 pad_maximum_fusion
  7.4 11.8 %all-to-all-start = ((bf16[3,64,16,256]{3,2,0,1:T(8,128)(2,1)}), bf16[3,64,16,256]{3,2,0,1:T(8,128)(2,1)S(1)}, u32[]{:S(2)}, u32[]{:S(2)}) async-start(bf16[3,64,16,256]{3,2,0,1:T(8,128)(2,1)} %pad_maximum_fusion), calls=%async_computation | async-start | bytes 3145728 | tf_op jit(solution)/shard_map/all_to_all | solution.py:38
  19.2 1.8 copy.149
  21.0 23.5 %all-to-all-done = bf16[3,64,16,256]{3,2,0,1:T(8,128)(2,1)S(1)} async-done(((bf16[3,64,16,256]{3,2,0,1:T(8,128)(2,1)}), bf16[3,64,16,256]{3,2,0,1:T(8,128)(2,1)S(1)}, u32[]{:S(2)}, u32[]{:S(2)}) %all-to-all-start) | async-done | bytes 1572896 | tf_op jit(solution)/shard_map/all_to_all | solution.py:38
  48.3 3.5 %fusion.7 = (bf16[8,448,256]{2,1,0:T(8,128)(2,1)S(1)}, bf16[8,448,256]{2,1,0:T(8,128)(2,1)}, bf16[8,448,256]{2,1,0:T(8,128)(2,1)}) fusion(f32[8,256,448]{1,2,0:T(8,128)S(1)} %fusion.48, f32[8,256,448]{1,2,0:T(8,128)S(1)} %fusion.47, bf16[8,128,448]{1,2,0:T(8,128)(2,1)S(1)} %copy-done.20, bf16[8,128,256]{2,1,0:T(8,128)(2,1)S(1)} %bitcast.184), kind=kOutput, calls=%fused_computation.12 | convolution fusion | flops 248643584 | bytes 14286848 | tf_op jit(solution)/shard_map/jct,jco->jot/dot_general | solution.py:29
  51.8 1.3 copy-done.16
  55.0 4.1 %all-to-all-start.2 = ((bf16[64,16,256]{2,1,0:T(8,128)(2,1)}), bf16[64,16,256]{2,1,0:T(8,128)(2,1)S(1)}, u32[]{:S(2)}, u32[]{:S(2)}) async-start(bf16[64,16,256]{2,1,0:T(8,128)(2,1)} %copy.151), calls=%async_computation.2 | async-start | bytes 1048576 | tf_op jit(solution)/shard_map/all_to_all | solution.py:50
  59.1 1.8 copy.136
  60.9 1.9 copy.138
  62.8 2.7 %fusion.15 = bf16[8,256,64,2]{1,2,3,0:T(8,128)(2,1)S(1)} fusion(bf16[8,448,256]{2,1,0:T(8,128)(2,1)} %get-tuple-element.43, bf16[8,64,2,448]{3,0,2,1:T(8,128)(2,1)} %bitcast.196), kind=kOutput, calls=%fused_computation.28 | convolution fusion | flops 235143168 | bytes 3276800 | tf_op jit(solution)/shard_map/jot,jkpo->kjpt/dot_general | solution.py:67
  68.0 2.1 %all-to-all-done.2 = bf16[64,16,256]{2,1,0:T(8,128)(2,1)S(1)} async-done(((bf16[64,16,256]{2,1,0:T(8,128)(2,1)}), bf16[64,16,256]{2,1,0:T(8,128)(2,1)S(1)}, u32[]{:S(2)}, u32[]{:S(2)}) %all-to-all-start.2) | async-done | bytes 524320 | tf_op jit(solution)/shard_map/all_to_all | solution.py:50
  70.1 6.9 %all-to-all-start.1 = ((bf16[2,64,16,256]{3,2,0,1:T(8,128)(2,1)}), bf16[2,64,16,256]{3,2,0,1:T(8,128)(2,1)}, u32[]{:S(2)}, u32[]{:S(2)}) async-start(bf16[2,64,16,256]{3,2,0,1:T(8,128)(2,1)} %pad_maximum_fusion.1), calls=%async_computation.1 | async-start | bytes 2097152 | tf_op jit(solution)/shard_map/all_to_all | solution.py:70
  77.0 2.1 %fusion.46 = f32[8,448,128]{2,1,0:T(8,128)S(1)} fusion(bf16[8,448,256]{2,1,0:T(8,128)(2,1)} %copy-done.16, bf16[8,128,256]{2,1,0:T(8,128)(2,1)S(1)} %bitcast.180), kind=kOutput, calls=%fused_computation.71 | convolution fusion | flops 234881024 | bytes 4194304 | tf_op jit(solution)/shard_map/jot,jqt->joq/dot_general | solution.py:54
  79.2 2.2 %concatenate.20 = f32[8,4,4,2,1792]{4,3,2,1,0:T(2,128)} reshape(f32[8,448,128]{2,1,0:T(8,128)S(1)} %fusion.46) | data formatting | bytes 3670016 | tf_op jit(solution)/shard_map/concatenate | solution.py:87
  81.4 2.2 %fusion.44 = f32[8,128,448]{2,1,0:T(8,128)S(1)} fusion(bf16[8,128,256]{2,1,0:T(8,128)(2,1)S(1)} %bitcast.172, bf16[8,448,256]{2,1,0:T(8,128)(2,1)} %get-tuple-element.43), kind=kOutput, calls=%fused_computation.69 | convolution fusion | flops 234881024 | bytes 4194304 | tf_op jit(solution)/shard_map/jct,jot->jco/dot_general | solution.py:60
  83.6 2.9 %concatenate.17 = f32[8,4,4,2,1792]{4,3,2,1,0:T(2,128)} reshape(f32[8,128,448]{2,1,0:T(8,128)S(1)} %fusion.44) | data formatting | bytes 3670016 | tf_op jit(solution)/shard_map/concatenate | solution.py:87
  86.5 2.2 %fusion.45 = f32[8,128,448]{2,1,0:T(8,128)S(1)} fusion(bf16[8,128,256]{2,1,0:T(8,128)(2,1)S(1)} %bitcast.185, bf16[8,448,256]{2,1,0:T(8,128)(2,1)} %get-tuple-element.44), kind=kOutput, calls=%fused_computation.70 | convolution fusion | flops 234881024 | bytes 4194304 | tf_op jit(solution)/shard_map/jct,jot->jco/dot_general | solution.py:63
  88.7 2.9 %concatenate.19 = f32[8,4,4,2,1792]{4,3,2,1,0:T(2,128)} reshape(f32[8,128,448]{2,1,0:T(8,128)S(1)} %fusion.45) | data formatting | bytes 3670016 | tf_op jit(solution)/shard_map/concatenate | solution.py:87
  93.5 1.4 copy.219
  97.6 2.1 %copy.147 = f32[8,128,128]{2,1,0:T(8,128)} copy(f32[8,128,128]{1,2,0:T(8,128)} %convolution_bitcast_fusion) | data formatting | bytes 1048576 | tf_op jit(solution)/shard_map/tki,kot->kio/dot_general | solution.py:82
  99.7 2.1 %concatenate.18 = f32[8,4,4,2,512]{4,3,2,1,0:T(2,128)} reshape(f32[8,128,128]{2,1,0:T(8,128)} %copy.147) | data formatting | bytes 1048576 | tf_op jit(solution)/shard_map/concatenate | solution.py:87
  105.3 1.3 copy_dynamic-update-slice_fusion
  107.0 2.3 %constant_dynamic-slice_fusion = f32[8,4,4,1,6912]{4,0,3,2,1:T(8,128)} fusion(f32[8,4,4,2,6912]{4,0,3,2,1:T(8,128)S(1)} %copy_dynamic-update-slice_fusion.3, s32[]{:T(128)S(6)} %select_n.8), kind=kLoop, calls=%fused_computation.66 | loop fusion | bytes 7077892 | tf_op jit(solution)/shard_map/jit(dynamic_index_in_dim)/dynamic_slice | solution.py:94
  109.3 1.6 copy-done
  110.9 23.0 %collective-permute-start = (f32[8,4,4,1,6912]{4,0,3,2,1:T(8,128)}, f32[8,4,4,1,6912]{4,0,3,2,1:T(8,128)}, u32[]{:S(2)}, u32[]{:S(2)}) collective-permute-start(f32[8,4,4,1,6912]{4,0,3,2,1:T(8,128)} %constant_dynamic-slice_fusion), channel_id=1, source_target_pairs={{0,8},{8,0},{1,9},{9,1},{2,10},{10,2},{3,11},{11,3},{4,12},{12,4},... | collective-permute-start | bytes 10616840 | tf_op jit(solution)/shard_map/ppermute | solution.py:95
  133.8 6.2 %collective-permute-done = f32[8,4,4,1,6912]{4,0,3,2,1:T(8,128)} collective-permute-done((f32[8,4,4,1,6912]{4,0,3,2,1:T(8,128)}, f32[8,4,4,1,6912]{4,0,3,2,1:T(8,128)}, u32[]{:S(2)}, u32[]{:S(2)}) %collective-permute-start) | collective-permute-done | bytes 3538976 | tf_op jit(solution)/shard_map/ppermute | solution.py:95
  140.0 3.4 %add_convert_fusion = bf16[8,4,4,1,6912]{4,0,3,2,1:T(8,128)(2,1)S(1)} fusion(f32[8,4,4,1,6912]{4,0,3,2,1:T(8,128)} %collective-permute-done, f32[8,4,4,2,6912]{4,0,3,2,1:T(8,128)} %copy-done, s32[]{:T(128)S(6)} %select_n.7), kind=kLoop, calls=%fused_computation.15 | loop fusion | flops 1769472 | bytes 8847364 | tf_op jit(solution)/shard_map/convert_element_type | solution.py:97
  143.5 26.1 %all_to_all.58 = bf16[8,4,4,1,6912]{4,0,3,1,2:T(8,128)(2,1)S(1)} all-to-all(bf16[8,4,4,1,6912]{4,0,3,1,2:T(8,128)(2,1)S(1)} %copy.160), channel_id=1, replica_groups=mesh['dz'=4,'dx'=4,'dc'=2,'mp'=8] {'dx'}, dimensions={2} | all-to-all | bytes 3538944 | tf_op jit(solution)/shard_map/all_to_all | solution.py:98
  169.6 1.1 reduce_sum.21
  170.8 3.5 %all-to-all-start.4 = ((bf16[8,4,1,1,6912]{4,0,3,2,1:T(8,128)(2,1)}), bf16[8,4,1,1,6912]{4,0,3,2,1:T(8,128)(2,1)S(1)}, u32[]{:S(2)}, u32[]{:S(2)}) async-start(bf16[8,4,1,1,6912]{4,0,3,2,1:T(8,128)(2,1)} %bitcast.46), calls=%async_computation.4 | async-start | bytes 884736 | tf_op jit(solution)/shard_map/all_to_all | solution.py:98
  175.8 10.6 %all-to-all-done.4 = bf16[8,4,1,1,6912]{4,0,3,2,1:T(8,128)(2,1)S(1)} async-done(((bf16[8,4,1,1,6912]{4,0,3,2,1:T(8,128)(2,1)}), bf16[8,4,1,1,6912]{4,0,3,2,1:T(8,128)(2,1)S(1)}, u32[]{:S(2)}, u32[]{:S(2)}) %all-to-all-start.4) | async-done | bytes 442400 | tf_op jit(solution)/shard_map/all_to_all | solution.py:98
  (87 shorter events, 26.3 us)
Async XLA Ops:
  4.1 1.3 copy-start.8
  4.4 1.1 copy-start.21
  7.4 11.8 %copy-start.5 = (bf16[8,448,128]{2,1,0:T(8,128)(2,1)S(1)}, bf16[8,448,128]{2,1,0:T(8,128)(2,1)}, u32[]{:S(2)}) copy-start(bf16[8,448,128]{2,1,0:T(8,128)(2,1)} %param.14) | copy-start | bytes 2752516
  7.4 37.2 %all-to-all-start = ((bf16[3,64,16,256]{3,2,0,1:T(8,128)(2,1)}), bf16[3,64,16,256]{3,2,0,1:T(8,128)(2,1)S(1)}, u32[]{:S(2)}, u32[]{:S(2)}) async-start(bf16[3,64,16,256]{3,2,0,1:T(8,128)(2,1)} %pad_maximum_fusion), calls=%async_computation | async-start | bytes 3145728 | tf_op jit(solution)/shard_map/all_to_all | solution.py:38
  44.8 1.2 copy-start.6
  45.9 1.2 copy-start.7
  47.1 1.2 copy-start.20
  48.3 4.8 %copy-start.19 = (bf16[8,448,128]{1,0,2:T(8,128)(2,1)S(1)}, bf16[8,448,128]{1,0,2:T(8,128)(2,1)}, u32[]{:S(2)}) copy-start(bf16[8,448,128]{1,0,2:T(8,128)(2,1)} %copy.149) | copy-start | bytes 2752516
  51.8 1.3 copy-start.16
  55.0 15.1 %all-to-all-start.2 = ((bf16[64,16,256]{2,1,0:T(8,128)(2,1)}), bf16[64,16,256]{2,1,0:T(8,128)(2,1)S(1)}, u32[]{:S(2)}, u32[]{:S(2)}) async-start(bf16[64,16,256]{2,1,0:T(8,128)(2,1)} %copy.151), calls=%async_computation.2 | async-start | bytes 1048576 | tf_op jit(solution)/shard_map/all_to_all | solution.py:50
  62.8 3.0 %copy-start.15 = (bf16[8,448,256]{2,1,0:T(8,128)(2,1)S(1)}, bf16[8,448,256]{2,1,0:T(8,128)(2,1)}, u32[]{:S(2)}) copy-start(bf16[8,448,256]{2,1,0:T(8,128)(2,1)} %get-tuple-element.44) | copy-start | bytes 5505028
  70.1 6.9 %copy-start.10 = (bf16[64,16,256]{2,1,0:T(8,128)(2,1)}, bf16[64,16,256]{2,1,0:T(8,128)(2,1)S(1)}, u32[]{:S(2)}) copy-start(bf16[64,16,256]{2,1,0:T(8,128)(2,1)S(1)} %all-to-all-done.2) | copy-start | bytes 1572868
  70.1 23.4 %all-to-all-start.1 = ((bf16[2,64,16,256]{3,2,0,1:T(8,128)(2,1)}), bf16[2,64,16,256]{3,2,0,1:T(8,128)(2,1)}, u32[]{:S(2)}, u32[]{:S(2)}) async-start(bf16[2,64,16,256]{3,2,0,1:T(8,128)(2,1)} %pad_maximum_fusion.1), calls=%async_computation.1 | async-start | bytes 2097152 | tf_op jit(solution)/shard_map/all_to_all | solution.py:70
  88.7 2.9 %copy-start.11 = (bf16[64,16,256]{2,1,0:T(8,128)(2,1)S(1)}, bf16[64,16,256]{2,1,0:T(8,128)(2,1)}, u32[]{:S(2)}) copy-start(bf16[64,16,256]{2,1,0:T(8,128)(2,1)} %copy-done.10) | copy-start | bytes 1572868
  88.7 2.9 %copy-start.9 = (bf16[256,1024]{1,0:T(8,128)(2,1)S(1)}, bf16[256,1024]{1,0:T(8,128)(2,1)}, u32[]{:S(2)}) copy-start(bf16[256,1024]{1,0:T(8,128)(2,1)} %param.9) | copy-start | bytes 1572868
  93.5 1.5 copy-start.4
  96.5 5.6 %copy-start.3 = (f32[8,4,4,2,1792]{4,3,2,1,0:T(2,128)S(1)}, f32[8,4,4,2,1792]{4,3,2,1,0:T(2,128)}, u32[]{:S(2)}) copy-start(f32[8,4,4,2,1792]{4,3,2,1,0:T(2,128)} %concatenate.17) | copy-start | bytes 5505028
  97.6 4.2 %copy-start.13 = (f32[8,4,4,2,512]{4,3,2,1,0:T(2,128)S(1)}, f32[8,4,4,2,512]{4,3,2,1,0:T(2,128)}, u32[]{:S(2)}) copy-start(f32[8,4,4,2,512]{4,3,2,1,0:T(2,128)} %concatenate.16) | copy-start | bytes 1572868
  102.2 1.1 copy-start.14
  102.2 1.7 copy-start.2
  103.8 1.5 copy-start.1
  105.3 1.3 copy-start.12
  107.0 3.9 %copy-start = (f32[8,4,4,2,6912]{4,0,3,2,1:T(8,128)}, f32[8,4,4,2,6912]{4,0,3,2,1:T(8,128)S(1)}, u32[]{:S(2)}) copy-start(f32[8,4,4,2,6912]{4,0,3,2,1:T(8,128)S(1)} %copy_dynamic-update-slice_fusion.3) | copy-start | bytes 21233668
  110.9 29.1 %collective-permute-start = (f32[8,4,4,1,6912]{4,0,3,2,1:T(8,128)}, f32[8,4,4,1,6912]{4,0,3,2,1:T(8,128)}, u32[]{:S(2)}, u32[]{:S(2)}) collective-permute-start(f32[8,4,4,1,6912]{4,0,3,2,1:T(8,128)} %constant_dynamic-slice_fusion), channel_id=1, source_target_pairs={{0,8},{8,0},{1,9},{9,1},{2,10},{10,2},{3,11},{11,3},{4,12},{12,4},... | collective-permute-start | bytes 10616840 | tf_op jit(solution)/shard_map/ppermute | solution.py:95
  169.6 4.6 %copy-start.17 = (bf16[8,128,128]{2,1,0:T(8,128)(2,1)S(1)}, bf16[8,128,128]{2,1,0:T(8,128)(2,1)}, u32[]{:S(2)}) copy-start(bf16[8,128,128]{2,1,0:T(8,128)(2,1)} %param.10) | copy-start | bytes 786436
  169.6 4.9 %copy-start.18 = (bf16[8,128,128]{2,1,0:T(8,128)(2,1)S(1)}, bf16[8,128,128]{2,1,0:T(8,128)(2,1)}, u32[]{:S(2)}) copy-start(bf16[8,128,128]{2,1,0:T(8,128)(2,1)} %param.12) | copy-start | bytes 786436
  170.8 15.7 %all-to-all-start.4 = ((bf16[8,4,1,1,6912]{4,0,3,2,1:T(8,128)(2,1)}), bf16[8,4,1,1,6912]{4,0,3,2,1:T(8,128)(2,1)S(1)}, u32[]{:S(2)}, u32[]{:S(2)}) async-start(bf16[8,4,1,1,6912]{4,0,3,2,1:T(8,128)(2,1)} %bitcast.46), calls=%async_computation.4 | async-start | bytes 884736 | tf_op jit(solution)/shard_map/all_to_all | solution.py:98

commit v11 on v5

--- a/solution.py
+++ b/solution.py
@@ -83,29 +83,25 @@
     grad_x = input_grad.astype(jnp.bfloat16).reshape(rows, local_blocks * BLK)
     terms = (term_gate_in, term_gate_out, term_up_in, term_up_out, term_down_in, term_down_out)
     sizes = [lax.axis_size(name) for name in DP]
+    me = lax.axis_index(DP[-1])
 
-    def reduce_stage(summed, position, ring=False):
-        wire = summed if position == len(DP) - 1 else summed.astype(jnp.bfloat16)
-        if ring:
-            return lax.psum_scatter(
-                wire, DP[position], scatter_dimension=1 + position, tiled=True
-            ).astype(jnp.float32)
-        return lax.all_to_all(
-            wire, DP[position], split_axis=1 + position, concat_axis=1 + position, tiled=True
-        ).astype(jnp.float32).sum(axis=1 + position, keepdims=True)
-
-    def inner_stages(members, ring):
+    def pair_stage(members):
         flat = [terms[m].reshape(terms[m].shape[0], groups, -1) for m in members]
         stacked = jnp.concatenate(flat, axis=2)
         summed = stacked.reshape(stacked.shape[0], *sizes, stacked.shape[2])
-        for position in reversed(range(1, len(DP))):
-            summed = reduce_stage(summed, position, ring)
-        return summed, [piece.shape[2] for piece in flat]
+        own = lax.dynamic_index_in_dim(summed, me, axis=len(DP), keepdims=False)
+        other = lax.dynamic_index_in_dim(summed, 1 - me, axis=len(DP), keepdims=False)
+        return own + lax.ppermute(other, DP[-1], [(0, 1), (1, 0)]), [p.shape[2] for p in flat]
 
     order = (1, 3, 4, 5, 0, 2)
-    early, early_widths = inner_stages(order[:4], True)
-    late, late_widths = inner_stages(order[4:], False)
-    summed = reduce_stage(jnp.concatenate([early, late], axis=-1), 0)
+    early, early_widths = pair_stage(order[:4])
+    late, late_widths = pair_stage(order[4:])
+    summed = jnp.expand_dims(jnp.concatenate([early, late], axis=-1), len(DP))
+    for position in reversed(range(len(DP) - 1)):
+        summed = lax.all_to_all(
+            summed.astype(jnp.bfloat16), DP[position], split_axis=1 + position,
+            concat_axis=1 + position, tiled=True,
+        ).astype(jnp.float32).sum(axis=1 + position, keepdims=True)
     summed = summed.reshape(summed.shape[0], summed.shape[-1])
     outs = [None] * len(terms)
     start = 0

time: 217 us -> 215 us (level); the launches traced: 215 us -> 211 us
  local copies, waits for them, and re-layouts: 37.5 us -> 69.8 us
  starting transfers between devices: 21.7 us -> 49.3 us
  waiting for transfers between devices: 59.8 us -> 33.8 us
  blocking collectives: 50.5 us -> 26.1 us
  between operations: 14.5 us -> 1.47 us
    reduce_scatter x2 -> x0, waiting for transfers between devices: 27.4 us -> none  [reduce_stage(): lax.psum_scatter(wire, DP[position], scatter_dimension=1 + position, tile...]
    all_to_all x3 -> x1, blocking collectives: 50.5 us -> 26.1 us  [shards(): lax.all_to_all(summed.astype(jnp.bfloat16), DP[position], split_axis=1 +...]
    ppermute x0 -> x2, starting transfers between devices: none -> 20.6 us  [pair_stage(): lax.ppermute(other, DP[-1], [(0, 1), (1, 0)])]
    dynamic_slice x0 -> x4, local copies, waits for them, and re-layouts: none -> 19 us  [the longest x2 13.5 us: pair_stage(): own = lax.dynamic_index_in_dim(summed, me, axis=len(DP), keepdims=False)]
    all_to_all x1 -> x2, starting transfers between devices: 5.32 us -> 12.6 us  [the longest x1 7.07 us: shards(): lax.all_to_all(summed.astype(jnp.bfloat16), DP[position], split_axis=1 +...]
    unnamed x42 -> x50, local copies, waits for them, and re-layouts: 12.9 us -> 18.6 us
    all_to_all x1, waiting for transfers between devices: 23.5 us -> 18.1 us  [shards(): lax.all_to_all(jnp.stack([gate_mid, up_mid, back_mid]), 'mp', split_axis=...]
    all_to_all x1, waiting for transfers between devices: 0.01 us -> 3.65 us  [shards(): lax.all_to_all(down_mid, 'mp', split_axis=0, concat_axis=1, tiled=True)]
  transfers between devices with their start and end apart: 5 -> 6, of which waited for: 3 -> 4; matrix products, arithmetic and copies ran while one was open for 14% -> 24% of each run, Pallas kernels for 0% -> 0%
where the time goes in v11:
time: 215 us; the launch traced here: 211 us
  local copies, waits for them, and re-layouts  69.8 us (32%)
  starting transfers between devices  49.3 us (23%)
  waiting for transfers between devices  33.8 us (16%)
  blocking collectives  26.1 us (12%)
  matrix products  20.8 us (10%)
  other arithmetic  9.58 us (4%)
    all_to_all x1, blocking collectives, shards(): lax.all_to_all(summed.astype(jnp.bfloat16), DP[position], split_axis=1 +...  26.1 us
    ppermute x2, starting transfers between devices, pair_stage(): lax.ppermute(other, DP[-1], [(0, 1), (1, 0)])  20.6 us
    unnamed x50, local copies, waits for them, and re-layouts  18.6 us
    all_to_all x1, waiting for transfers between devices, shards(): lax.all_to_all(jnp.stack([gate_mid, up_mid, back_mid]), 'mp', split_axis=...  18.1 us
    concatenate x8, local copies, waits for them, and re-layouts, pair_stage(): stacked = jnp.concatenate(flat, axis=2)  15.8 us
    dynamic_slice x2, local copies, waits for them, and re-layouts, pair_stage(): own = lax.dynamic_index_in_dim(summed, me, axis=len(DP), keepdims=False)  13.5 us
    all_to_all x1, starting transfers between devices, shards(): lax.all_to_all(jnp.stack([gate_mid, up_mid, back_mid]), 'mp', split_axis=...  12 us
    all_to_all x1, waiting for transfers between devices, shards(): lax.all_to_all(summed.astype(jnp.bfloat16), DP[position], split_axis=1 +...  10.6 us
  transfers between devices with their start and end apart: 6, of which 4 were waited for; matrix products, arithmetic and copies ran while one was open for 24% of the time, Pallas kernels for 0%

profile of v11, /device:TPU:1, one launch (start us, length us, event | category | flops | bytes accessed | tf_op | source)
XLA Modules:
  0.0 210.8 jit_solution(7545958195345375901)
XLA Ops:
  6.6 12.0 %all-to-all-start = ((bf16[3,64,16,256]{3,2,0,1:T(8,128)(2,1)}), bf16[3,64,16,256]{3,2,0,1:T(8,128)(2,1)S(1)}, u32[]{:S(2)}, u32[]{:S(2)}) async-start(bf16[3,64,16,256]{3,2,0,1:T(8,128)(2,1)} %pad_maximum_fusion.1), calls=%async_computation | async-start | bytes 3145728 | tf_op jit(solution)/shard_map/all_to_all | solution.py:38
  18.6 2.7 %copy.137 = bf16[8,128,448]{2,0,1:T(8,128)(2,1)} copy(bf16[8,128,448]{1,2,0:T(8,128)(2,1)} %param.13) | data formatting | bytes 1835008 | tf_op args[5]
  21.3 1.8 copy.135
  23.1 2.7 %copy.144 = bf16[8,448,128]{1,0,2:T(8,128)(2,1)} copy(bf16[8,448,128]{2,1,0:T(8,128)(2,1)} %param.14) | data formatting | bytes 1835008 | tf_op args[6]
  25.9 18.1 %all-to-all-done = bf16[3,64,16,256]{3,2,0,1:T(8,128)(2,1)S(1)} async-done(((bf16[3,64,16,256]{3,2,0,1:T(8,128)(2,1)}), bf16[3,64,16,256]{3,2,0,1:T(8,128)(2,1)S(1)}, u32[]{:S(2)}, u32[]{:S(2)}) %all-to-all-start) | async-done | bytes 1572896 | tf_op jit(solution)/shard_map/all_to_all | solution.py:38
  47.7 3.2 %fusion.7 = (bf16[8,448,256]{2,1,0:T(8,128)(2,1)}, bf16[8,448,256]{2,1,0:T(8,128)(2,1)S(1)}, bf16[8,448,256]{2,1,0:T(8,128)(2,1)S(1)}) fusion(f32[8,256,448]{1,2,0:T(8,128)S(1)} %fusion.52, f32[8,256,448]{1,2,0:T(8,128)S(1)} %fusion.51, bf16[8,128,448]{1,2,0:T(8,128)(2,1)S(1)} %copy-done.18, bf16[8,128,256]{2,1,0:T(8,128)(2,1)S(1)} %bitcast.196), kind=kOutput, calls=%fused_computation.12 | convolution fusion | flops 248643584 | bytes 14286848 | tf_op jit(solution)/shard_map/jct,jco->jot/dot_general | solution.py:29
  54.0 2.1 fusion.48
  57.9 3.9 %concatenate.35 = f32[8,4,4,2,1792]{4,3,2,1,0:T(2,128)} reshape(f32[8,128,448]{2,1,0:T(8,128)} %fusion.48) | data formatting | bytes 3670016 | tf_op jit(solution)/shard_map/concatenate | solution.py:90
  61.8 2.9 %concatenate.36 = f32[8,4,4,2,1792]{4,3,2,1,0:T(2,128)} reshape(f32[8,128,448]{2,1,0:T(8,128)S(1)} %fusion.49) | data formatting | bytes 3670016 | tf_op jit(solution)/shard_map/concatenate | solution.py:90
  64.7 3.4 %fusion.50 = f32[8,448,128]{2,1,0:T(8,128)} fusion(bf16[8,448,256]{2,1,0:T(8,128)(2,1)} %get-tuple-element.42, bf16[8,128,256]{2,1,0:T(8,128)(2,1)S(1)} %bitcast.191), kind=kOutput, calls=%fused_computation.82 | convolution fusion | flops 234881024 | bytes 4194304 | tf_op jit(solution)/shard_map/jot,jqt->joq/dot_general | solution.py:54
  68.1 2.4 %concatenate.37 = f32[8,4,4,2,1792]{4,3,2,1,0:T(2,128)S(1)} reshape(f32[8,448,128]{2,1,0:T(8,128)} %fusion.50) | data formatting | bytes 3670016 | tf_op jit(solution)/shard_map/concatenate | solution.py:90
  70.6 2.6 %fusion.23 = bf16[8,256,64,2]{1,2,3,0:T(8,128)(2,1)S(1)} fusion(bf16[8,448,256]{2,1,0:T(8,128)(2,1)} %get-tuple-element.42, bf16[8,448,64,2]{1,0,3,2:T(8,128)(2,1)} %bitcast.207), kind=kOutput, calls=%fused_computation.31 | convolution fusion | flops 235143168 | bytes 3276800 | tf_op jit(solution)/shard_map/jot,jokp->kjpt/dot_general | solution.py:48
  74.4 4.1 %all-to-all-start.2 = ((bf16[64,16,256]{2,1,0:T(8,128)(2,1)}), bf16[64,16,256]{2,1,0:T(8,128)(2,1)S(1)}, u32[]{:S(2)}, u32[]{:S(2)}) async-start(bf16[64,16,256]{2,1,0:T(8,128)(2,1)} %copy.146), calls=%async_computation.2 | async-start | bytes 1048576 | tf_op jit(solution)/shard_map/all_to_all | solution.py:50
  78.5 2.2 %pad_maximum_fusion.2 = bf16[2,64,16,256]{3,2,0,1:T(8,128)(2,1)} fusion(bf16[1,64,16,256]{3,2,0,1:T(8,128)(2,1)S(1)} %copy-done.11, bf16[1,64,16,256]{3,2,0,1:T(8,128)(2,1)} %copy.139), kind=kLoop, calls=%fused_computation.38 | loop fusion | flops 524288 | bytes 2097152 | tf_op jit(solution)/shard_map/stack | solution.py:71
  80.7 1.4 constant_dynamic-update-slice_fusion.3
  84.3 1.5 constant_dynamic-update-slice_fusion.1
  85.8 3.7 %all-to-all-done.2 = bf16[64,16,256]{2,1,0:T(8,128)(2,1)S(1)} async-done(((bf16[64,16,256]{2,1,0:T(8,128)(2,1)}), bf16[64,16,256]{2,1,0:T(8,128)(2,1)S(1)}, u32[]{:S(2)}, u32[]{:S(2)}) %all-to-all-start.2) | async-done | bytes 524320 | tf_op jit(solution)/shard_map/all_to_all | solution.py:50
  89.5 5.5 %all-to-all-start.1 = ((bf16[2,64,16,256]{3,2,0,1:T(8,128)(2,1)}), bf16[2,64,16,256]{3,2,0,1:T(8,128)(2,1)}, u32[]{:S(2)}, u32[]{:S(2)}) async-start(bf16[2,64,16,256]{3,2,0,1:T(8,128)(2,1)} %pad_maximum_fusion.2), calls=%async_computation.1 | async-start | bytes 2097152 | tf_op jit(solution)/shard_map/all_to_all | solution.py:70
  96.6 12.4 %constant_dynamic-slice_fusion.3 = (f32[8,4,4,1,5888]{4,3,2,1,0:T(1,128)S(1)}, f32[8,4,4,1,5888]{4,3,2,1,0:T(1,128)}) fusion(f32[8,4,4,2,5888]{4,3,2,1,0:T(2,128)} %constant_dynamic-update-slice_fusion, s32[]{:T(128)S(6)} %select_n.10, s32[]{:T(128)S(6)} %select_n.11), kind=kLoop, calls=%fused_computation.77 | loop fusion | bytes 12058632 | tf_op jit(solution)/shard_map/jit(dynamic_index_in_dim)/dynamic_slice | solution.py:92
  109.0 5.2 %copy.218 = f32[8,4,4,1,5888]{4,0,3,2,1:T(8,128)} copy(f32[8,4,4,1,5888]{4,3,2,1,0:T(1,128)} %get-tuple-element.46) | data formatting | bytes 6029312 | tf_op jit(solution)/shard_map/jit(dynamic_index_in_dim)/dynamic_slice | solution.py:93
  114.2 15.3 %collective-permute-start = (f32[8,4,4,5888]{3,0,2,1:T(8,128)}, f32[8,4,4,5888]{3,0,2,1:T(8,128)}, u32[]{:S(2)}, u32[]{:S(2)}) collective-permute-start(f32[8,4,4,5888]{3,0,2,1:T(8,128)} %bitcast.175), channel_id=1, source_target_pairs={{0,8},{8,0},{1,9},{9,1},{2,10},{10,2},{3,11},{11,3},{4,12},{12,4},... | collective-permute-start | bytes 9043976 | tf_op jit(solution)/shard_map/ppermute | solution.py:94
  133.6 2.0 copy.152
  135.6 2.1 concatenate.41
  137.7 2.2 %convolution_bitcast_fusion = f32[8,128,128]{1,2,0:T(8,128)} fusion(bf16[8,128,256]{2,1,0:T(8,128)(2,1)} %bitcast.188, bf16[256,1024]{1,0:T(8,128)(2,1)S(1)} %copy-done.2), kind=kOutput, calls=%fused_computation.36 | convolution fusion | flops 67108864 | bytes 1572864 | tf_op jit(solution)/shard_map/tki,kot->kio/dot_general | solution.py:82
  139.9 2.1 copy.154
  142.0 2.1 %concatenate.42 = f32[8,4,4,2,512]{4,3,2,1,0:T(2,128)} reshape(f32[8,128,128]{2,1,0:T(8,128)} %copy.154) | data formatting | bytes 1048576 | tf_op jit(solution)/shard_map/concatenate | solution.py:90
  146.7 5.4 %collective-permute-start.1 = (f32[8,4,4,1024]{3,0,2,1:T(8,128)S(1)}, f32[8,4,4,1024]{3,0,2,1:T(8,128)S(1)}, u32[]{:S(2)}, u32[]{:S(2)}) collective-permute-start(f32[8,4,4,1024]{3,0,2,1:T(8,128)S(1)} %bitcast.209), channel_id=1, source_target_pairs={{0,8},{8,0},{1,9},{9,1},{2,10},{10,2},{3,11},{11,3},{4,12},{12,4},... | collective-permute-start | bytes 1572872 | tf_op jit(solution)/shard_map/ppermute | solution.py:94
  152.0 1.5 collective-permute-done.1
  153.9 3.5 %fusion.16 = bf16[8,4,4,1,5888]{4,0,2,1,3:T(8,128)(2,1)S(1)} fusion(f32[8,4,4,5888]{3,0,2,1:T(8,128)} %collective-permute-done, f32[8,4,4,1,5888]{4,3,2,1,0:T(1,128)S(1)} %get-tuple-element.45), kind=kLoop, calls=%fused_computation.27 | loop fusion | flops 1507328 | bytes 7536640 | tf_op jit(solution)/shard_map/concatenate | solution.py:99
  158.9 26.1 %all_to_all.58 = bf16[8,4,4,1,6912]{4,1,0,3,2:T(4,128)(2,1)S(1)} all-to-all(bf16[8,4,4,1,6912]{4,1,0,3,2:T(4,128)(2,1)S(1)} %copy.157), channel_id=1, replica_groups=mesh['dz'=4,'dx'=4,'dc'=2,'mp'=8] {'dx'}, dimensions={2} | all-to-all | bytes 3538944 | tf_op jit(solution)/shard_map/all_to_all | solution.py:101
  187.1 7.1 %all-to-all-start.4 = ((bf16[8,4,1,1,6912]{4,0,3,2,1:T(8,128)(2,1)}), bf16[8,4,1,1,6912]{4,0,3,2,1:T(8,128)(2,1)S(1)}, u32[]{:S(2)}, u32[]{:S(2)}) async-start(bf16[8,4,1,1,6912]{4,0,3,2,1:T(8,128)(2,1)} %copy.158), calls=%async_computation.4 | async-start | bytes 884736 | tf_op jit(solution)/shard_map/all_to_all | solution.py:101
  195.8 10.6 %all-to-all-done.4 = bf16[8,4,1,1,6912]{4,0,3,2,1:T(8,128)(2,1)S(1)} async-done(((bf16[8,4,1,1,6912]{4,0,3,2,1:T(8,128)(2,1)}), bf16[8,4,1,1,6912]{4,0,3,2,1:T(8,128)(2,1)S(1)}, u32[]{:S(2)}, u32[]{:S(2)}) %all-to-all-start.4) | async-done | bytes 442400 | tf_op jit(solution)/shard_map/all_to_all | solution.py:101
  (89 shorter events, 35.5 us)
Async XLA Ops:
  0.6 2.8 %copy-start.2 = (bf16[256,1024]{1,0:T(8,128)(2,1)S(1)}, bf16[256,1024]{1,0:T(8,128)(2,1)}, u32[]{:S(2)}) copy-start(bf16[256,1024]{1,0:T(8,128)(2,1)} %param.8) | copy-start | bytes 1572868
  0.6 2.9 %copy-start.14 = (bf16[8,128,128]{2,1,0:T(8,128)(2,1)S(1)}, bf16[8,128,128]{2,1,0:T(8,128)(2,1)}, u32[]{:S(2)}) copy-start(bf16[8,128,128]{2,1,0:T(8,128)(2,1)} %param.12) | copy-start | bytes 786436
  3.4 1.0 copy-start.12
  6.6 14.7 %copy-start.6 = (bf16[8,128,448]{1,2,0:T(8,128)(2,1)S(1)}, bf16[8,128,448]{1,2,0:T(8,128)(2,1)}, u32[]{:S(2)}) copy-start(bf16[8,128,448]{1,2,0:T(8,128)(2,1)} %param.11) | copy-start | bytes 2752516
  6.6 37.3 %all-to-all-start = ((bf16[3,64,16,256]{3,2,0,1:T(8,128)(2,1)}), bf16[3,64,16,256]{3,2,0,1:T(8,128)(2,1)S(1)}, u32[]{:S(2)}, u32[]{:S(2)}) async-start(bf16[3,64,16,256]{3,2,0,1:T(8,128)(2,1)} %pad_maximum_fusion.1), calls=%async_computation | async-start | bytes 3145728 | tf_op jit(solution)/shard_map/all_to_all | solution.py:38
  44.1 1.2 copy-start.7
  45.3 1.2 copy-start.8
  46.5 1.2 copy-start.18
  50.9 1.2 copy-start.17
  54.0 2.1 copy-start.16
  70.6 7.9 %copy-start.11 = (bf16[1,64,16,256]{3,2,0,1:T(8,128)(2,1)S(1)}, bf16[1,64,16,256]{3,2,0,1:T(8,128)(2,1)}, u32[]{:S(2)}) copy-start(bf16[1,64,16,256]{3,2,0,1:T(8,128)(2,1)} %copy.140) | copy-start | bytes 1572868
  74.4 15.1 %all-to-all-start.2 = ((bf16[64,16,256]{2,1,0:T(8,128)(2,1)}), bf16[64,16,256]{2,1,0:T(8,128)(2,1)S(1)}, u32[]{:S(2)}, u32[]{:S(2)}) async-start(bf16[64,16,256]{2,1,0:T(8,128)(2,1)} %copy.146), calls=%async_computation.2 | async-start | bytes 1048576 | tf_op jit(solution)/shard_map/all_to_all | solution.py:50
  78.5 2.2 %copy-start = (f32[8,4,4,2,1792]{4,3,2,1,0:T(2,128)S(1)}, f32[8,4,4,2,1792]{4,3,2,1,0:T(2,128)}, u32[]{:S(2)}) copy-start(f32[8,4,4,2,1792]{4,3,2,1,0:T(2,128)} %concatenate.35) | copy-start | bytes 5505028
  80.7 2.2 %copy-start.1 = (f32[8,4,4,2,1792]{4,3,2,1,0:T(2,128)S(1)}, f32[8,4,4,2,1792]{4,3,2,1,0:T(2,128)}, u32[]{:S(2)}) copy-start(f32[8,4,4,2,1792]{4,3,2,1,0:T(2,128)} %concatenate.36) | copy-start | bytes 5505028
  85.8 9.2 %copy-start.9 = (bf16[256,1024]{1,0:T(8,128)(2,1)S(1)}, bf16[256,1024]{1,0:T(8,128)(2,1)}, u32[]{:S(2)}) copy-start(bf16[256,1024]{1,0:T(8,128)(2,1)} %param.9) | copy-start | bytes 1572868
  89.5 39.9 %all-to-all-start.1 = ((bf16[2,64,16,256]{3,2,0,1:T(8,128)(2,1)}), bf16[2,64,16,256]{3,2,0,1:T(8,128)(2,1)}, u32[]{:S(2)}, u32[]{:S(2)}) async-start(bf16[2,64,16,256]{3,2,0,1:T(8,128)(2,1)} %pad_maximum_fusion.2), calls=%async_computation.1 | async-start | bytes 2097152 | tf_op jit(solution)/shard_map/all_to_all | solution.py:70
  114.2 39.7 %collective-permute-start = (f32[8,4,4,5888]{3,0,2,1:T(8,128)}, f32[8,4,4,5888]{3,0,2,1:T(8,128)}, u32[]{:S(2)}, u32[]{:S(2)}) collective-permute-start(f32[8,4,4,5888]{3,0,2,1:T(8,128)} %bitcast.175), channel_id=1, source_target_pairs={{0,8},{8,0},{1,9},{9,1},{2,10},{10,2},{3,11},{11,3},{4,12},{12,4},... | collective-permute-start | bytes 9043976 | tf_op jit(solution)/shard_map/ppermute | solution.py:94
  131.7 0.8 copy-start.3
  139.9 4.2 %copy-start.10 = (f32[8,4,4,2,512]{4,3,2,1,0:T(2,128)S(1)}, f32[8,4,4,2,512]{4,3,2,1,0:T(2,128)}, u32[]{:S(2)}) copy-start(f32[8,4,4,2,512]{4,3,2,1,0:T(2,128)} %concatenate.41) | copy-start | bytes 1572868
  146.7 6.9 %collective-permute-start.1 = (f32[8,4,4,1024]{3,0,2,1:T(8,128)S(1)}, f32[8,4,4,1024]{3,0,2,1:T(8,128)S(1)}, u32[]{:S(2)}, u32[]{:S(2)}) collective-permute-start(f32[8,4,4,1024]{3,0,2,1:T(8,128)S(1)} %bitcast.209), channel_id=1, source_target_pairs={{0,8},{8,0},{1,9},{9,1},{2,10},{10,2},{3,11},{11,3},{4,12},{12,4},... | collective-permute-start | bytes 1572872 | tf_op jit(solution)/shard_map/ppermute | solution.py:94
  185.0 9.2 %copy-start.4 = (bf16[1,8,8,16,256]{4,3,2,1,0:T(8,128)(2,1)S(1)}, bf16[1,8,8,16,256]{4,3,2,1,0:T(8,128)(2,1)}, u32[]{:S(2)}) copy-start(bf16[1,8,8,16,256]{4,3,2,1,0:T(8,128)(2,1)} %copy-done.3) | copy-start | bytes 1572868
  185.0 9.2 %copy-start.13 = (bf16[8,128,128]{2,1,0:T(8,128)(2,1)S(1)}, bf16[8,128,128]{2,1,0:T(8,128)(2,1)}, u32[]{:S(2)}) copy-start(bf16[8,128,128]{2,1,0:T(8,128)(2,1)} %param.10) | copy-start | bytes 786436
  186.3 8.2 %copy-start.5 = (bf16[1,8,8,16,256]{4,3,2,1,0:T(8,128)(2,1)S(1)}, bf16[1,8,8,16,256]{4,3,2,1,0:T(8,128)(2,1)}, u32[]{:S(2)}) copy-start(bf16[1,8,8,16,256]{4,3,2,1,0:T(8,128)(2,1)} %get-tuple-element.52) | copy-start | bytes 1572868
  186.3 8.2 %copy-start.15 = (bf16[8,128,128]{2,1,0:T(8,128)(2,1)S(1)}, bf16[8,128,128]{2,1,0:T(8,128)(2,1)}, u32[]{:S(2)}) copy-start(bf16[8,128,128]{2,1,0:T(8,128)(2,1)} %param.12) | copy-start | bytes 786436
  187.1 19.2 %all-to-all-start.4 = ((bf16[8,4,1,1,6912]{4,0,3,2,1:T(8,128)(2,1)}), bf16[8,4,1,1,6912]{4,0,3,2,1:T(8,128)(2,1)S(1)}, u32[]{:S(2)}, u32[]{:S(2)}) async-start(bf16[8,4,1,1,6912]{4,0,3,2,1:T(8,128)(2,1)} %copy.158), calls=%async_computation.4 | async-start | bytes 884736 | tf_op jit(solution)/shard_map/all_to_all | solution.py:101

commit v12 on v10

--- a/solution.py
+++ b/solution.py
@@ -90,9 +90,12 @@
     for position in reversed(range(len(DP))):
         if position == len(DP) - 1 and sizes[position] == 2:
             me = lax.axis_index(DP[position])
-            own = lax.dynamic_index_in_dim(summed, me, axis=1 + position)
-            other = lax.dynamic_index_in_dim(summed, 1 - me, axis=1 + position)
-            summed = own + lax.ppermute(other, DP[position], [(0, 1), (1, 0)])
+            major = jnp.moveaxis(summed, 1 + position, 0)
+            own = lax.dynamic_index_in_dim(major, me, axis=0, keepdims=False)
+            other = lax.dynamic_index_in_dim(major, 1 - me, axis=0, keepdims=False)
+            summed = jnp.expand_dims(
+                own + lax.ppermute(other, DP[position], [(0, 1), (1, 0)]), 1 + position
+            )
             continue
         wire = summed if position == len(DP) - 1 else summed.astype(jnp.bfloat16)
         summed = lax.all_to_all(

time: 191 us -> 194 us (1.016)
  local copies, waits for them, and re-layouts: 44.8 us -> 49.8 us
  starting transfers between devices: 49.2 us -> 51.2 us
    another operation x0 -> x2, local copies, waits for them, and re-layouts: none -> 9.6 us
    all_to_all x1, starting transfers between devices: 3.47 us -> 8.61 us  [shards(): lax.all_to_all(wire, DP[position], split_axis=1 + position, concat_axis=1...]
    ppermute x1, starting transfers between devices: 23 us -> 19.1 us  [shards(): lax.ppermute(other, DP[position], [(0, 1), (1, 0)])]
    dynamic_slice x1 -> x0, local copies, waits for them, and re-layouts: 2.34 us -> none  [shards(): other = lax.dynamic_index_in_dim(summed, 1 - me, axis=1 + position)]
    unnamed x57 -> x53, local copies, waits for them, and re-layouts: 19.8 us -> 17.5 us
    convert_element_type x1 -> x2, local copies, waits for them, and re-layouts: 0.12 us -> 2.19 us  [shards(): wire = summed if position == len(DP) - 1 else summed.astype(jnp.bfloat16)]
where the time goes in v12:
time: 194 us
  starting transfers between devices  51.2 us (26%)
  local copies, waits for them, and re-layouts  49.8 us (26%)
  waiting for transfers between devices  41.2 us (21%)
  blocking collectives  25.1 us (13%)
  matrix products  18.9 us (10%)
  other arithmetic  6.39 us (3%)
    all_to_all x1, blocking collectives, shards(): lax.all_to_all(wire, DP[position], split_axis=1 + position, concat_axis=1...  25.1 us
    all_to_all x1, waiting for transfers between devices, shards(): lax.all_to_all(jnp.stack([gate_mid, up_mid, back_mid]), 'mp', split_axis=...  23.5 us
    ppermute x1, starting transfers between devices, shards(): lax.ppermute(other, DP[position], [(0, 1), (1, 0)])  19.1 us
    unnamed x53, local copies, waits for them, and re-layouts  17.5 us
    concatenate x7, local copies, waits for them, and re-layouts, shards(): stacked = jnp.concatenate(flat, axis=2)  11.6 us
    all_to_all x1, starting transfers between devices, shards(): lax.all_to_all(jnp.stack([gate_mid, up_mid, back_mid]), 'mp', split_axis=...  11.6 us
    all_to_all x1, waiting for transfers between devices, shards(): lax.all_to_all(wire, DP[position], split_axis=1 + position, concat_axis=1...  9.69 us
    another operation x2, local copies, waits for them, and re-layouts  9.6 us
  transfers between devices with their start and end apart: 5, of which 5 were waited for; matrix products, arithmetic and copies ran while one was open for 15% of the time, Pallas kernels for 0%

profile of v12, /device:TPU:1, one launch (start us, length us, event | category | flops | bytes accessed | tf_op | source)
XLA Modules:
  0.0 193.7 jit_solution(17220350724068070132)
XLA Ops:
  6.2 1.4 pad_maximum_fusion
  7.5 11.6 %all-to-all-start = ((bf16[3,64,16,256]{3,2,0,1:T(8,128)(2,1)}), bf16[3,64,16,256]{3,2,0,1:T(8,128)(2,1)S(1)}, u32[]{:S(2)}, u32[]{:S(2)}) async-start(bf16[3,64,16,256]{3,2,0,1:T(8,128)(2,1)} %pad_maximum_fusion), calls=%async_computation | async-start | bytes 3145728 | tf_op jit(solution)/shard_map/all_to_all | solution.py:38
  19.2 1.8 copy.146
  21.0 23.5 %all-to-all-done = bf16[3,64,16,256]{3,2,0,1:T(8,128)(2,1)S(1)} async-done(((bf16[3,64,16,256]{3,2,0,1:T(8,128)(2,1)}), bf16[3,64,16,256]{3,2,0,1:T(8,128)(2,1)S(1)}, u32[]{:S(2)}, u32[]{:S(2)}) %all-to-all-start) | async-done | bytes 1572896 | tf_op jit(solution)/shard_map/all_to_all | solution.py:38
  47.5 3.5 %fusion.7 = (bf16[8,448,256]{2,1,0:T(8,128)(2,1)S(1)}, bf16[8,448,256]{2,1,0:T(8,128)(2,1)}, bf16[8,448,256]{2,1,0:T(8,128)(2,1)}) fusion(f32[8,256,448]{1,2,0:T(8,128)S(1)} %fusion.50, f32[8,256,448]{1,2,0:T(8,128)S(1)} %fusion.49, bf16[8,128,448]{1,2,0:T(8,128)(2,1)S(1)} %copy-done.18, bf16[8,128,256]{2,1,0:T(8,128)(2,1)S(1)} %bitcast.196), kind=kOutput, calls=%fused_computation.12 | convolution fusion | flops 248643584 | bytes 14286848 | tf_op jit(solution)/shard_map/jct,jco->jot/dot_general | solution.py:29
  51.0 1.3 copy-done.14
  54.2 4.1 %all-to-all-start.2 = ((bf16[64,16,256]{2,1,0:T(8,128)(2,1)}), bf16[64,16,256]{2,1,0:T(8,128)(2,1)S(1)}, u32[]{:S(2)}, u32[]{:S(2)}) async-start(bf16[64,16,256]{2,1,0:T(8,128)(2,1)} %copy.148), calls=%async_computation.2 | async-start | bytes 1048576 | tf_op jit(solution)/shard_map/all_to_all | solution.py:50
  58.3 1.9 copy.133
  60.2 2.7 %copy.135 = bf16[8,128,448]{2,0,1:T(8,128)(2,1)} copy(bf16[8,128,448]{1,2,0:T(8,128)(2,1)} %param.13) | data formatting | bytes 1835008 | tf_op args[5]
  62.8 2.7 %fusion.17 = bf16[8,256,64,2]{1,2,3,0:T(8,128)(2,1)S(1)} fusion(bf16[8,448,256]{2,1,0:T(8,128)(2,1)} %get-tuple-element.43, bf16[8,64,2,448]{3,0,2,1:T(8,128)(2,1)} %bitcast.209), kind=kOutput, calls=%fused_computation.28 | convolution fusion | flops 235143168 | bytes 3276800 | tf_op jit(solution)/shard_map/jot,jkpo->kjpt/dot_general | solution.py:67
  68.0 1.3 all-to-all-done.2
  69.3 7.7 %all-to-all-start.1 = ((bf16[2,64,16,256]{3,2,0,1:T(8,128)(2,1)}), bf16[2,64,16,256]{3,2,0,1:T(8,128)(2,1)}, u32[]{:S(2)}, u32[]{:S(2)}) async-start(bf16[2,64,16,256]{3,2,0,1:T(8,128)(2,1)} %pad_maximum_fusion.1), calls=%async_computation.1 | async-start | bytes 2097152 | tf_op jit(solution)/shard_map/all_to_all | solution.py:70
  77.1 2.1 %fusion.48 = f32[8,448,128]{2,1,0:T(8,128)S(1)} fusion(bf16[8,448,256]{2,1,0:T(8,128)(2,1)} %copy-done.14, bf16[8,128,256]{2,1,0:T(8,128)(2,1)S(1)} %bitcast.191), kind=kOutput, calls=%fused_computation.75 | convolution fusion | flops 234881024 | bytes 4194304 | tf_op jit(solution)/shard_map/jot,jqt->joq/dot_general | solution.py:54
  79.2 2.2 %concatenate.20 = f32[8,4,4,2,1792]{4,3,2,1,0:T(2,128)} reshape(f32[8,448,128]{2,1,0:T(8,128)S(1)} %fusion.48) | data formatting | bytes 3670016 | tf_op jit(solution)/shard_map/concatenate | solution.py:87
  81.4 2.3 %fusion.46 = f32[8,128,448]{2,1,0:T(8,128)S(1)} fusion(bf16[8,128,256]{2,1,0:T(8,128)(2,1)S(1)} %bitcast.183, bf16[8,448,256]{2,1,0:T(8,128)(2,1)} %get-tuple-element.43), kind=kOutput, calls=%fused_computation.73 | convolution fusion | flops 234881024 | bytes 4194304 | tf_op jit(solution)/shard_map/jct,jot->jco/dot_general | solution.py:60
  83.7 2.9 %concatenate.17 = f32[8,4,4,2,1792]{4,3,2,1,0:T(2,128)} reshape(f32[8,128,448]{2,1,0:T(8,128)S(1)} %fusion.46) | data formatting | bytes 3670016 | tf_op jit(solution)/shard_map/concatenate | solution.py:87
  86.6 2.2 %fusion.47 = f32[8,128,448]{2,1,0:T(8,128)S(1)} fusion(bf16[8,128,256]{2,1,0:T(8,128)(2,1)S(1)} %bitcast.197, bf16[8,448,256]{2,1,0:T(8,128)(2,1)} %get-tuple-element.44), kind=kOutput, calls=%fused_computation.74 | convolution fusion | flops 234881024 | bytes 4194304 | tf_op jit(solution)/shard_map/jct,jot->jco/dot_general | solution.py:63
  88.8 2.9 %concatenate.19 = f32[8,4,4,2,1792]{4,3,2,1,0:T(2,128)} reshape(f32[8,128,448]{2,1,0:T(8,128)S(1)} %fusion.47) | data formatting | bytes 3670016 | tf_op jit(solution)/shard_map/concatenate | solution.py:87
  93.2 1.3 copy.212
  97.4 2.2 %concatenate.18 = f32[8,4,4,2,512]{4,3,2,1,0:T(2,128)} reshape(f32[8,128,128]{2,1,0:T(8,128)} %copy.144) | data formatting | bytes 1048576 | tf_op jit(solution)/shard_map/concatenate | solution.py:87
  100.8 2.0 %constant_dynamic-update-slice_fusion.4 = f32[8,4,4,2,6912]{4,3,2,1,0:T(2,128)S(1)} fusion(f32[8,4,4,2,6912]{4,3,2,1,0:T(2,128)S(1)} %constant_dynamic-update-slice_fusion.5, f32[8,4,4,2,1792]{4,3,2,1,0:T(2,128)} %concatenate.17), kind=kLoop, calls=%fused_computation.67 | loop fusion | bytes 3670016
  103.7 7.5 %constant_dynamic-slice_fusion.1 = (f32[8,4,4,1,6912]{4,3,2,1,0:T(1,128)S(1)}, f32[8,4,4,1,6912]{4,3,2,1,0:T(1,128)S(1)}) fusion(f32[8,4,4,2,6912]{4,3,2,1,0:T(2,128)S(1)} %constant_dynamic-update-slice_fusion, s32[]{:T(128)S(6)} %select_n.7, s32[]{:T(128)S(6)} %select_n.8), kind=kLoop, calls=%fused_computation.70 | loop fusion | bytes 14155784 | tf_op jit(solution)/shard_map/dynamic-slice
  111.2 2.1 %copy.210 = f32[8,4,4,1,6912]{4,0,3,2,1:T(8,128)S(1)} copy(f32[8,4,4,1,6912]{4,3,2,1,0:T(1,128)S(1)} %get-tuple-element.46) | data formatting | bytes 7077888 | tf_op jit(solution)/shard_map/dynamic-slice.1
  113.3 19.1 %collective-permute-start = (f32[8,4,4,6912]{3,0,2,1:T(8,128)S(1)}, f32[8,4,4,6912]{3,0,2,1:T(8,128)S(1)}, u32[]{:S(2)}, u32[]{:S(2)}) collective-permute-start(f32[8,4,4,6912]{3,0,2,1:T(8,128)S(1)} %bitcast.193), channel_id=1, source_target_pairs={{0,8},{8,0},{1,9},{9,1},{2,10},{10,2},{3,11},{11,3},{4,12},{12,4},... | collective-permute-start | bytes 10616840 | tf_op jit(solution)/shard_map/ppermute | solution.py:97
  132.4 5.8 %collective-permute-done = f32[8,4,4,6912]{3,0,2,1:T(8,128)S(1)} collective-permute-done((f32[8,4,4,6912]{3,0,2,1:T(8,128)S(1)}, f32[8,4,4,6912]{3,0,2,1:T(8,128)S(1)}, u32[]{:S(2)}, u32[]{:S(2)}) %collective-permute-start) | collective-permute-done | bytes 3538976 | tf_op jit(solution)/shard_map/ppermute | solution.py:97
  138.3 2.0 %fusion.16 = bf16[8,4,4,1,6912]{4,0,2,1,3:T(8,128)(2,1)S(1)} fusion(f32[8,4,4,6912]{3,0,2,1:T(8,128)S(1)} %collective-permute-done, f32[8,4,4,1,6912]{4,3,2,1,0:T(1,128)S(1)} %get-tuple-element.45), kind=kLoop, calls=%fused_computation.24 | loop fusion | flops 1769472 | bytes 8847360 | tf_op jit(solution)/shard_map/convert_element_type | solution.py:100
  140.3 1.4 copy.153
  141.7 25.1 %all_to_all.58 = bf16[8,4,4,1,6912]{4,1,0,3,2:T(4,128)(2,1)S(1)} all-to-all(bf16[8,4,4,1,6912]{4,1,0,3,2:T(4,128)(2,1)S(1)} %copy.153), channel_id=1, replica_groups=mesh['dz'=4,'dx'=4,'dc'=2,'mp'=8] {'dx'}, dimensions={2} | all-to-all | bytes 3538944 | tf_op jit(solution)/shard_map/all_to_all | solution.py:101
  166.8 1.2 reduce_sum.21
  168.9 8.6 %all-to-all-start.4 = ((bf16[8,4,1,1,6912]{4,0,3,2,1:T(8,128)(2,1)}), bf16[8,4,1,1,6912]{4,0,3,2,1:T(8,128)(2,1)S(1)}, u32[]{:S(2)}, u32[]{:S(2)}) async-start(bf16[8,4,1,1,6912]{4,0,3,2,1:T(8,128)(2,1)} %copy.154), calls=%async_computation.4 | async-start | bytes 884736 | tf_op jit(solution)/shard_map/all_to_all | solution.py:101
  177.5 1.2 fusion.51
  180.0 9.7 %all-to-all-done.4 = bf16[8,4,1,1,6912]{4,0,3,2,1:T(8,128)(2,1)S(1)} async-done(((bf16[8,4,1,1,6912]{4,0,3,2,1:T(8,128)(2,1)}), bf16[8,4,1,1,6912]{4,0,3,2,1:T(8,128)(2,1)S(1)}, u32[]{:S(2)}, u32[]{:S(2)}) %all-to-all-start.4) | async-done | bytes 442400 | tf_op jit(solution)/shard_map/all_to_all | solution.py:101
  (85 shorter events, 25.2 us)
Async XLA Ops:
  0.6 4.8 %copy-start.6 = (bf16[256,1024]{1,0:T(8,128)(2,1)S(1)}, bf16[256,1024]{1,0:T(8,128)(2,1)}, u32[]{:S(2)}) copy-start(bf16[256,1024]{1,0:T(8,128)(2,1)} %param.9) | copy-start | bytes 1572868
  3.0 2.6 %copy-start.19 = (bf16[8,128,128]{2,1,0:T(8,128)(2,1)S(1)}, bf16[8,128,128]{2,1,0:T(8,128)(2,1)}, u32[]{:S(2)}) copy-start(bf16[8,128,128]{2,1,0:T(8,128)(2,1)} %param.15) | copy-start | bytes 786436
  5.9 13.3 %copy-start.3 = (bf16[8,448,128]{2,1,0:T(8,128)(2,1)S(1)}, bf16[8,448,128]{2,1,0:T(8,128)(2,1)}, u32[]{:S(2)}) copy-start(bf16[8,448,128]{2,1,0:T(8,128)(2,1)} %param.14) | copy-start | bytes 2752516
  7.5 37.0 %all-to-all-start = ((bf16[3,64,16,256]{3,2,0,1:T(8,128)(2,1)}), bf16[3,64,16,256]{3,2,0,1:T(8,128)(2,1)S(1)}, u32[]{:S(2)}, u32[]{:S(2)}) async-start(bf16[3,64,16,256]{3,2,0,1:T(8,128)(2,1)} %pad_maximum_fusion), calls=%async_computation | async-start | bytes 3145728 | tf_op jit(solution)/shard_map/all_to_all | solution.py:38
  44.5 1.2 copy-start.4
  44.7 1.7 copy-start.5
  44.8 2.2 %copy-start.8 = (bf16[1,8,8,16,256]{4,3,2,1,0:T(8,128)(2,1)}, bf16[1,8,8,16,256]{4,3,2,1,0:T(8,128)(2,1)S(1)}, u32[]{:S(2)}) copy-start(bf16[1,8,8,16,256]{4,3,2,1,0:T(8,128)(2,1)S(1)} %get-tuple-element.47) | copy-start | bytes 1572868
  46.3 1.2 copy-start.18
  47.5 4.8 %copy-start.16 = (bf16[8,448,128]{1,0,2:T(8,128)(2,1)S(1)}, bf16[8,448,128]{1,0,2:T(8,128)(2,1)}, u32[]{:S(2)}) copy-start(bf16[8,448,128]{1,0,2:T(8,128)(2,1)} %copy.146) | copy-start | bytes 2752516
  51.0 1.3 copy-start.14
  54.2 15.1 %all-to-all-start.2 = ((bf16[64,16,256]{2,1,0:T(8,128)(2,1)}), bf16[64,16,256]{2,1,0:T(8,128)(2,1)S(1)}, u32[]{:S(2)}, u32[]{:S(2)}) async-start(bf16[64,16,256]{2,1,0:T(8,128)(2,1)} %copy.148), calls=%async_computation.2 | async-start | bytes 1048576 | tf_op jit(solution)/shard_map/all_to_all | solution.py:50
  62.8 3.0 %copy-start.13 = (bf16[8,448,256]{2,1,0:T(8,128)(2,1)S(1)}, bf16[8,448,256]{2,1,0:T(8,128)(2,1)}, u32[]{:S(2)}) copy-start(bf16[8,448,256]{2,1,0:T(8,128)(2,1)} %get-tuple-element.44) | copy-start | bytes 5505028
  62.8 3.0 %copy-start.17 = (bf16[8,128,448]{2,0,1:T(8,128)(2,1)S(1)}, bf16[8,128,448]{2,0,1:T(8,128)(2,1)}, u32[]{:S(2)}) copy-start(bf16[8,128,448]{2,0,1:T(8,128)(2,1)} %copy.135) | copy-start | bytes 2752516
  69.3 7.7 %copy-start.10 = (bf16[64,16,256]{2,1,0:T(8,128)(2,1)}, bf16[64,16,256]{2,1,0:T(8,128)(2,1)S(1)}, u32[]{:S(2)}) copy-start(bf16[64,16,256]{2,1,0:T(8,128)(2,1)S(1)} %all-to-all-done.2) | copy-start | bytes 1572868
  69.3 23.8 %all-to-all-start.1 = ((bf16[2,64,16,256]{3,2,0,1:T(8,128)(2,1)}), bf16[2,64,16,256]{3,2,0,1:T(8,128)(2,1)}, u32[]{:S(2)}, u32[]{:S(2)}) async-start(bf16[2,64,16,256]{3,2,0,1:T(8,128)(2,1)} %pad_maximum_fusion.1), calls=%async_computation.1 | async-start | bytes 2097152 | tf_op jit(solution)/shard_map/all_to_all | solution.py:70
  81.4 5.1 %copy-start.9 = (bf16[1,8,8,16,256]{4,3,2,1,0:T(8,128)(2,1)S(1)}, bf16[1,8,8,16,256]{4,3,2,1,0:T(8,128)(2,1)}, u32[]{:S(2)}) copy-start(bf16[1,8,8,16,256]{4,3,2,1,0:T(8,128)(2,1)} %copy-done.8) | copy-start | bytes 1572868
  88.8 2.9 %copy-start.11 = (bf16[64,16,256]{2,1,0:T(8,128)(2,1)S(1)}, bf16[64,16,256]{2,1,0:T(8,128)(2,1)}, u32[]{:S(2)}) copy-start(bf16[64,16,256]{2,1,0:T(8,128)(2,1)} %copy-done.10) | copy-start | bytes 1572868
  88.8 3.0 %copy-start.7 = (bf16[256,1024]{1,0:T(8,128)(2,1)S(1)}, bf16[256,1024]{1,0:T(8,128)(2,1)}, u32[]{:S(2)}) copy-start(bf16[256,1024]{1,0:T(8,128)(2,1)} %param.9) | copy-start | bytes 1572868
  91.7 2.8 %copy-start.2 = (bf16[256,1024]{1,0:T(8,128)(2,1)S(1)}, bf16[256,1024]{1,0:T(8,128)(2,1)}, u32[]{:S(2)}) copy-start(bf16[256,1024]{1,0:T(8,128)(2,1)} %param.8) | copy-start | bytes 1572868
  97.4 5.4 %copy-start.1 = (f32[8,4,4,2,1792]{4,3,2,1,0:T(2,128)S(1)}, f32[8,4,4,2,1792]{4,3,2,1,0:T(2,128)}, u32[]{:S(2)}) copy-start(f32[8,4,4,2,1792]{4,3,2,1,0:T(2,128)} %concatenate.19) | copy-start | bytes 5505028
  99.7 3.1 %copy-start.12 = (f32[8,4,4,2,512]{4,3,2,1,0:T(2,128)S(1)}, f32[8,4,4,2,512]{4,3,2,1,0:T(2,128)}, u32[]{:S(2)}) copy-start(f32[8,4,4,2,512]{4,3,2,1,0:T(2,128)} %concatenate.18) | copy-start | bytes 1572868
  100.8 2.4 %copy-start = (f32[8,4,4,2,1792]{4,3,2,1,0:T(2,128)S(1)}, f32[8,4,4,2,1792]{4,3,2,1,0:T(2,128)}, u32[]{:S(2)}) copy-start(f32[8,4,4,2,1792]{4,3,2,1,0:T(2,128)} %concatenate.20) | copy-start | bytes 5505028
  113.3 25.0 %collective-permute-start = (f32[8,4,4,6912]{3,0,2,1:T(8,128)S(1)}, f32[8,4,4,6912]{3,0,2,1:T(8,128)S(1)}, u32[]{:S(2)}, u32[]{:S(2)}) collective-permute-start(f32[8,4,4,6912]{3,0,2,1:T(8,128)S(1)} %bitcast.193), channel_id=1, source_target_pairs={{0,8},{8,0},{1,9},{9,1},{2,10},{10,2},{3,11},{11,3},{4,12},{12,4},... | collective-permute-start | bytes 10616840 | tf_op jit(solution)/shard_map/ppermute | solution.py:97
  168.0 10.7 %copy-start.15 = (bf16[8,128,128]{2,1,0:T(8,128)(2,1)S(1)}, bf16[8,128,128]{2,1,0:T(8,128)(2,1)}, u32[]{:S(2)}) copy-start(bf16[8,128,128]{2,1,0:T(8,128)(2,1)} %param.12) | copy-start | bytes 786436
  168.9 20.8 %all-to-all-start.4 = ((bf16[8,4,1,1,6912]{4,0,3,2,1:T(8,128)(2,1)}), bf16[8,4,1,1,6912]{4,0,3,2,1:T(8,128)(2,1)S(1)}, u32[]{:S(2)}, u32[]{:S(2)}) async-start(bf16[8,4,1,1,6912]{4,0,3,2,1:T(8,128)(2,1)} %copy.154), calls=%async_computation.4 | async-start | bytes 884736 | tf_op jit(solution)/shard_map/all_to_all | solution.py:101

commit v13 on v10

--- a/solution.py
+++ b/solution.py
@@ -90,8 +90,10 @@
     for position in reversed(range(len(DP))):
         if position == len(DP) - 1 and sizes[position] == 2:
             me = lax.axis_index(DP[position])
-            own = lax.dynamic_index_in_dim(summed, me, axis=1 + position)
-            other = lax.dynamic_index_in_dim(summed, 1 - me, axis=1 + position)
+            first = lax.index_in_dim(summed, 0, axis=1 + position)
+            second = lax.index_in_dim(summed, 1, axis=1 + position)
+            own = jnp.where(me == 0, first, second)
+            other = jnp.where(me == 0, second, first)
             summed = own + lax.ppermute(other, DP[position], [(0, 1), (1, 0)])
             continue
         wire = summed if position == len(DP) - 1 else summed.astype(jnp.bfloat16)

time: 191 us -> 185 us (0.969)
  local copies, waits for them, and re-layouts: 44.8 us -> 40.9 us
  other arithmetic: 7.7 us -> 5.12 us
    convert_element_type x1, other arithmetic: 3.39 us -> 0.47 us  [shards(): wire = summed if position == len(DP) - 1 else summed.astype(jnp.bfloat16)]
    dynamic_slice x1 -> x0, local copies, waits for them, and re-layouts: 2.34 us -> none  [shards(): other = lax.dynamic_index_in_dim(summed, 1 - me, axis=1 + position)]
    unnamed x57 -> x55, local copies, waits for them, and re-layouts: 19.8 us -> 18.2 us
where the time goes in v13:
time: 185 us; the launch traced here: 184 us
  starting transfers between devices  49.3 us (27%)
  waiting for transfers between devices  42.6 us (23%)
  local copies, waits for them, and re-layouts  40.9 us (22%)
  blocking collectives  26.1 us (14%)
  matrix products  18.7 us (10%)
  other arithmetic  5.12 us (3%)
    all_to_all x1, blocking collectives, shards(): lax.all_to_all(wire, DP[position], split_axis=1 + position, concat_axis=1...  26.1 us
    all_to_all x1, waiting for transfers between devices, shards(): lax.all_to_all(jnp.stack([gate_mid, up_mid, back_mid]), 'mp', split_axis=...  23.5 us
    ppermute x1, starting transfers between devices, shards(): summed = own + lax.ppermute(other, DP[position], [(0, 1), (1, 0)])  23 us
    unnamed x55, local copies, waits for them, and re-layouts  18.2 us
    concatenate x7, local copies, waits for them, and re-layouts, shards(): stacked = jnp.concatenate(flat, axis=2)  12.5 us
    all_to_all x1, starting transfers between devices, shards(): lax.all_to_all(jnp.stack([gate_mid, up_mid, back_mid]), 'mp', split_axis=...  11.8 us
    all_to_all x1, waiting for transfers between devices, shards(): lax.all_to_all(wire, DP[position], split_axis=1 + position, concat_axis=1...  10.6 us
    all_to_all x1, starting transfers between devices, shards(): lax.all_to_all(jnp.stack([narrow(gate_grad, gate_out), narrow(up_grad, up...  6.93 us
  transfers between devices with their start and end apart: 5, of which 5 were waited for; matrix products, arithmetic and copies ran while one was open for 15% of the time, Pallas kernels for 0%

profile of v13, /device:TPU:1, one launch (start us, length us, event | category | flops | bytes accessed | tf_op | source)
XLA Modules:
  0.0 183.7 jit_solution(8856865039467534076)
XLA Ops:
  0.6 1.1 copy.124
  1.8 1.1 copy.127
  2.9 1.1 copy.178
  6.1 1.4 pad_maximum_fusion
  7.4 11.8 %all-to-all-start = ((bf16[3,64,16,256]{3,2,0,1:T(8,128)(2,1)}), bf16[3,64,16,256]{3,2,0,1:T(8,128)(2,1)S(1)}, u32[]{:S(2)}, u32[]{:S(2)}) async-start(bf16[3,64,16,256]{3,2,0,1:T(8,128)(2,1)} %pad_maximum_fusion), calls=%async_computation | async-start | bytes 3145728 | tf_op jit(solution)/shard_map/all_to_all | solution.py:38
  19.2 1.8 %copy.149 = bf16[8,448,128]{1,0,2:T(8,128)(2,1)} copy(bf16[8,448,128]{2,1,0:T(8,128)(2,1)S(1)} %copy-done.4) | data formatting | bytes 1835008 | tf_op args[6]
  21.0 23.5 %all-to-all-done = bf16[3,64,16,256]{3,2,0,1:T(8,128)(2,1)S(1)} async-done(((bf16[3,64,16,256]{3,2,0,1:T(8,128)(2,1)}), bf16[3,64,16,256]{3,2,0,1:T(8,128)(2,1)S(1)}, u32[]{:S(2)}, u32[]{:S(2)}) %all-to-all-start) | async-done | bytes 1572896 | tf_op jit(solution)/shard_map/all_to_all | solution.py:38
  48.3 3.5 %fusion.7 = (bf16[8,448,256]{2,1,0:T(8,128)(2,1)S(1)}, bf16[8,448,256]{2,1,0:T(8,128)(2,1)}, bf16[8,448,256]{2,1,0:T(8,128)(2,1)}) fusion(f32[8,256,448]{1,2,0:T(8,128)S(1)} %fusion.48, f32[8,256,448]{1,2,0:T(8,128)S(1)} %fusion.47, bf16[8,128,448]{1,2,0:T(8,128)(2,1)S(1)} %copy-done.19, bf16[8,128,256]{2,1,0:T(8,128)(2,1)S(1)} %bitcast.184), kind=kOutput, calls=%fused_computation.12 | convolution fusion | flops 248643584 | bytes 14286848 | tf_op jit(solution)/shard_map/jct,jco->jot/dot_general | solution.py:29
  51.8 1.2 copy-done.15
  54.9 4.1 %all-to-all-start.2 = ((bf16[64,16,256]{2,1,0:T(8,128)(2,1)}), bf16[64,16,256]{2,1,0:T(8,128)(2,1)S(1)}, u32[]{:S(2)}, u32[]{:S(2)}) async-start(bf16[64,16,256]{2,1,0:T(8,128)(2,1)} %copy.151), calls=%async_computation.2 | async-start | bytes 1048576 | tf_op jit(solution)/shard_map/all_to_all | solution.py:50
  59.0 1.8 %copy.136 = bf16[8,128,448]{2,0,1:T(8,128)(2,1)} copy(bf16[8,128,448]{1,2,0:T(8,128)(2,1)S(1)} %copy-done.6) | data formatting | bytes 1835008 | tf_op args[3]
  60.9 1.9 %copy.138 = bf16[8,128,448]{2,0,1:T(8,128)(2,1)S(1)} copy(bf16[8,128,448]{1,2,0:T(8,128)(2,1)} %param.13) | data formatting | bytes 1835008 | tf_op args[5]
  62.8 2.7 %fusion.15 = bf16[8,256,64,2]{1,2,3,0:T(8,128)(2,1)S(1)} fusion(bf16[8,448,256]{2,1,0:T(8,128)(2,1)} %get-tuple-element.43, bf16[8,64,2,448]{3,0,2,1:T(8,128)(2,1)} %bitcast.196), kind=kOutput, calls=%fused_computation.29 | convolution fusion | flops 235143168 | bytes 3276800 | tf_op jit(solution)/shard_map/jot,jkpo->kjpt/dot_general | solution.py:67
  66.9 1.1 pad_maximum_fusion.1
  68.0 2.1 %all-to-all-done.2 = bf16[64,16,256]{2,1,0:T(8,128)(2,1)S(1)} async-done(((bf16[64,16,256]{2,1,0:T(8,128)(2,1)}), bf16[64,16,256]{2,1,0:T(8,128)(2,1)S(1)}, u32[]{:S(2)}, u32[]{:S(2)}) %all-to-all-start.2) | async-done | bytes 524320 | tf_op jit(solution)/shard_map/all_to_all | solution.py:50
  70.1 6.9 %all-to-all-start.1 = ((bf16[2,64,16,256]{3,2,0,1:T(8,128)(2,1)}), bf16[2,64,16,256]{3,2,0,1:T(8,128)(2,1)}, u32[]{:S(2)}, u32[]{:S(2)}) async-start(bf16[2,64,16,256]{3,2,0,1:T(8,128)(2,1)} %pad_maximum_fusion.1), calls=%async_computation.1 | async-start | bytes 2097152 | tf_op jit(solution)/shard_map/all_to_all | solution.py:70
  77.0 2.1 %fusion.46 = f32[8,448,128]{2,1,0:T(8,128)S(1)} fusion(bf16[8,448,256]{2,1,0:T(8,128)(2,1)} %copy-done.15, bf16[8,128,256]{2,1,0:T(8,128)(2,1)S(1)} %bitcast.180), kind=kOutput, calls=%fused_computation.71 | convolution fusion | flops 234881024 | bytes 4194304 | tf_op jit(solution)/shard_map/jot,jqt->joq/dot_general | solution.py:54
  79.2 2.2 %concatenate.20 = f32[8,4,4,2,1792]{4,3,2,1,0:T(2,128)} reshape(f32[8,448,128]{2,1,0:T(8,128)S(1)} %fusion.46) | data formatting | bytes 3670016 | tf_op jit(solution)/shard_map/concatenate | solution.py:87
  81.4 2.2 %fusion.44 = f32[8,128,448]{2,1,0:T(8,128)S(1)} fusion(bf16[8,128,256]{2,1,0:T(8,128)(2,1)S(1)} %bitcast.172, bf16[8,448,256]{2,1,0:T(8,128)(2,1)} %get-tuple-element.43), kind=kOutput, calls=%fused_computation.69 | convolution fusion | flops 234881024 | bytes 4194304 | tf_op jit(solution)/shard_map/jct,jot->jco/dot_general | solution.py:60
  83.6 2.9 %concatenate.17 = f32[8,4,4,2,1792]{4,3,2,1,0:T(2,128)} reshape(f32[8,128,448]{2,1,0:T(8,128)S(1)} %fusion.44) | data formatting | bytes 3670016 | tf_op jit(solution)/shard_map/concatenate | solution.py:87
  86.5 2.2 %fusion.45 = f32[8,128,448]{2,1,0:T(8,128)S(1)} fusion(bf16[8,128,256]{2,1,0:T(8,128)(2,1)S(1)} %bitcast.185, bf16[8,448,256]{2,1,0:T(8,128)(2,1)} %get-tuple-element.44), kind=kOutput, calls=%fused_computation.70 | convolution fusion | flops 234881024 | bytes 4194304 | tf_op jit(solution)/shard_map/jct,jot->jco/dot_general | solution.py:63
  88.7 2.9 %concatenate.19 = f32[8,4,4,2,1792]{4,3,2,1,0:T(2,128)} reshape(f32[8,128,448]{2,1,0:T(8,128)S(1)} %fusion.45) | data formatting | bytes 3670016 | tf_op jit(solution)/shard_map/concatenate | solution.py:87
  93.5 1.4 copy.219
  97.6 2.1 %copy.147 = f32[8,128,128]{2,1,0:T(8,128)} copy(f32[8,128,128]{1,2,0:T(8,128)} %convolution_bitcast_fusion) | data formatting | bytes 1048576 | tf_op jit(solution)/shard_map/tki,kot->kio/dot_general | solution.py:82
  99.7 2.1 %concatenate.18 = f32[8,4,4,2,512]{4,3,2,1,0:T(2,128)} reshape(f32[8,128,128]{2,1,0:T(8,128)} %copy.147) | data formatting | bytes 1048576 | tf_op jit(solution)/shard_map/concatenate | solution.py:87
  105.3 1.3 copy_dynamic-update-slice_fusion
  107.3 23.0 %collective-permute-start = (f32[8,4,4,1,6912]{4,0,3,2,1:T(8,128)S(1)}, f32[8,4,4,1,6912]{4,0,3,2,1:T(8,128)S(1)}, u32[]{:S(2)}, u32[]{:S(2)}) collective-permute-start(f32[8,4,4,1,6912]{4,0,3,2,1:T(8,128)S(1)} %slice_select_fusion), channel_id=1, source_target_pairs={{0,8},{8,0},{1,9},{9,1},{2,10},{10,2},{3,11},{11,3},{4,12},{12,4},... | collective-permute-start | bytes 10616840 | tf_op jit(solution)/shard_map/ppermute | solution.py:97
  130.3 5.8 %collective-permute-done = f32[8,4,4,1,6912]{4,0,3,2,1:T(8,128)S(1)} collective-permute-done((f32[8,4,4,1,6912]{4,0,3,2,1:T(8,128)S(1)}, f32[8,4,4,1,6912]{4,0,3,2,1:T(8,128)S(1)}, u32[]{:S(2)}, u32[]{:S(2)}) %collective-permute-start) | collective-permute-done | bytes 3538976 | tf_op jit(solution)/shard_map/ppermute | solution.py:97
  136.8 26.1 %all_to_all.58 = bf16[8,4,4,1,6912]{4,0,3,1,2:T(8,128)(2,1)S(1)} all-to-all(bf16[8,4,4,1,6912]{4,0,3,1,2:T(8,128)(2,1)S(1)} %copy.160), channel_id=1, replica_groups=mesh['dz'=4,'dx'=4,'dc'=2,'mp'=8] {'dx'}, dimensions={2} | all-to-all | bytes 3538944 | tf_op jit(solution)/shard_map/all_to_all | solution.py:100
  162.9 1.1 reduce_sum.21
  164.0 3.5 %all-to-all-start.4 = ((bf16[8,4,1,1,6912]{4,0,3,2,1:T(8,128)(2,1)}), bf16[8,4,1,1,6912]{4,0,3,2,1:T(8,128)(2,1)S(1)}, u32[]{:S(2)}, u32[]{:S(2)}) async-start(bf16[8,4,1,1,6912]{4,0,3,2,1:T(8,128)(2,1)} %bitcast.46), calls=%async_computation.4 | async-start | bytes 884736 | tf_op jit(solution)/shard_map/all_to_all | solution.py:100
  169.1 10.6 %all-to-all-done.4 = bf16[8,4,1,1,6912]{4,0,3,2,1:T(8,128)(2,1)S(1)} async-done(((bf16[8,4,1,1,6912]{4,0,3,2,1:T(8,128)(2,1)}), bf16[8,4,1,1,6912]{4,0,3,2,1:T(8,128)(2,1)S(1)}, u32[]{:S(2)}, u32[]{:S(2)}) %all-to-all-start.4) | async-done | bytes 442400 | tf_op jit(solution)/shard_map/all_to_all | solution.py:100
  (85 shorter events, 23.8 us)
Async XLA Ops:
  4.1 1.3 copy-start.7
  4.4 1.1 copy-start.20
  7.4 11.8 %copy-start.4 = (bf16[8,448,128]{2,1,0:T(8,128)(2,1)S(1)}, bf16[8,448,128]{2,1,0:T(8,128)(2,1)}, u32[]{:S(2)}) copy-start(bf16[8,448,128]{2,1,0:T(8,128)(2,1)} %param.14) | copy-start | bytes 2752516
  7.4 37.2 %all-to-all-start = ((bf16[3,64,16,256]{3,2,0,1:T(8,128)(2,1)}), bf16[3,64,16,256]{3,2,0,1:T(8,128)(2,1)S(1)}, u32[]{:S(2)}, u32[]{:S(2)}) async-start(bf16[3,64,16,256]{3,2,0,1:T(8,128)(2,1)} %pad_maximum_fusion), calls=%async_computation | async-start | bytes 3145728 | tf_op jit(solution)/shard_map/all_to_all | solution.py:38
  44.7 1.2 copy-start.5
  45.9 1.2 copy-start.6
  47.1 1.2 copy-start.19
  48.3 4.8 %copy-start.18 = (bf16[8,448,128]{1,0,2:T(8,128)(2,1)S(1)}, bf16[8,448,128]{1,0,2:T(8,128)(2,1)}, u32[]{:S(2)}) copy-start(bf16[8,448,128]{1,0,2:T(8,128)(2,1)} %copy.149) | copy-start | bytes 2752516
  51.8 1.2 copy-start.15
  54.9 15.1 %all-to-all-start.2 = ((bf16[64,16,256]{2,1,0:T(8,128)(2,1)}), bf16[64,16,256]{2,1,0:T(8,128)(2,1)S(1)}, u32[]{:S(2)}, u32[]{:S(2)}) async-start(bf16[64,16,256]{2,1,0:T(8,128)(2,1)} %copy.151), calls=%async_computation.2 | async-start | bytes 1048576 | tf_op jit(solution)/shard_map/all_to_all | solution.py:50
  62.7 3.0 %copy-start.14 = (bf16[8,448,256]{2,1,0:T(8,128)(2,1)S(1)}, bf16[8,448,256]{2,1,0:T(8,128)(2,1)}, u32[]{:S(2)}) copy-start(bf16[8,448,256]{2,1,0:T(8,128)(2,1)} %get-tuple-element.44) | copy-start | bytes 5505028
  70.1 6.9 %copy-start.9 = (bf16[64,16,256]{2,1,0:T(8,128)(2,1)}, bf16[64,16,256]{2,1,0:T(8,128)(2,1)S(1)}, u32[]{:S(2)}) copy-start(bf16[64,16,256]{2,1,0:T(8,128)(2,1)S(1)} %all-to-all-done.2) | copy-start | bytes 1572868
  70.1 23.4 %all-to-all-start.1 = ((bf16[2,64,16,256]{3,2,0,1:T(8,128)(2,1)}), bf16[2,64,16,256]{3,2,0,1:T(8,128)(2,1)}, u32[]{:S(2)}, u32[]{:S(2)}) async-start(bf16[2,64,16,256]{3,2,0,1:T(8,128)(2,1)} %pad_maximum_fusion.1), calls=%async_computation.1 | async-start | bytes 2097152 | tf_op jit(solution)/shard_map/all_to_all | solution.py:70
  88.7 2.9 %copy-start.10 = (bf16[64,16,256]{2,1,0:T(8,128)(2,1)S(1)}, bf16[64,16,256]{2,1,0:T(8,128)(2,1)}, u32[]{:S(2)}) copy-start(bf16[64,16,256]{2,1,0:T(8,128)(2,1)} %copy-done.9) | copy-start | bytes 1572868
  88.7 2.9 %copy-start.8 = (bf16[256,1024]{1,0:T(8,128)(2,1)S(1)}, bf16[256,1024]{1,0:T(8,128)(2,1)}, u32[]{:S(2)}) copy-start(bf16[256,1024]{1,0:T(8,128)(2,1)} %param.9) | copy-start | bytes 1572868
  93.5 1.5 copy-start.3
  96.6 5.6 %copy-start.2 = (f32[8,4,4,2,1792]{4,3,2,1,0:T(2,128)S(1)}, f32[8,4,4,2,1792]{4,3,2,1,0:T(2,128)}, u32[]{:S(2)}) copy-start(f32[8,4,4,2,1792]{4,3,2,1,0:T(2,128)} %concatenate.17) | copy-start | bytes 5505028
  97.6 4.2 %copy-start.12 = (f32[8,4,4,2,512]{4,3,2,1,0:T(2,128)S(1)}, f32[8,4,4,2,512]{4,3,2,1,0:T(2,128)}, u32[]{:S(2)}) copy-start(f32[8,4,4,2,512]{4,3,2,1,0:T(2,128)} %concatenate.16) | copy-start | bytes 1572868
  102.2 1.1 copy-start.13
  102.2 1.7 copy-start.1
  103.8 1.5 copy-start
  105.3 1.3 copy-start.11
  107.3 28.9 %collective-permute-start = (f32[8,4,4,1,6912]{4,0,3,2,1:T(8,128)S(1)}, f32[8,4,4,1,6912]{4,0,3,2,1:T(8,128)S(1)}, u32[]{:S(2)}, u32[]{:S(2)}) collective-permute-start(f32[8,4,4,1,6912]{4,0,3,2,1:T(8,128)S(1)} %slice_select_fusion), channel_id=1, source_target_pairs={{0,8},{8,0},{1,9},{9,1},{2,10},{10,2},{3,11},{11,3},{4,12},{12,4},... | collective-permute-start | bytes 10616840 | tf_op jit(solution)/shard_map/ppermute | solution.py:97
  162.9 4.6 %copy-start.16 = (bf16[8,128,128]{2,1,0:T(8,128)(2,1)S(1)}, bf16[8,128,128]{2,1,0:T(8,128)(2,1)}, u32[]{:S(2)}) copy-start(bf16[8,128,128]{2,1,0:T(8,128)(2,1)} %param.10) | copy-start | bytes 786436
  162.9 4.9 %copy-start.17 = (bf16[8,128,128]{2,1,0:T(8,128)(2,1)S(1)}, bf16[8,128,128]{2,1,0:T(8,128)(2,1)}, u32[]{:S(2)}) copy-start(bf16[8,128,128]{2,1,0:T(8,128)(2,1)} %param.12) | copy-start | bytes 786436
  164.0 15.7 %all-to-all-start.4 = ((bf16[8,4,1,1,6912]{4,0,3,2,1:T(8,128)(2,1)}), bf16[8,4,1,1,6912]{4,0,3,2,1:T(8,128)(2,1)S(1)}, u32[]{:S(2)}, u32[]{:S(2)}) async-start(bf16[8,4,1,1,6912]{4,0,3,2,1:T(8,128)(2,1)} %bitcast.46), calls=%async_computation.4 | async-start | bytes 884736 | tf_op jit(solution)/shard_map/all_to_all | solution.py:100

commit v14 on v10

--- a/solution.py
+++ b/solution.py
@@ -90,8 +90,17 @@
     for position in reversed(range(len(DP))):
         if position == len(DP) - 1 and sizes[position] == 2:
             me = lax.axis_index(DP[position])
-            own = lax.dynamic_index_in_dim(summed, me, axis=1 + position)
-            other = lax.dynamic_index_in_dim(summed, 1 - me, axis=1 + position)
+            parts = [
+                piece.reshape(piece.shape[0], *sizes, piece.shape[2]) for piece in flat
+            ]
+            firsts = [lax.index_in_dim(p, 0, axis=1 + position) for p in parts]
+            seconds = [lax.index_in_dim(p, 1, axis=1 + position) for p in parts]
+            own = jnp.concatenate(
+                [jnp.where(me == 0, a, b) for a, b in zip(firsts, seconds)], axis=-1
+            )
+            other = jnp.concatenate(
+                [jnp.where(me == 0, b, a) for a, b in zip(firsts, seconds)], axis=-1
+            )
             summed = own + lax.ppermute(other, DP[position], [(0, 1), (1, 0)])
             continue
         wire = summed if position == len(DP) - 1 else summed.astype(jnp.bfloat16)

time: 191 us -> 192 us (level)
  waiting for transfers between devices: 42.9 us -> 35.4 us
  other arithmetic: 7.7 us -> 12.2 us
  local copies, waits for them, and re-layouts: 44.8 us -> 48.7 us
  matrix products: 18.7 us -> 16.5 us
    slice x0 -> x6, local copies, waits for them, and re-layouts: none -> 16.5 us  [shards(): firsts = [lax.index_in_dim(p, 0, axis=1 + position) for p in parts]]
    concatenate x7 -> x0, local copies, waits for them, and re-layouts: 12.6 us -> none  [shards(): stacked = jnp.concatenate(flat, axis=2)]
    another operation x0 -> x6, local copies, waits for them, and re-layouts: none -> 9.86 us  [shards(): piece.reshape(piece.shape[0], *sizes, piece.shape[2])]
    unnamed x57 -> x58, local copies, waits for them, and re-layouts: 19.8 us -> 13.1 us
    unnamed x0 -> x5, other arithmetic: none -> 6.29 us
    all_to_all x1, waiting for transfers between devices: 23.5 us -> 19 us  [shards(): lax.all_to_all(jnp.stack([gate_mid, up_mid, back_mid]), 'mp', split_axis=...]
    convert_element_type x1, other arithmetic: 3.39 us -> 0.32 us  [shards(): wire = summed if position == len(DP) - 1 else summed.astype(jnp.bfloat16)]
    dynamic_slice x1 -> x0, local copies, waits for them, and re-layouts: 2.34 us -> none  [shards(): other = lax.dynamic_index_in_dim(summed, 1 - me, axis=1 + position)]
  transfers between devices with their start and end apart: 5 -> 5, of which waited for: 5 -> 3; matrix products, arithmetic and copies ran while one was open for 15% -> 19% of each run, Pallas kernels for 0% -> 0%
where the time goes in v14:
time: 192 us; the launch traced here: 191 us
  starting transfers between devices  51 us (27%)
  local copies, waits for them, and re-layouts  48.7 us (25%)
  waiting for transfers between devices  35.4 us (18%)
  blocking collectives  26.2 us (14%)
  matrix products  16.5 us (9%)
  other arithmetic  12.2 us (6%)
    all_to_all x1, blocking collectives, shards(): lax.all_to_all(wire, DP[position], split_axis=1 + position, concat_axis=1...  26.2 us
    ppermute x1, starting transfers between devices, shards(): summed = own + lax.ppermute(other, DP[position], [(0, 1), (1, 0)])  22.3 us
    all_to_all x1, waiting for transfers between devices, shards(): lax.all_to_all(jnp.stack([gate_mid, up_mid, back_mid]), 'mp', split_axis=...  19 us
    slice x6, local copies, waits for them, and re-layouts, shards(): firsts = [lax.index_in_dim(p, 0, axis=1 + position) for p in parts]  16.5 us
    unnamed x58, local copies, waits for them, and re-layouts  13.1 us
    all_to_all x1, starting transfers between devices, shards(): lax.all_to_all(jnp.stack([gate_mid, up_mid, back_mid]), 'mp', split_axis=...  11.8 us
    all_to_all x1, waiting for transfers between devices, shards(): lax.all_to_all(wire, DP[position], split_axis=1 + position, concat_axis=1...  10.6 us
    another operation x6, local copies, waits for them, and re-layouts, shards(): piece.reshape(piece.shape[0], *sizes, piece.shape[2])  9.86 us
  transfers between devices with their start and end apart: 5, of which 3 were waited for; matrix products, arithmetic and copies ran while one was open for 19% of the time, Pallas kernels for 0%

profile of v14, /device:TPU:1, one launch (start us, length us, event | category | flops | bytes accessed | tf_op | source)
XLA Modules:
  0.0 191.2 jit_solution(5943244618015140536)
XLA Ops:
  0.6 1.2 copy.128
  3.0 1.2 copy.200
  6.2 1.3 pad_maximum_fusion
  7.5 11.8 %all-to-all-start = ((bf16[3,64,16,256]{3,2,0,1:T(8,128)(2,1)}), bf16[3,64,16,256]{3,2,0,1:T(8,128)(2,1)S(1)}, u32[]{:S(2)}, u32[]{:S(2)}) async-start(bf16[3,64,16,256]{3,2,0,1:T(8,128)(2,1)} %pad_maximum_fusion), calls=%async_computation | async-start | bytes 3145728 | tf_op jit(solution)/shard_map/all_to_all | solution.py:38
  19.3 1.9 %copy.140 = bf16[8,128,448]{2,0,1:T(8,128)(2,1)} copy(bf16[8,128,448]{1,2,0:T(8,128)(2,1)S(1)} %copy-done.2) | data formatting | bytes 1835008 | tf_op args[3]
  21.2 2.7 %copy.142 = bf16[8,128,448]{2,0,1:T(8,128)(2,1)} copy(bf16[8,128,448]{1,2,0:T(8,128)(2,1)} %param.13) | data formatting | bytes 1835008 | tf_op args[5]
  23.9 1.8 copy.163
  25.7 19.0 %all-to-all-done = bf16[3,64,16,256]{3,2,0,1:T(8,128)(2,1)S(1)} async-done(((bf16[3,64,16,256]{3,2,0,1:T(8,128)(2,1)}), bf16[3,64,16,256]{3,2,0,1:T(8,128)(2,1)S(1)}, u32[]{:S(2)}, u32[]{:S(2)}) %all-to-all-start) | async-done | bytes 1572896 | tf_op jit(solution)/shard_map/all_to_all | solution.py:38
  46.8 3.5 %fusion.7 = (bf16[8,448,256]{2,1,0:T(8,128)(2,1)S(1)}, bf16[8,448,256]{2,1,0:T(8,128)(2,1)}, bf16[8,448,256]{2,1,0:T(8,128)(2,1)}) fusion(f32[8,256,448]{1,2,0:T(8,128)S(1)} %fusion.54, f32[8,256,448]{1,2,0:T(8,128)S(1)} %fusion.53, bf16[8,128,448]{1,2,0:T(8,128)(2,1)S(1)} %copy-done.23, bf16[8,128,256]{2,1,0:T(8,128)(2,1)S(1)} %bitcast.185), kind=kOutput, calls=%fused_computation.12 | convolution fusion | flops 248643584 | bytes 14286848 | tf_op jit(solution)/shard_map/jct,jco->jot/dot_general | solution.py:29
  52.4 2.2 %reshape_reshape.22 = f32[8,4,4,2,1792]{4,3,2,1,0:T(2,128)} reshape(f32[8,448,128]{2,1,0:T(8,128)S(1)} %fusion.52) | data formatting | bytes 3670016 | tf_op jit(solution)/shard_map/reshape;reshape | solution.py:94
  55.7 2.5 %fusion.15 = bf16[8,256,64,2]{1,2,3,0:T(8,128)(2,1)S(1)} fusion(bf16[8,448,256]{2,1,0:T(8,128)(2,1)} %get-tuple-element.43, bf16[8,64,2,448]{3,0,2,1:T(8,128)(2,1)} %bitcast.196), kind=kOutput, calls=%fused_computation.25 | convolution fusion | flops 235143168 | bytes 3276800 | tf_op jit(solution)/shard_map/jot,jkpo->kjpt/dot_general | solution.py:67
  61.2 4.1 %all-to-all-start.2 = ((bf16[64,16,256]{2,1,0:T(8,128)(2,1)}), bf16[64,16,256]{2,1,0:T(8,128)(2,1)S(1)}, u32[]{:S(2)}, u32[]{:S(2)}) async-start(bf16[64,16,256]{2,1,0:T(8,128)(2,1)} %copy.165), calls=%async_computation.2 | async-start | bytes 1048576 | tf_op jit(solution)/shard_map/all_to_all | solution.py:50
  65.3 2.2 %fusion.50 = f32[8,128,448]{2,1,0:T(8,128)S(1)} fusion(bf16[8,128,256]{2,1,0:T(8,128)(2,1)S(1)} %bitcast.174, bf16[8,448,256]{2,1,0:T(8,128)(2,1)} %get-tuple-element.43), kind=kOutput, calls=%fused_computation.80 | convolution fusion | flops 234881024 | bytes 4194304 | tf_op jit(solution)/shard_map/jct,jot->jco/dot_general | solution.py:60
  67.5 2.9 %reshape_reshape.19 = f32[8,4,4,2,1792]{4,3,2,1,0:T(2,128)} reshape(f32[8,128,448]{2,1,0:T(8,128)S(1)} %fusion.50) | data formatting | bytes 3670016 | tf_op jit(solution)/shard_map/reshape;reshape | solution.py:94
  70.4 2.1 %pad_maximum_fusion.1 = bf16[2,64,16,256]{3,2,0,1:T(8,128)(2,1)} fusion(bf16[1,64,16,256]{3,2,0,1:T(8,128)(2,1)} %copy.145, bf16[1,64,16,256]{3,2,0,1:T(8,128)(2,1)S(1)} %copy-done.15), kind=kLoop, calls=%fused_computation.34 | loop fusion | flops 524288 | bytes 2097152 | tf_op jit(solution)/shard_map/stack | solution.py:71
  72.6 5.2 %fusion.42 = (f32[8,4,4,1,1792]{4,3,2,1,0:T(1,128)}, f32[8,4,4,1,1792]{4,3,2,1,0:T(1,128)}) fusion(f32[8,4,4,2,1792]{4,3,2,1,0:T(2,128)} %reshape_reshape.22), kind=kLoop, calls=%fused_computation.72 | loop fusion | bytes 3670016 | tf_op jit(solution)/shard_map/slice | solution.py:96
  78.5 9.0 %all-to-all-start.1 = ((bf16[2,64,16,256]{3,2,0,1:T(8,128)(2,1)}), bf16[2,64,16,256]{3,2,0,1:T(8,128)(2,1)S(1)}, u32[]{:S(2)}, u32[]{:S(2)}) async-start(bf16[2,64,16,256]{3,2,0,1:T(8,128)(2,1)} %pad_maximum_fusion.1), calls=%async_computation.1 | async-start | bytes 2097152 | tf_op jit(solution)/shard_map/all_to_all | solution.py:70
  87.6 2.4 %fusion.51 = f32[8,128,448]{2,1,0:T(8,128)S(1)} fusion(bf16[8,128,256]{2,1,0:T(8,128)(2,1)} %bitcast.186, bf16[8,448,256]{2,1,0:T(8,128)(2,1)} %get-tuple-element.44), kind=kOutput, calls=%fused_computation.81 | convolution fusion | flops 234881024 | bytes 4194304 | tf_op jit(solution)/shard_map/jct,jot->jco/dot_general | solution.py:63
  89.9 2.9 %reshape_reshape.21 = f32[8,4,4,2,1792]{4,3,2,1,0:T(2,128)} reshape(f32[8,128,448]{2,1,0:T(8,128)S(1)} %fusion.51) | data formatting | bytes 3670016 | tf_op jit(solution)/shard_map/reshape;reshape | solution.py:94
  92.9 5.2 %fusion.44 = (f32[8,4,4,1,1792]{4,3,2,1,0:T(1,128)}, f32[8,4,4,1,1792]{4,3,2,1,0:T(1,128)}) fusion(f32[8,4,4,2,1792]{4,3,2,1,0:T(2,128)} %reshape_reshape.19), kind=kLoop, calls=%fused_computation.74 | loop fusion | bytes 3670016 | tf_op jit(solution)/shard_map/slice | solution.py:96
  98.1 3.0 %fusion.43 = (f32[8,4,4,1,1792]{4,3,2,1,0:T(1,128)}, f32[8,4,4,1,1792]{4,3,2,1,0:T(1,128)}) fusion(f32[8,4,4,2,1792]{4,3,2,1,0:T(2,128)S(1)} %copy-done), kind=kLoop, calls=%fused_computation.73 | loop fusion | bytes 3670016 | tf_op jit(solution)/shard_map/slice | solution.py:96
  101.8 1.3 fusion.47
  104.1 1.3 fusion.49
  106.7 1.3 reshape_reshape.20
  108.4 1.4 select_dynamic-update-slice_fusion.8
  109.9 2.3 %select_dynamic-update-slice_fusion.2 = (f32[8,4,4,1,6912]{4,0,3,2,1:T(8,128)S(1)}, f32[8,4,4,1,6912]{4,0,3,2,1:T(8,128)S(1)}) fusion(f32[8,4,4,1,6912]{4,0,3,2,1:T(8,128)S(1)} %get-tuple-element.66, f32[8,4,4,1,1792]{4,3,2,1,0:T(1,128)} %get-tuple-element.56, f32[8,4,4,1,1792]{4,3,2,1,0:T(1,128)S(1)} %copy-done.9, pred[]{:T(512)S(6)} %eq.2, ...), kind=kLoop, calls=%fused_computation.41 | loop fusion | flops 458752 | bytes 3670017
  113.6 1.2 select_dynamic-update-slice_fusion
  115.2 22.3 %collective-permute-start = (f32[8,4,4,1,6912]{4,0,3,2,1:T(8,128)S(1)}, f32[8,4,4,1,6912]{4,0,3,2,1:T(8,128)S(1)}, u32[]{:S(2)}, u32[]{:S(2)}) collective-permute-start(f32[8,4,4,1,6912]{4,0,3,2,1:T(8,128)S(1)} %get-tuple-element.62), channel_id=1, source_target_pairs={{0,8},{8,0},{1,9},{9,1},{2,10},{10,2},{3,11},{11,3},{4,12},{12,4},... | collective-permute-start | bytes 10616840 | tf_op jit(solution)/shard_map/ppermute | solution.py:104
  137.5 5.8 %collective-permute-done = f32[8,4,4,1,6912]{4,0,3,2,1:T(8,128)S(1)} collective-permute-done((f32[8,4,4,1,6912]{4,0,3,2,1:T(8,128)S(1)}, f32[8,4,4,1,6912]{4,0,3,2,1:T(8,128)S(1)}, u32[]{:S(2)}, u32[]{:S(2)}) %collective-permute-start) | collective-permute-done | bytes 3538976 | tf_op jit(solution)/shard_map/ppermute | solution.py:104
  143.8 26.2 %all_to_all.58 = bf16[8,4,4,1,6912]{4,0,3,1,2:T(8,128)(2,1)S(1)} all-to-all(bf16[8,4,4,1,6912]{4,0,3,1,2:T(8,128)(2,1)S(1)} %copy.170), channel_id=1, replica_groups=mesh['dz'=4,'dx'=4,'dc'=2,'mp'=8] {'dx'}, dimensions={2} | all-to-all | bytes 3538944 | tf_op jit(solution)/shard_map/all_to_all | solution.py:107
  171.1 3.8 %all-to-all-start.4 = ((bf16[8,4,1,1,6912]{4,0,3,2,1:T(8,128)(2,1)}), bf16[8,4,1,1,6912]{4,0,3,2,1:T(8,128)(2,1)S(1)}, u32[]{:S(2)}, u32[]{:S(2)}) async-start(bf16[8,4,1,1,6912]{4,0,3,2,1:T(8,128)(2,1)} %bitcast.46), calls=%async_computation.4 | async-start | bytes 884736 | tf_op jit(solution)/shard_map/all_to_all | solution.py:107
  176.5 10.6 %all-to-all-done.4 = bf16[8,4,1,1,6912]{4,0,3,2,1:T(8,128)(2,1)S(1)} async-done(((bf16[8,4,1,1,6912]{4,0,3,2,1:T(8,128)(2,1)}), bf16[8,4,1,1,6912]{4,0,3,2,1:T(8,128)(2,1)S(1)}, u32[]{:S(2)}, u32[]{:S(2)}) %all-to-all-start.4) | async-done | bytes 442400 | tf_op jit(solution)/shard_map/all_to_all | solution.py:107
  (98 shorter events, 24.1 us)
Async XLA Ops:
  0.6 4.8 %copy-start.10 = (bf16[256,1024]{1,0:T(8,128)(2,1)S(1)}, bf16[256,1024]{1,0:T(8,128)(2,1)}, u32[]{:S(2)}) copy-start(bf16[256,1024]{1,0:T(8,128)(2,1)} %param.9) | copy-start | bytes 1572868
  3.0 2.6 %copy-start.24 = (bf16[8,128,128]{2,1,0:T(8,128)(2,1)S(1)}, bf16[8,128,128]{2,1,0:T(8,128)(2,1)}, u32[]{:S(2)}) copy-start(bf16[8,128,128]{2,1,0:T(8,128)(2,1)} %param.15) | copy-start | bytes 786436
  5.9 13.4 %copy-start.2 = (bf16[8,128,448]{1,2,0:T(8,128)(2,1)S(1)}, bf16[8,128,448]{1,2,0:T(8,128)(2,1)}, u32[]{:S(2)}) copy-start(bf16[8,128,448]{1,2,0:T(8,128)(2,1)} %param.11) | copy-start | bytes 2752516
  7.5 16.3 %copy-start.3 = (bf16[8,448,128]{2,1,0:T(8,128)(2,1)S(1)}, bf16[8,448,128]{2,1,0:T(8,128)(2,1)}, u32[]{:S(2)}) copy-start(bf16[8,448,128]{2,1,0:T(8,128)(2,1)} %param.14) | copy-start | bytes 2752516
  7.5 37.1 %all-to-all-start = ((bf16[3,64,16,256]{3,2,0,1:T(8,128)(2,1)}), bf16[3,64,16,256]{3,2,0,1:T(8,128)(2,1)S(1)}, u32[]{:S(2)}, u32[]{:S(2)}) async-start(bf16[3,64,16,256]{3,2,0,1:T(8,128)(2,1)} %pad_maximum_fusion), calls=%async_computation | async-start | bytes 3145728 | tf_op jit(solution)/shard_map/all_to_all | solution.py:38
  44.8 1.4 copy-start.4
  45.0 5.4 %copy-start.12 = (bf16[1,8,8,16,256]{4,3,2,1,0:T(8,128)(2,1)}, bf16[1,8,8,16,256]{4,3,2,1,0:T(8,128)(2,1)S(1)}, u32[]{:S(2)}) copy-start(bf16[1,8,8,16,256]{4,3,2,1,0:T(8,128)(2,1)S(1)} %get-tuple-element.57) | copy-start | bytes 1572868
  45.6 1.3 copy-start.23
  50.4 1.2 copy-start.20
  54.6 4.8 %copy-start.16 = (bf16[8,448,256]{2,1,0:T(8,128)(2,1)S(1)}, bf16[8,448,256]{2,1,0:T(8,128)(2,1)}, u32[]{:S(2)}) copy-start(bf16[8,448,256]{2,1,0:T(8,128)(2,1)} %get-tuple-element.44) | copy-start | bytes 5505028
  54.6 4.8 %copy-start.19 = (bf16[8,128,448]{2,0,1:T(8,128)(2,1)S(1)}, bf16[8,128,448]{2,0,1:T(8,128)(2,1)}, u32[]{:S(2)}) copy-start(bf16[8,128,448]{2,0,1:T(8,128)(2,1)} %copy.142) | copy-start | bytes 2752516
  61.2 16.5 %all-to-all-start.2 = ((bf16[64,16,256]{2,1,0:T(8,128)(2,1)}), bf16[64,16,256]{2,1,0:T(8,128)(2,1)S(1)}, u32[]{:S(2)}, u32[]{:S(2)}) async-start(bf16[64,16,256]{2,1,0:T(8,128)(2,1)} %copy.165), calls=%async_computation.2 | async-start | bytes 1048576 | tf_op jit(solution)/shard_map/all_to_all | solution.py:50
  67.5 2.9 %copy-start.15 = (bf16[1,64,16,256]{3,2,0,1:T(8,128)(2,1)S(1)}, bf16[1,64,16,256]{3,2,0,1:T(8,128)(2,1)}, u32[]{:S(2)}) copy-start(bf16[1,64,16,256]{3,2,0,1:T(8,128)(2,1)} %copy.144) | copy-start | bytes 1572868
  77.7 0.8 copy-start.13
  78.5 24.6 %all-to-all-start.1 = ((bf16[2,64,16,256]{3,2,0,1:T(8,128)(2,1)}), bf16[2,64,16,256]{3,2,0,1:T(8,128)(2,1)S(1)}, u32[]{:S(2)}, u32[]{:S(2)}) async-start(bf16[2,64,16,256]{3,2,0,1:T(8,128)(2,1)} %pad_maximum_fusion.1), calls=%async_computation.1 | async-start | bytes 2097152 | tf_op jit(solution)/shard_map/all_to_all | solution.py:70
  92.8 5.2 %copy-start = (f32[8,4,4,2,1792]{4,3,2,1,0:T(2,128)S(1)}, f32[8,4,4,2,1792]{4,3,2,1,0:T(2,128)}, u32[]{:S(2)}) copy-start(f32[8,4,4,2,1792]{4,3,2,1,0:T(2,128)} %reshape_reshape.21) | copy-start | bytes 5505028
  92.9 8.3 %copy-start.14 = (bf16[64,16,256]{2,1,0:T(8,128)(2,1)S(1)}, bf16[64,16,256]{2,1,0:T(8,128)(2,1)}, u32[]{:S(2)}) copy-start(bf16[64,16,256]{2,1,0:T(8,128)(2,1)} %copy-done.13) | copy-start | bytes 1572868
  92.9 8.3 %copy-start.11 = (bf16[256,1024]{1,0:T(8,128)(2,1)S(1)}, bf16[256,1024]{1,0:T(8,128)(2,1)}, u32[]{:S(2)}) copy-start(bf16[256,1024]{1,0:T(8,128)(2,1)} %param.9) | copy-start | bytes 1572868
  101.5 1.8 copy-start.1
  104.1 5.8 %copy-start.9 = (f32[8,4,4,1,1792]{4,3,2,1,0:T(1,128)S(1)}, f32[8,4,4,1,1792]{4,3,2,1,0:T(1,128)}, u32[]{:S(2)}) copy-start(f32[8,4,4,1,1792]{4,3,2,1,0:T(1,128)} %get-tuple-element.55) | copy-start | bytes 2752516
  108.0 4.5 %copy-start.7 = (f32[8,4,4,1,1792]{4,3,2,1,0:T(1,128)S(1)}, f32[8,4,4,1,1792]{4,3,2,1,0:T(1,128)}, u32[]{:S(2)}) copy-start(f32[8,4,4,1,1792]{4,3,2,1,0:T(1,128)} %get-tuple-element.53) | copy-start | bytes 2752516
  108.0 4.5 %copy-start.8 = (f32[8,4,4,1,1792]{4,3,2,1,0:T(1,128)S(1)}, f32[8,4,4,1,1792]{4,3,2,1,0:T(1,128)}, u32[]{:S(2)}) copy-start(f32[8,4,4,1,1792]{4,3,2,1,0:T(1,128)} %get-tuple-element.54) | copy-start | bytes 2752516
  109.9 3.7 %copy-start.5 = (f32[8,4,4,1,1792]{4,3,2,1,0:T(1,128)S(1)}, f32[8,4,4,1,1792]{4,3,2,1,0:T(1,128)}, u32[]{:S(2)}) copy-start(f32[8,4,4,1,1792]{4,3,2,1,0:T(1,128)} %get-tuple-element.51) | copy-start | bytes 2752516
  109.9 3.7 %copy-start.6 = (f32[8,4,4,1,1792]{4,3,2,1,0:T(1,128)S(1)}, f32[8,4,4,1,1792]{4,3,2,1,0:T(1,128)}, u32[]{:S(2)}) copy-start(f32[8,4,4,1,1792]{4,3,2,1,0:T(1,128)} %get-tuple-element.52) | copy-start | bytes 2752516
  112.6 2.3 %copy-start.21 = (f32[8,4,4,1,512]{4,3,2,1,0:T(1,128)S(1)}, f32[8,4,4,1,512]{4,3,2,1,0:T(1,128)}, u32[]{:S(2)}) copy-start(f32[8,4,4,1,512]{4,3,2,1,0:T(1,128)} %get-tuple-element.68) | copy-start | bytes 786436
  112.6 2.3 %copy-start.22 = (f32[8,4,4,1,512]{4,3,2,1,0:T(1,128)S(1)}, f32[8,4,4,1,512]{4,3,2,1,0:T(1,128)}, u32[]{:S(2)}) copy-start(f32[8,4,4,1,512]{4,3,2,1,0:T(1,128)} %get-tuple-element.69) | copy-start | bytes 786436
  115.2 28.1 %collective-permute-start = (f32[8,4,4,1,6912]{4,0,3,2,1:T(8,128)S(1)}, f32[8,4,4,1,6912]{4,0,3,2,1:T(8,128)S(1)}, u32[]{:S(2)}, u32[]{:S(2)}) collective-permute-start(f32[8,4,4,1,6912]{4,0,3,2,1:T(8,128)S(1)} %get-tuple-element.62), channel_id=1, source_target_pairs={{0,8},{8,0},{1,9},{9,1},{2,10},{10,2},{3,11},{11,3},{4,12},{12,4},... | collective-permute-start | bytes 10616840 | tf_op jit(solution)/shard_map/ppermute | solution.py:104
  143.8 31.1 %copy-start.17 = (bf16[8,128,128]{2,1,0:T(8,128)(2,1)S(1)}, bf16[8,128,128]{2,1,0:T(8,128)(2,1)}, u32[]{:S(2)}) copy-start(bf16[8,128,128]{2,1,0:T(8,128)(2,1)} %param.10) | copy-start | bytes 786436
  143.8 31.4 %copy-start.18 = (bf16[8,128,128]{2,1,0:T(8,128)(2,1)S(1)}, bf16[8,128,128]{2,1,0:T(8,128)(2,1)}, u32[]{:S(2)}) copy-start(bf16[8,128,128]{2,1,0:T(8,128)(2,1)} %param.12) | copy-start | bytes 786436
  171.1 16.0 %all-to-all-start.4 = ((bf16[8,4,1,1,6912]{4,0,3,2,1:T(8,128)(2,1)}), bf16[8,4,1,1,6912]{4,0,3,2,1:T(8,128)(2,1)S(1)}, u32[]{:S(2)}, u32[]{:S(2)}) async-start(bf16[8,4,1,1,6912]{4,0,3,2,1:T(8,128)(2,1)} %bitcast.46), calls=%async_computation.4 | async-start | bytes 884736 | tf_op jit(solution)/shard_map/all_to_all | solution.py:107

commit v15 on v13

--- a/solution.py
+++ b/solution.py
@@ -82,7 +82,7 @@
     term_up_in = jnp.einsum("tki,kot->kio", x_blocks, up_back, preferred_element_type=jnp.float32)
     grad_x = input_grad.astype(jnp.bfloat16).reshape(rows, local_blocks * BLK)
     terms = (term_gate_in, term_gate_out, term_up_in, term_up_out, term_down_in, term_down_out)
-    flat = [term.reshape(term.shape[0], groups, -1) for term in terms]
+    flat = [(term * scale).reshape(term.shape[0], groups, -1) for term in terms]
     widths = [piece.shape[2] for piece in flat]
     stacked = jnp.concatenate(flat, axis=2)
     sizes = [lax.axis_size(name) for name in DP]
@@ -106,7 +106,7 @@
     for term, width in zip(terms, widths):
         piece = summed[:, 0, start:start + width]
         start += width
-        outs.append(piece.reshape(term.shape[0], term.shape[1] // groups, term.shape[2]) * scale)
+        outs.append(piece.reshape(term.shape[0], term.shape[1] // groups, term.shape[2]))
     return (grad_x, *outs)
 
 

time: 185 us -> 187 us (1.011)
  local copies, waits for them, and re-layouts: 40.9 us -> 44.4 us
  starting transfers between devices: 49.3 us -> 47.3 us
    ppermute x1, starting transfers between devices: 23 us -> 17.4 us  [shards(): summed = own + lax.ppermute(other, DP[position], [(0, 1), (1, 0)])]
    another operation x0 -> x6, local copies, waits for them, and re-layouts: none -> 3.96 us  [shards(): piece.reshape(term.shape[0], term.shape[1] // groups, term.shape[2])]
    all_to_all x1, starting transfers between devices: 3.46 us -> 7.01 us  [shards(): lax.all_to_all(wire, DP[position], split_axis=1 + position, concat_axis=1...]
    dot_general x2 -> x0, local copies, waits for them, and re-layouts: 2.29 us -> none  [the longest x1 2.1 us: shards(): jnp.einsum('tki,kot->kio', x_blocks, up_back, preferred_element_type=jnp....]
    mul x5 -> x4, local copies, waits for them, and re-layouts: 3.32 us -> 4.95 us  [shards(): flat = [(term * scale).reshape(term.shape[0], groups, -1) for term in terms]]
    unnamed x55 -> x53, local copies, waits for them, and re-layouts: 18.2 us -> 19.3 us
  transfers between devices with their start and end apart: 5 -> 5, of which waited for: 5 -> 4; matrix products, arithmetic and copies ran while one was open for 15% -> 19% of each run, Pallas kernels for 0% -> 0%
where the time goes in v15:
time: 187 us; the launch traced here: 186 us
  starting transfers between devices  47.3 us (25%)
  local copies, waits for them, and re-layouts  44.4 us (24%)
  waiting for transfers between devices  42 us (22%)
  blocking collectives  26.1 us (14%)
  matrix products  20.3 us (11%)
  other arithmetic  4.58 us (2%)
    all_to_all x1, blocking collectives, shards(): lax.all_to_all(wire, DP[position], split_axis=1 + position, concat_axis=1...  26.1 us
    all_to_all x1, waiting for transfers between devices, shards(): lax.all_to_all(jnp.stack([gate_mid, up_mid, back_mid]), 'mp', split_axis=...  23.5 us
    unnamed x53, local copies, waits for them, and re-layouts  19.3 us
    ppermute x1, starting transfers between devices, shards(): summed = own + lax.ppermute(other, DP[position], [(0, 1), (1, 0)])  17.4 us
    all_to_all x1, starting transfers between devices, shards(): lax.all_to_all(jnp.stack([gate_mid, up_mid, back_mid]), 'mp', split_axis=...  11.8 us
    concatenate x7, local copies, waits for them, and re-layouts, shards(): stacked = jnp.concatenate(flat, axis=2)  11.7 us
    all_to_all x1, waiting for transfers between devices, shards(): lax.all_to_all(wire, DP[position], split_axis=1 + position, concat_axis=1...  10.6 us
    all_to_all x1, starting transfers between devices, shards(): lax.all_to_all(jnp.stack([narrow(gate_grad, gate_out), narrow(up_grad, up...  7.04 us
  transfers between devices with their start and end apart: 5, of which 4 were waited for; matrix products, arithmetic and copies ran while one was open for 19% of the time, Pallas kernels for 0%

profile of v15, /device:TPU:1, one launch (start us, length us, event | category | flops | bytes accessed | tf_op | source)
XLA Modules:
  0.0 185.8 jit_solution(8745416009333616605)
XLA Ops:
  2.9 1.1 copy.176
  6.3 1.3 pad_maximum_fusion
  7.7 11.8 %all-to-all-start = ((bf16[3,64,16,256]{3,2,0,1:T(8,128)(2,1)}), bf16[3,64,16,256]{3,2,0,1:T(8,128)(2,1)S(1)}, u32[]{:S(2)}, u32[]{:S(2)}) async-start(bf16[3,64,16,256]{3,2,0,1:T(8,128)(2,1)} %pad_maximum_fusion), calls=%async_computation | async-start | bytes 3145728 | tf_op jit(solution)/shard_map/all_to_all | solution.py:38
  19.4 1.8 copy.149
  21.3 23.5 %all-to-all-done = bf16[3,64,16,256]{3,2,0,1:T(8,128)(2,1)S(1)} async-done(((bf16[3,64,16,256]{3,2,0,1:T(8,128)(2,1)}), bf16[3,64,16,256]{3,2,0,1:T(8,128)(2,1)S(1)}, u32[]{:S(2)}, u32[]{:S(2)}) %all-to-all-start) | async-done | bytes 1572896 | tf_op jit(solution)/shard_map/all_to_all | solution.py:38
  45.1 1.2 copy-done.5
  48.7 3.5 %fusion.7 = (bf16[8,448,256]{2,1,0:T(8,128)(2,1)S(1)}, bf16[8,448,256]{2,1,0:T(8,128)(2,1)}, bf16[8,448,256]{2,1,0:T(8,128)(2,1)}) fusion(f32[8,256,448]{1,2,0:T(8,128)S(1)} %fusion.46, f32[8,256,448]{1,2,0:T(8,128)S(1)} %fusion.45, bf16[8,128,448]{1,2,0:T(8,128)(2,1)S(1)} %copy-done.18, bf16[8,128,256]{2,1,0:T(8,128)(2,1)S(1)} %bitcast.190), kind=kOutput, calls=%fused_computation.12 | convolution fusion | flops 248643584 | bytes 14286848 | tf_op jit(solution)/shard_map/jct,jco->jot/dot_general | solution.py:29
  52.3 1.2 copy-done.14
  55.3 4.1 %all-to-all-start.2 = ((bf16[64,16,256]{2,1,0:T(8,128)(2,1)}), bf16[64,16,256]{2,1,0:T(8,128)(2,1)S(1)}, u32[]{:S(2)}, u32[]{:S(2)}) async-start(bf16[64,16,256]{2,1,0:T(8,128)(2,1)} %copy.151), calls=%async_computation.2 | async-start | bytes 1048576 | tf_op jit(solution)/shard_map/all_to_all | solution.py:50
  59.4 1.8 copy.136
  61.3 1.9 %copy.138 = bf16[8,128,448]{2,0,1:T(8,128)(2,1)S(1)} copy(bf16[8,128,448]{1,2,0:T(8,128)(2,1)} %param.13) | data formatting | bytes 1835008 | tf_op args[5]
  63.1 2.7 %fusion.15 = bf16[8,256,64,2]{1,2,3,0:T(8,128)(2,1)S(1)} fusion(bf16[8,448,256]{2,1,0:T(8,128)(2,1)} %get-tuple-element.43, bf16[8,64,2,448]{3,0,2,1:T(8,128)(2,1)} %bitcast.196), kind=kOutput, calls=%fused_computation.32 | convolution fusion | flops 235143168 | bytes 3276800 | tf_op jit(solution)/shard_map/jot,jkpo->kjpt/dot_general | solution.py:67
  67.3 1.2 pad_maximum_fusion.1
  68.5 2.0 %all-to-all-done.2 = bf16[64,16,256]{2,1,0:T(8,128)(2,1)S(1)} async-done(((bf16[64,16,256]{2,1,0:T(8,128)(2,1)}), bf16[64,16,256]{2,1,0:T(8,128)(2,1)S(1)}, u32[]{:S(2)}, u32[]{:S(2)}) %all-to-all-start.2) | async-done | bytes 524320 | tf_op jit(solution)/shard_map/all_to_all | solution.py:50
  70.5 7.0 %all-to-all-start.1 = ((bf16[2,64,16,256]{3,2,0,1:T(8,128)(2,1)}), bf16[2,64,16,256]{3,2,0,1:T(8,128)(2,1)}, u32[]{:S(2)}, u32[]{:S(2)}) async-start(bf16[2,64,16,256]{3,2,0,1:T(8,128)(2,1)} %pad_maximum_fusion.1), calls=%async_computation.1 | async-start | bytes 2097152 | tf_op jit(solution)/shard_map/all_to_all | solution.py:70
  77.5 2.1 %convolution_multiply_fusion = f32[8,448,128]{2,1,0:T(8,128)S(1)} fusion(bf16[8,448,256]{2,1,0:T(8,128)(2,1)} %copy-done.14, bf16[8,128,256]{2,1,0:T(8,128)(2,1)S(1)} %bitcast.180), kind=kOutput, calls=%fused_computation.28 | convolution fusion | flops 235339776 | bytes 4194304 | tf_op jit(solution)/shard_map/jot,jqt->joq/dot_general | solution.py:54
  79.7 2.2 %concatenate.20 = f32[8,4,4,2,1792]{4,3,2,1,0:T(2,128)} reshape(f32[8,448,128]{2,1,0:T(8,128)S(1)} %convolution_multiply_fusion) | data formatting | bytes 3670016 | tf_op jit(solution)/shard_map/concatenate | solution.py:87
  81.8 3.4 %convolution_multiply_fusion.2 = f32[8,128,448]{1,2,0:T(8,128)} fusion(bf16[8,128,256]{2,1,0:T(8,128)(2,1)S(1)} %bitcast.178, bf16[8,448,256]{2,1,0:T(8,128)(2,1)} %get-tuple-element.43), kind=kOutput, calls=%fused_computation.30 | convolution fusion | flops 235339776 | bytes 4194304 | tf_op jit(solution)/shard_map/jct,jot->jco/dot_general | solution.py:60
  85.2 1.9 %copy.145 = f32[8,128,448]{2,1,0:T(8,128)S(1)} copy(f32[8,128,448]{1,2,0:T(8,128)} %convolution_multiply_fusion.2) | data formatting | bytes 3670016 | tf_op jit(solution)/shard_map/mul | solution.py:85
  87.1 2.9 %concatenate.17 = f32[8,4,4,2,1792]{4,3,2,1,0:T(2,128)} reshape(f32[8,128,448]{2,1,0:T(8,128)S(1)} %copy.145) | data formatting | bytes 3670016 | tf_op jit(solution)/shard_map/concatenate | solution.py:87
  90.0 3.4 %convolution_multiply_fusion.1 = f32[8,128,448]{1,2,0:T(8,128)} fusion(bf16[8,128,256]{2,1,0:T(8,128)(2,1)S(1)} %bitcast.191, bf16[8,448,256]{2,1,0:T(8,128)(2,1)} %get-tuple-element.44), kind=kOutput, calls=%fused_computation.29 | convolution fusion | flops 235339776 | bytes 4194304 | tf_op jit(solution)/shard_map/jct,jot->jco/dot_general | solution.py:63
  93.4 1.9 %copy.148 = f32[8,128,448]{2,1,0:T(8,128)S(1)} copy(f32[8,128,448]{1,2,0:T(8,128)} %convolution_multiply_fusion.1) | data formatting | bytes 3670016 | tf_op jit(solution)/shard_map/mul | solution.py:85
  95.3 2.9 %concatenate.19 = f32[8,4,4,2,1792]{4,3,2,1,0:T(2,128)} reshape(f32[8,128,448]{2,1,0:T(8,128)S(1)} %copy.148) | data formatting | bytes 3670016 | tf_op jit(solution)/shard_map/concatenate | solution.py:87
  99.6 1.4 copy.217
  104.0 1.3 concatenate.18
  105.3 1.4 copy_dynamic-update-slice_fusion.5
  111.4 17.4 %collective-permute-start = (f32[8,4,4,1,6912]{4,0,3,2,1:T(8,128)S(1)}, f32[8,4,4,1,6912]{4,0,3,2,1:T(8,128)S(1)}, u32[]{:S(2)}, u32[]{:S(2)}) collective-permute-start(f32[8,4,4,1,6912]{4,0,3,2,1:T(8,128)S(1)} %slice_select_fusion), channel_id=1, source_target_pairs={{0,8},{8,0},{1,9},{9,1},{2,10},{10,2},{3,11},{11,3},{4,12},{12,4},... | collective-permute-start | bytes 10616840 | tf_op jit(solution)/shard_map/ppermute | solution.py:97
  128.8 5.8 %collective-permute-done = f32[8,4,4,1,6912]{4,0,3,2,1:T(8,128)S(1)} collective-permute-done((f32[8,4,4,1,6912]{4,0,3,2,1:T(8,128)S(1)}, f32[8,4,4,1,6912]{4,0,3,2,1:T(8,128)S(1)}, u32[]{:S(2)}, u32[]{:S(2)}) %collective-permute-start) | collective-permute-done | bytes 3538976 | tf_op jit(solution)/shard_map/ppermute | solution.py:97
  135.3 26.1 %all_to_all.58 = bf16[8,4,4,1,6912]{4,0,3,1,2:T(8,128)(2,1)S(1)} all-to-all(bf16[8,4,4,1,6912]{4,0,3,1,2:T(8,128)(2,1)S(1)} %copy.160), channel_id=1, replica_groups=mesh['dz'=4,'dx'=4,'dc'=2,'mp'=8] {'dx'}, dimensions={2} | all-to-all | bytes 3538944 | tf_op jit(solution)/shard_map/all_to_all | solution.py:100
  161.3 1.2 reduce_sum.21
  162.5 7.0 %all-to-all-start.4 = ((bf16[8,4,1,1,6912]{4,0,3,2,1:T(8,128)(2,1)}), bf16[8,4,1,1,6912]{4,0,3,2,1:T(8,128)(2,1)S(1)}, u32[]{:S(2)}, u32[]{:S(2)}) async-start(bf16[8,4,1,1,6912]{4,0,3,2,1:T(8,128)(2,1)} %bitcast.46), calls=%async_computation.4 | async-start | bytes 884736 | tf_op jit(solution)/shard_map/all_to_all | solution.py:100
  171.1 10.6 %all-to-all-done.4 = bf16[8,4,1,1,6912]{4,0,3,2,1:T(8,128)(2,1)S(1)} async-done(((bf16[8,4,1,1,6912]{4,0,3,2,1:T(8,128)(2,1)}), bf16[8,4,1,1,6912]{4,0,3,2,1:T(8,128)(2,1)S(1)}, u32[]{:S(2)}, u32[]{:S(2)}) %all-to-all-start.4) | async-done | bytes 442400 | tf_op jit(solution)/shard_map/all_to_all | solution.py:100
  (85 shorter events, 25.5 us)
Async XLA Ops:
  4.4 1.0 copy-start.7
  4.7 1.0 copy-start.19
  7.7 11.8 %copy-start.4 = (bf16[8,448,128]{2,1,0:T(8,128)(2,1)S(1)}, bf16[8,448,128]{2,1,0:T(8,128)(2,1)}, u32[]{:S(2)}) copy-start(bf16[8,448,128]{2,1,0:T(8,128)(2,1)} %param.14) | copy-start | bytes 2752516
  7.7 37.2 %all-to-all-start = ((bf16[3,64,16,256]{3,2,0,1:T(8,128)(2,1)}), bf16[3,64,16,256]{3,2,0,1:T(8,128)(2,1)S(1)}, u32[]{:S(2)}, u32[]{:S(2)}) async-start(bf16[3,64,16,256]{3,2,0,1:T(8,128)(2,1)} %pad_maximum_fusion), calls=%async_computation | async-start | bytes 3145728 | tf_op jit(solution)/shard_map/all_to_all | solution.py:38
  45.0 1.4 copy-start.5
  45.1 3.1 %copy-start.11 = (bf16[1,8,8,16,256]{4,3,2,1,0:T(8,128)(2,1)}, bf16[1,8,8,16,256]{4,3,2,1,0:T(8,128)(2,1)S(1)}, u32[]{:S(2)}) copy-start(bf16[1,8,8,16,256]{4,3,2,1,0:T(8,128)(2,1)S(1)} %get-tuple-element.45) | copy-start | bytes 1572868
  46.4 1.2 copy-start.6
  47.5 1.2 copy-start.18
  48.7 4.7 %copy-start.17 = (bf16[8,448,128]{1,0,2:T(8,128)(2,1)S(1)}, bf16[8,448,128]{1,0,2:T(8,128)(2,1)}, u32[]{:S(2)}) copy-start(bf16[8,448,128]{1,0,2:T(8,128)(2,1)} %copy.149) | copy-start | bytes 2752516
  52.3 1.2 copy-start.14
  55.3 15.1 %all-to-all-start.2 = ((bf16[64,16,256]{2,1,0:T(8,128)(2,1)}), bf16[64,16,256]{2,1,0:T(8,128)(2,1)S(1)}, u32[]{:S(2)}, u32[]{:S(2)}) async-start(bf16[64,16,256]{2,1,0:T(8,128)(2,1)} %copy.151), calls=%async_computation.2 | async-start | bytes 1048576 | tf_op jit(solution)/shard_map/all_to_all | solution.py:50
  63.1 3.0 %copy-start.13 = (bf16[8,448,256]{2,1,0:T(8,128)(2,1)S(1)}, bf16[8,448,256]{2,1,0:T(8,128)(2,1)}, u32[]{:S(2)}) copy-start(bf16[8,448,256]{2,1,0:T(8,128)(2,1)} %get-tuple-element.44) | copy-start | bytes 5505028
  70.5 7.0 %copy-start.8 = (bf16[64,16,256]{2,1,0:T(8,128)(2,1)}, bf16[64,16,256]{2,1,0:T(8,128)(2,1)S(1)}, u32[]{:S(2)}) copy-start(bf16[64,16,256]{2,1,0:T(8,128)(2,1)S(1)} %all-to-all-done.2) | copy-start | bytes 1572868
  70.5 29.2 %all-to-all-start.1 = ((bf16[2,64,16,256]{3,2,0,1:T(8,128)(2,1)}), bf16[2,64,16,256]{3,2,0,1:T(8,128)(2,1)}, u32[]{:S(2)}, u32[]{:S(2)}) async-start(bf16[2,64,16,256]{3,2,0,1:T(8,128)(2,1)} %pad_maximum_fusion.1), calls=%async_computation.1 | async-start | bytes 2097152 | tf_op jit(solution)/shard_map/all_to_all | solution.py:70
  87.1 2.9 %copy-start.12 = (bf16[1,8,8,16,256]{4,3,2,1,0:T(8,128)(2,1)S(1)}, bf16[1,8,8,16,256]{4,3,2,1,0:T(8,128)(2,1)}, u32[]{:S(2)}) copy-start(bf16[1,8,8,16,256]{4,3,2,1,0:T(8,128)(2,1)} %copy-done.11) | copy-start | bytes 1572868
  95.3 2.9 %copy-start.9 = (bf16[64,16,256]{2,1,0:T(8,128)(2,1)S(1)}, bf16[64,16,256]{2,1,0:T(8,128)(2,1)}, u32[]{:S(2)}) copy-start(bf16[64,16,256]{2,1,0:T(8,128)(2,1)} %copy-done.8) | copy-start | bytes 1572868
  99.6 1.5 copy-start.3
  103.0 3.7 %copy-start.1 = (f32[8,4,4,2,1792]{4,3,2,1,0:T(2,128)S(1)}, f32[8,4,4,2,1792]{4,3,2,1,0:T(2,128)}, u32[]{:S(2)}) copy-start(f32[8,4,4,2,1792]{4,3,2,1,0:T(2,128)} %concatenate.17) | copy-start | bytes 5505028
  106.7 1.5 copy-start.2
  108.2 1.5 copy-start
  109.7 1.1 copy-start.10
  111.4 23.3 %collective-permute-start = (f32[8,4,4,1,6912]{4,0,3,2,1:T(8,128)S(1)}, f32[8,4,4,1,6912]{4,0,3,2,1:T(8,128)S(1)}, u32[]{:S(2)}, u32[]{:S(2)}) collective-permute-start(f32[8,4,4,1,6912]{4,0,3,2,1:T(8,128)S(1)} %slice_select_fusion), channel_id=1, source_target_pairs={{0,8},{8,0},{1,9},{9,1},{2,10},{10,2},{3,11},{11,3},{4,12},{12,4},... | collective-permute-start | bytes 10616840 | tf_op jit(solution)/shard_map/ppermute | solution.py:97
  161.3 8.2 %copy-start.15 = (bf16[8,128,128]{2,1,0:T(8,128)(2,1)S(1)}, bf16[8,128,128]{2,1,0:T(8,128)(2,1)}, u32[]{:S(2)}) copy-start(bf16[8,128,128]{2,1,0:T(8,128)(2,1)} %param.10) | copy-start | bytes 786436
  162.5 7.3 %copy-start.16 = (bf16[8,128,128]{2,1,0:T(8,128)(2,1)S(1)}, bf16[8,128,128]{2,1,0:T(8,128)(2,1)}, u32[]{:S(2)}) copy-start(bf16[8,128,128]{2,1,0:T(8,128)(2,1)} %param.12) | copy-start | bytes 786436
  162.5 19.2 %all-to-all-start.4 = ((bf16[8,4,1,1,6912]{4,0,3,2,1:T(8,128)(2,1)}), bf16[8,4,1,1,6912]{4,0,3,2,1:T(8,128)(2,1)S(1)}, u32[]{:S(2)}, u32[]{:S(2)}) async-start(bf16[8,4,1,1,6912]{4,0,3,2,1:T(8,128)(2,1)} %bitcast.46), calls=%async_computation.4 | async-start | bytes 884736 | tf_op jit(solution)/shard_map/all_to_all | solution.py:100
